TPU v7x, 32 devices: a whole 2x2x4 slice. The times are simulated.
32 devices in a mesh: dp: 2 (over x), ctx: 16 (over z, y, core).
Axes of the slice: x: 2, y: 2, z: 4, core: 2. Of those that a mesh axis runs over, the one named last changes fastest.
Arguments:
- queries: bfloat16 [4096, 4096], P(('dp', 'ctx')), parts along dimension 0, may hold values from -6 to 6
- keys: bfloat16 [4096, 4096], P(('dp', 'ctx')), parts along dimension 0, may hold values from -6 to 6
- values: bfloat16 [4096, 4096], P(('dp', 'ctx')), parts along dimension 0, may hold values from -6 to 6
- taps: bfloat16 [512, 256], P('ctx'), may hold values from -0.25 to 0.25
- segment_ids: int32 [4096], P(('dp', 'ctx')), parts along dimension 0, may hold values from 0 to 3, never falling along the last dimension, each value on 1 to 1024 neighbouring positions
Outputs:
- mixed: bfloat16 [4096, 4096], P(('dp', 'ctx')), parts along dimension 0
There are 2 independent parts, one for each index of `dp`. A program takes and returns all parts, laid end to end along the dimension named above; an argument that names none is the same for every part. Nothing has to cross between parts.
Inputs may be any that keep to these rules, and one draw needn't show every extreme that they name: `segment_ids`: ids never fall along the sequence; every id from 0 to 3 appears; each document holds 1 to 1024 positions and one holds exactly 1024.
All inputs are finite; a program needn't handle non-finite values.
Results may differ from a plain program's by a relative error of at most 0.0056.
Values may be sent and summed in bfloat16 or wider, within the bound.
No kernel may reach another device: no remote copies, remote signals or barrier semaphores. Data moves between devices by JAX's collectives and lax.ppermute only.
A program may use at most 128 MiB of HBM per device.

v0:
```python
import jax
import jax.numpy as jnp
from jax import lax
from jax.sharding import PartitionSpec as P


def shifted(value, axis, steps):
    count = lax.axis_size(axis)
    first, last = (max(0, -steps), min(count, count - steps))
    return lax.ppermute(value, axis, [(source, source + steps) for source in range(first, last)])


def pair_term(taps_major, lag_blocks, seg_target, seg_source, source_major):
    filters = source_major.shape[0]
    block_rows = source_major.shape[1]
    group_size = source_major.shape[2]
    row_step = min(128, block_rows)
    span = block_rows + row_step - 1
    window = lax.dynamic_slice_in_dim(taps_major, lag_blocks * block_rows, 2 * block_rows, 1)
    reversed_taps = window[:, ::-1]

    def row_block(start):
        segment = lax.dynamic_slice_in_dim(reversed_taps, block_rows - start - row_step, span, 1)
        repeated = jnp.tile(segment, (1, row_step + 1))
        skewed = repeated[:, row_step - 1 : row_step - 1 + row_step * (span - 1)]
        slab = skewed.reshape(filters, row_step, span - 1)[:, :, :block_rows]
        allowed = seg_target[:, None] == seg_source[None, :]
        weights = jnp.where(allowed[None, :, :], slab, jnp.zeros((), jnp.bfloat16))
        return jnp.einsum("fts,fsg->ftg", weights, source_major, preferred_element_type=jnp.float32)

    starts = jnp.arange(block_rows // row_step, dtype=jnp.int32) * row_step
    result = lax.map(row_block, starts)
    return result.transpose(1, 0, 2, 3).reshape(filters, block_rows, group_size)


def shards(queries, keys, values, taps, segment_ids):
    block_rows = queries.shape[0]
    channels = queries.shape[1]
    filters = taps.shape[1]
    group_size = channels // filters
    ctx_count = lax.axis_size("ctx")
    own_index = lax.axis_index("ctx")
    gated = (keys.astype(jnp.float32) * values.astype(jnp.float32)).astype(jnp.bfloat16)
    gated_major = gated.reshape(block_rows, filters, group_size).transpose(1, 0, 2)
    all_taps = lax.all_gather(taps, "ctx", axis=0, tiled=True)
    zero_cols = jnp.zeros((filters, block_rows), jnp.bfloat16)
    taps_major = jnp.concatenate([zero_cols, all_taps.T, zero_cols], axis=1)
    summed = pair_term(taps_major, jnp.int32(0), segment_ids, segment_ids, gated_major)
    lag_count = all_taps.shape[0] // block_rows
    empty_bf = jnp.zeros((filters, block_rows, group_size), jnp.bfloat16)
    for lag in range(1, lag_count + 1):
        seg_target = shifted(segment_ids, "ctx", -lag)
        live = own_index + lag < ctx_count

        def outgoing_term(seg_target=seg_target, lag=lag):
            return pair_term(
                taps_major, jnp.int32(lag), seg_target, segment_ids, gated_major
            ).astype(jnp.bfloat16)

        term = lax.cond(live, outgoing_term, lambda: empty_bf)
        arrived = shifted(term, "ctx", lag)
        summed = summed + arrived.astype(jnp.float32)
    conv = summed.transpose(1, 0, 2).reshape(block_rows, channels)
    return (queries.astype(jnp.float32) * conv).astype(jnp.bfloat16)


def solution(mesh):
    return jax.shard_map(
        shards,
        mesh=mesh,
        in_specs=(
            P(("dp", "ctx"), None),
            P(("dp", "ctx"), None),
            P(("dp", "ctx"), None),
            P("ctx", None),
            P(("dp", "ctx")),
        ),
        out_specs=P(("dp", "ctx"), None),
        check_vma=False,
    )
```

profile of v0, /device:TPU:0, one launch (start us, length us, event | category | flops | bytes accessed | tf_op | source)
XLA Modules:
  0.0 497.2 jit_solution(7928648411285687675)
XLA Ops:
  7.7 27.8 %all_gather.3 = bf16[512,256]{1,0:T(8,128)(2,1)S(1)} all-gather(bf16[32,256]{1,0:T(8,128)(2,1)} %param.16), channel_id=1, replica_groups=mesh['dp'=2,'ctx'=16] {'ctx'}, dimensions={0}, use_global_device_ids=true | all-gather | bytes 278528 | tf_op jit(solution)/shard_map/all_gather | solution.py:45
  35.5 89.2 %conditional.7 = (bf16[256,128,16]{1,2,0:T(8,128)(2,1)}) conditional(s32[]{:T(128)} %convert_element_type.61, () %tuple.45, (s32[128]{0:T(128)S(1)}, s32[128]{0:T(128)}, bf16[256,768]{0,1:T(8,128)(2,1)S(1)}, bf16[256,128,16]{1,2,0:T(8,128)(2,1)S(1)}) %tuple.58), branch_computations={%region_6.7_spmd, %region_7.8_spmd} | conditional | flops 138952704 | bytes 161840160 | solution.py:60
  42.3 19.4 %tile.67 = bf16[256,32895]{0,1:T(8,128)(2,1)} reshape(bf16[256,129,255]{0,2,1:T(8,128)(2,1)} %tile.66) | data formatting | bytes 33684480 | tf_op jit(solution)/shard_map/cond/branch_1_fun/while/body/eval_jaxpr/tile | solution.py:24
  61.7 15.1 %slice.64 = bf16[256,32512]{0,1:T(8,128)(2,1)} slice(bf16[256,32895]{0,1:T(8,128)(2,1)} %tile.67), slice={[0:256], [127:32639]} | slice | bytes 33292288 | tf_op jit(solution)/shard_map/cond/branch_1_fun/while/body/eval_jaxpr/slice | solution.py:25
  76.8 18.7 %reshape.192 = bf16[256,128,254]{0,2,1:T(8,128)(2,1)} reshape(bf16[256,32512]{0,1:T(8,128)(2,1)} %slice.64) | data formatting | bytes 33292288 | tf_op jit(solution)/shard_map/cond/branch_1_fun/while/body/eval_jaxpr/reshape | solution.py:26
  103.3 12.4 %copy.24 = bf16[256,128,128]{2,1,0:T(8,128)(2,1)} copy(bf16[256,128,128]{0,2,1:T(8,128)(2,1)} %slice.65) | data formatting | bytes 16777216 | tf_op jit(solution)/shard_map/cond
  127.0 88.2 %conditional.4 = (bf16[256,128,16]{1,2,0:T(8,128)(2,1)S(1)}) conditional(s32[]{:T(128)} %convert_element_type.55, () %tuple.39, (s32[128]{0:T(128)S(1)}, s32[128]{0:T(128)}, bf16[256,512]{0,1:T(8,128)(2,1)S(1)}, bf16[256,128,16]{1,2,0:T(8,128)(2,1)S(1)}) %tuple.59), branch_computations={%region_0.1_spmd, %region_1.2_spmd} | conditional | flops 138952704 | bytes 161840160 | solution.py:60
  133.8 19.4 %tile.61 = bf16[256,32895]{0,1:T(8,128)(2,1)} reshape(bf16[256,129,255]{0,2,1:T(8,128)(2,1)} %tile.60) | data formatting | bytes 33684480 | tf_op jit(solution)/shard_map/cond/branch_1_fun/while/body/eval_jaxpr/tile | solution.py:24
  153.2 15.1 %slice.58 = bf16[256,32512]{0,1:T(8,128)(2,1)} slice(bf16[256,32895]{0,1:T(8,128)(2,1)} %tile.61), slice={[0:256], [127:32639]} | slice | bytes 33292288 | tf_op jit(solution)/shard_map/cond/branch_1_fun/while/body/eval_jaxpr/slice | solution.py:25
  168.3 18.7 %reshape.189 = bf16[256,128,254]{0,2,1:T(8,128)(2,1)} reshape(bf16[256,32512]{0,1:T(8,128)(2,1)} %slice.58) | data formatting | bytes 33292288 | tf_op jit(solution)/shard_map/cond/branch_1_fun/while/body/eval_jaxpr/reshape | solution.py:26
  194.8 12.4 %copy.21 = bf16[256,128,128]{2,1,0:T(8,128)(2,1)} copy(bf16[256,128,128]{0,2,1:T(8,128)(2,1)} %slice.59) | data formatting | bytes 16777216 | tf_op jit(solution)/shard_map/cond
  218.5 89.2 %conditional.5 = (bf16[256,128,16]{1,2,0:T(8,128)(2,1)}) conditional(s32[]{:T(128)} %convert_element_type.57, () %tuple.41, (s32[128]{0:T(128)S(1)}, s32[128]{0:T(128)}, bf16[256,512]{0,1:T(8,128)(2,1)S(1)}, bf16[256,128,16]{1,2,0:T(8,128)(2,1)S(1)}) %tuple.60), branch_computations={%region_2.3_spmd, %region_3.4_spmd} | conditional | flops 138952704 | bytes 161840160 | solution.py:60
  225.2 19.4 %tile.63 = bf16[256,32895]{0,1:T(8,128)(2,1)} reshape(bf16[256,129,255]{0,2,1:T(8,128)(2,1)} %tile.62) | data formatting | bytes 33684480 | tf_op jit(solution)/shard_map/cond/branch_1_fun/while/body/eval_jaxpr/tile | solution.py:24
  244.7 15.1 %slice.60 = bf16[256,32512]{0,1:T(8,128)(2,1)} slice(bf16[256,32895]{0,1:T(8,128)(2,1)} %tile.63), slice={[0:256], [127:32639]} | slice | bytes 33292288 | tf_op jit(solution)/shard_map/cond/branch_1_fun/while/body/eval_jaxpr/slice | solution.py:25
  259.8 18.7 %reshape.190 = bf16[256,128,254]{0,2,1:T(8,128)(2,1)} reshape(bf16[256,32512]{0,1:T(8,128)(2,1)} %slice.60) | data formatting | bytes 33292288 | tf_op jit(solution)/shard_map/cond/branch_1_fun/while/body/eval_jaxpr/reshape | solution.py:26
  286.3 12.4 %copy.22 = bf16[256,128,128]{2,1,0:T(8,128)(2,1)} copy(bf16[256,128,128]{0,2,1:T(8,128)(2,1)} %slice.61) | data formatting | bytes 16777216 | tf_op jit(solution)/shard_map/cond
  309.9 89.1 %conditional.6 = (bf16[256,128,16]{1,2,0:T(8,128)(2,1)}) conditional(s32[]{:T(128)} %convert_element_type.59, () %tuple.43, (s32[128]{0:T(128)S(1)}, s32[128]{0:T(128)}, bf16[256,512]{0,1:T(8,128)(2,1)S(1)}, bf16[256,128,16]{1,2,0:T(8,128)(2,1)S(1)}) %tuple.61), branch_computations={%region_4.5_spmd, %region_5.6_spmd} | conditional | flops 138952704 | bytes 161840160 | solution.py:60
  316.7 19.4 %tile.65 = bf16[256,32895]{0,1:T(8,128)(2,1)} reshape(bf16[256,129,255]{0,2,1:T(8,128)(2,1)} %tile.64) | data formatting | bytes 33684480 | tf_op jit(solution)/shard_map/cond/branch_1_fun/while/body/eval_jaxpr/tile | solution.py:24
  336.2 15.1 %slice.62 = bf16[256,32512]{0,1:T(8,128)(2,1)} slice(bf16[256,32895]{0,1:T(8,128)(2,1)} %tile.65), slice={[0:256], [127:32639]} | slice | bytes 33292288 | tf_op jit(solution)/shard_map/cond/branch_1_fun/while/body/eval_jaxpr/slice | solution.py:25
  351.3 18.7 %reshape.191 = bf16[256,128,254]{0,2,1:T(8,128)(2,1)} reshape(bf16[256,32512]{0,1:T(8,128)(2,1)} %slice.62) | data formatting | bytes 33292288 | tf_op jit(solution)/shard_map/cond/branch_1_fun/while/body/eval_jaxpr/reshape | solution.py:26
  408.1 19.5 %tile.71 = bf16[256,32895]{0,1:T(8,128)(2,1)} reshape(bf16[256,129,255]{0,2,1:T(8,128)(2,1)} %tile.70) | data formatting | bytes 33684480 | tf_op jit(solution)/shard_map/while/body/eval_jaxpr/tile | solution.py:24
  427.5 15.1 %slice.66 = bf16[256,32512]{0,1:T(8,128)(2,1)} slice(bf16[256,32895]{0,1:T(8,128)(2,1)} %tile.71), slice={[0:256], [127:32639]} | slice | bytes 33292288 | tf_op jit(solution)/shard_map/while/body/eval_jaxpr/slice | solution.py:25
  442.6 18.7 %reshape.193 = bf16[256,128,254]{0,2,1:T(8,128)(2,1)} reshape(bf16[256,32512]{0,1:T(8,128)(2,1)} %slice.66) | data formatting | bytes 33292288 | tf_op jit(solution)/shard_map/while/body/eval_jaxpr/reshape | solution.py:26
  469.2 12.5 %copy.25 = bf16[256,128,128]{2,1,0:T(8,128)(2,1)} copy(bf16[256,128,128]{0,2,1:T(8,128)(2,1)} %slice.67) | data formatting | bytes 16777216
  (64 shorter events, 153.1 us)
Async XLA Ops:
  0.0 35.5 %collective-permute-start.6 = (s32[128]{0:T(128)}, s32[128]{0:T(128)S(1)}, u32[]{:S(2)}, u32[]{:S(2)}) collective-permute-start(s32[128]{0:T(128)} %param.17), channel_id=1, source_target_pairs={{4,0},{5,1},{6,2},{7,3},{8,4},{9,5},{10,6},{11,7},{12,8},{13,9},{1... | collective-permute-start | bytes 1544 | tf_op jit(solution)/shard_map/ppermute | solution.py:10
  1.3 125.7 %collective-permute-start = (s32[128]{0:T(128)}, s32[128]{0:T(128)S(1)}, u32[]{:S(2)}, u32[]{:S(2)}) collective-permute-start(s32[128]{0:T(128)} %param.17), channel_id=1, source_target_pairs={{1,0},{2,1},{3,2},{4,3},{5,4},{6,5},{7,6},{8,7},{9,8},{10,9},{11,1... | collective-permute-start | bytes 1544 | tf_op jit(solution)/shard_map/ppermute | solution.py:10
  2.6 215.9 %collective-permute-start.2 = (s32[128]{0:T(128)}, s32[128]{0:T(128)S(1)}, u32[]{:S(2)}, u32[]{:S(2)}) collective-permute-start(s32[128]{0:T(128)} %param.17), channel_id=1, source_target_pairs={{2,0},{3,1},{4,2},{5,3},{6,4},{7,5},{8,6},{9,7},{10,8},{11,9},{12,... | collective-permute-start | bytes 1544 | tf_op jit(solution)/shard_map/ppermute | solution.py:10
  3.9 306.1 %collective-permute-start.4 = (s32[128]{0:T(128)}, s32[128]{0:T(128)S(1)}, u32[]{:S(2)}, u32[]{:S(2)}) collective-permute-start(s32[128]{0:T(128)} %param.17), channel_id=1, source_target_pairs={{3,0},{4,1},{5,2},{6,3},{7,4},{8,5},{9,6},{10,7},{11,8},{12,9},{13... | collective-permute-start | bytes 1544 | tf_op jit(solution)/shard_map/ppermute | solution.py:10
  103.3 12.5 %copy-start.1 = (s32[128]{0:T(128)S(1)}, s32[128]{0:T(128)}, u32[]{:S(2)}) copy-start(s32[128]{0:T(128)} %get-tuple-element.137) | copy-start | bytes 1540 | tf_op jit(solution)/shard_map/cond
  124.7 363.8 %collective-permute-start.7 = (bf16[256,128,16]{1,2,0:T(8,128)(2,1)}, bf16[256,128,16]{1,2,0:T(8,128)(2,1)}, u32[]{:S(2)}, u32[]{:S(2)}) collective-permute-start(bf16[256,128,16]{1,2,0:T(8,128)(2,1)} %get-tuple-element.155), channel_id=1, source_target_pairs={{0,4},{1,5},{2,6},{3,7},{4,8},{5,9},{6,10},{7,11},{8,12},{9,13},{1... | collective-permute-start | bytes 3145736 | tf_op jit(solution)/shard_map/ppermute | solution.py:10
  194.8 12.5 %copy-start.2 = (s32[128]{0:T(128)S(1)}, s32[128]{0:T(128)}, u32[]{:S(2)}) copy-start(s32[128]{0:T(128)} %get-tuple-element.119) | copy-start | bytes 1540 | tf_op jit(solution)/shard_map/cond
  215.2 273.4 %collective-permute-start.1 = (bf16[256,128,16]{1,2,0:T(8,128)(2,1)S(1)}, bf16[256,128,16]{1,2,0:T(8,128)(2,1)}, u32[]{:S(2)}, u32[]{:S(2)}) collective-permute-start(bf16[256,128,16]{1,2,0:T(8,128)(2,1)S(1)} %get-tuple-element.152), channel_id=1, source_target_pairs={{0,1},{1,2},{2,3},{3,4},{4,5},{5,6},{6,7},{7,8},{8,9},{9,10},{10,1... | collective-permute-start | bytes 3145736 | tf_op jit(solution)/shard_map/ppermute | solution.py:10
  286.3 12.5 %copy-start.3 = (s32[128]{0:T(128)S(1)}, s32[128]{0:T(128)}, u32[]{:S(2)}) copy-start(s32[128]{0:T(128)} %get-tuple-element.123) | copy-start | bytes 1540 | tf_op jit(solution)/shard_map/cond
  307.7 180.9 %collective-permute-start.3 = (bf16[256,128,16]{1,2,0:T(8,128)(2,1)}, bf16[256,128,16]{1,2,0:T(8,128)(2,1)}, u32[]{:S(2)}, u32[]{:S(2)}) collective-permute-start(bf16[256,128,16]{1,2,0:T(8,128)(2,1)} %get-tuple-element.153), channel_id=1, source_target_pairs={{0,2},{1,3},{2,4},{3,5},{4,6},{5,7},{6,8},{7,9},{8,10},{9,11},{10,... | collective-permute-start | bytes 3145736 | tf_op jit(solution)/shard_map/ppermute | solution.py:10
  377.7 12.4 %copy-start.4 = (s32[128]{0:T(128)S(1)}, s32[128]{0:T(128)}, u32[]{:S(2)}) copy-start(s32[128]{0:T(128)} %get-tuple-element.133) | copy-start | bytes 1540 | tf_op jit(solution)/shard_map/cond
  399.1 89.5 %collective-permute-start.5 = (bf16[256,128,16]{1,2,0:T(8,128)(2,1)}, bf16[256,128,16]{1,2,0:T(8,128)(2,1)}, u32[]{:S(2)}, u32[]{:S(2)}) collective-permute-start(bf16[256,128,16]{1,2,0:T(8,128)(2,1)} %get-tuple-element.154), channel_id=1, source_target_pairs={{0,3},{1,4},{2,5},{3,6},{4,7},{5,8},{6,9},{7,10},{8,11},{9,12},{10... | collective-permute-start | bytes 3145736 | tf_op jit(solution)/shard_map/ppermute | solution.py:10
  469.2 12.5 %copy-start = (s32[128]{0:T(128)S(1)}, s32[128]{0:T(128)}, u32[]{:S(2)}) copy-start(s32[128]{0:T(128)} %param.17) | copy-start | bytes 1540
where the time goes:
time: 504 us; the launch traced here: 497 us
  local copies, waits for them, and re-layouts  404 us (80%)
  matrix products  41.1 us (8%)
  blocking collectives  27.8 us (6%)
  starting transfers between devices  15.2 us (3%)
  other arithmetic  8.87 us (2%)
    another operation x10, local copies, waits for them, and re-layouts, row_block(): repeated = jnp.tile(segment, (1, row_step + 1))  129 us
    reshape x5, local copies, waits for them, and re-layouts, row_block(): slab = skewed.reshape(filters, row_step, span - 1)[:, :, :block_rows]  93.4 us
    slice x5, local copies, waits for them, and re-layouts, row_block(): skewed = repeated[:, row_step - 1:row_step - 1 + row_step * (span - 1)]  75.5 us
    cond x12, local copies, waits for them, and re-layouts  49.7 us
    dot_general x5, matrix products, row_block(): jnp.einsum('fts,fsg->ftg', weights, source_major, preferred_element_type=...  41.1 us
    slice x5, local copies, waits for them, and re-layouts, row_block(): slab = skewed.reshape(filters, row_step, span - 1)[:, :, :block_rows]  39.1 us
    all_gather x1, blocking collectives, shards(): all_taps = lax.all_gather(taps, 'ctx', axis=0, tiled=True)  27.8 us
    ppermute x8, starting transfers between devices, shifted(): lax.ppermute(value, axis, [(source, source + steps) for source in range(f...  15.2 us
  transfers between devices with their start and end apart: 8, of which 0 were waited for; matrix products, arithmetic and copies ran while one was open for 90% of the time, Pallas kernels for 0%

commit v1 on v0

v1 whole, which is shorter than its diff:
```python
import functools

import jax
import jax.numpy as jnp
from jax import lax
from jax.experimental import pallas as pl
from jax.experimental.pallas import tpu as pltpu
from jax.sharding import PartitionSpec as P


def shifted(value, axis, steps):
    count = lax.axis_size(axis)
    first, last = (max(0, -steps), min(count, count - steps))
    return lax.ppermute(value, axis, [(source, source + steps) for source in range(first, last)])


def conv_kernel(*refs, lags, rows, group_size, lane_chunk):
    g_refs = refs[:lags + 1]
    p_ref, m_ref, q_ref, o_ref, lhs_ref, rhs_ref = refs[lags + 1:]
    per_chunk = lane_chunk // group_size
    row = lax.broadcasted_iota(jnp.int32, (rows, rows), 0)
    upper = lax.broadcasted_iota(jnp.int32, (rows, rows), 1) >= row
    owner = lax.broadcasted_iota(jnp.int32, (rows, lane_chunk), 1) // group_size
    for k in range(per_chunk):
        tap_row = p_ref[k : k + 1, :]
        rolled = [
            pltpu.roll(
                jnp.broadcast_to(tap_row[:, rows * m : rows * (m + 1)], (rows, rows)),
                0,
                1,
                stride=1,
                stride_axis=0,
            )
            for m in range(lags + 2)
        ]
        for n in range(lags + 1):
            tile = jnp.where(upper, rolled[n + 1], rolled[n]) * m_ref[:, rows * n : rows * (n + 1)]
            lhs_ref[n, :, rows * k : rows * (k + 1)] = tile.astype(jnp.bfloat16)
    acc = jnp.zeros((rows, lane_chunk), jnp.float32)
    for n in range(lags + 1):
        source = g_refs[n][...]
        for k in range(per_chunk):
            rhs_ref[rows * k : rows * (k + 1), :] = jnp.where(owner == k, source, jnp.zeros_like(source))
        term = jnp.dot(lhs_ref[n], rhs_ref[...], preferred_element_type=jnp.float32)
        if n < lags:
            term = term.astype(jnp.bfloat16).astype(jnp.float32)
        acc = acc + term
    o_ref[...] = (q_ref[...].astype(jnp.float32) * acc).astype(o_ref.dtype)


def shards(queries, keys, values, taps, segment_ids):
    rows = queries.shape[0]
    channels = queries.shape[1]
    filters = taps.shape[1]
    group_size = channels // filters
    gated = (keys.astype(jnp.float32) * values.astype(jnp.float32)).astype(jnp.bfloat16)
    all_taps = lax.all_gather(taps, "ctx", axis=0, tiled=True)
    filt_len = all_taps.shape[0]
    lags = filt_len // rows
    padded = jnp.concatenate(
        [
            jnp.zeros((filters, rows + 1), jnp.float32),
            all_taps.T[:, ::-1].astype(jnp.float32),
            jnp.zeros((filters, rows - 1), jnp.float32),
        ],
        axis=1,
    )
    sources = [shifted(gated, "ctx", lag) for lag in range(lags, 0, -1)] + [gated]
    seg_sources = [shifted(segment_ids, "ctx", lag) for lag in range(lags, 0, -1)]
    seg_all = jnp.concatenate(seg_sources + [segment_ids])
    mask = (segment_ids[:, None] == seg_all[None, :]).astype(jnp.float32)
    lane_chunk = 128
    filt_per_chunk = lane_chunk // group_size
    span = (lags + 1) * rows
    kernel = functools.partial(
        conv_kernel, lags=lags, rows=rows, group_size=group_size, lane_chunk=lane_chunk
    )
    block = pl.BlockSpec((rows, lane_chunk), lambda j: (0, j))
    return pl.pallas_call(
        kernel,
        grid=(channels // lane_chunk,),
        in_specs=[block] * (lags + 1)
        + [
            pl.BlockSpec((filt_per_chunk, (lags + 2) * rows), lambda j: (j, 0)),
            pl.BlockSpec((rows, span), lambda j: (0, 0)),
            block,
        ],
        out_specs=block,
        out_shape=jax.ShapeDtypeStruct((rows, channels), jnp.bfloat16),
        scratch_shapes=[
            pltpu.VMEM((lags + 1, rows, rows * filt_per_chunk), jnp.bfloat16),
            pltpu.VMEM((rows * filt_per_chunk, lane_chunk), jnp.bfloat16),
        ],
    )(*sources, padded, mask, queries)


def solution(mesh):
    return jax.shard_map(
        shards,
        mesh=mesh,
        in_specs=(
            P(("dp", "ctx"), None),
            P(("dp", "ctx"), None),
            P(("dp", "ctx"), None),
            P("ctx", None),
            P(("dp", "ctx")),
        ),
        out_specs=P(("dp", "ctx"), None),
        check_vma=False,
    )
```

time: 504 us -> 159 us (0.32)
  the two profiles are of different devices: /device:TPU:0 before, /device:TPU:25 now
where the time goes in v1:
time: 159 us; the launch traced here: 156 us
  blocking collectives  83.8 us (53%)
  Pallas kernels  42.8 us (27%)
  starting transfers between devices  14.6 us (9%)
  waiting for transfers between devices  8.77 us (6%)
  other arithmetic  3.84 us (2%)
  local copies, waits for them, and re-layouts  2.09 us (1%)
    all_gather x1, blocking collectives, shards(): all_taps = lax.all_gather(taps, 'ctx', axis=0, tiled=True)  83.8 us
    pallas_call x1, Pallas kernels, shards(): pl.pallas_call(kernel, grid=(channels // lane_chunk,), in_specs=[block] *...  42.8 us
    ppermute x8, starting transfers between devices, shifted(): lax.ppermute(value, axis, [(source, source + steps) for source in range(f...  14.6 us
    ppermute x8, waiting for transfers between devices, shifted(): lax.ppermute(value, axis, [(source, source + steps) for source in range(f...  8.77 us
  transfers between devices with their start and end apart: 8, of which 3 were waited for; matrix products, arithmetic and copies ran while one was open for 2% of the time, Pallas kernels for 0%

profile of v1, /device:TPU:25, one launch (start us, length us, event | category | flops | bytes accessed | tf_op | source)
XLA Modules:
  0.0 156.1 jit_solution(595216068920973839)
XLA Ops:
  0.0 1.8 %multiply_convert_fusion.refs_4_ = bf16[128,4096]{1,0:T(8,128)(2,1)S(1)} fusion(bf16[128,4096]{1,0:T(8,128)(2,1)} %param.7, bf16[128,4096]{1,0:T(8,128)(2,1)} %param.6), kind=kLoop, calls=%fused_computation | loop fusion | flops 2097152 | bytes 3145728 | tf_op jit(solution)/shard_map/convert_element_type | solution.py:56
  1.8 3.7 %collective-permute-start.3 = (bf16[128,4096]{1,0:T(8,128)(2,1)S(1)}, bf16[128,4096]{1,0:T(8,128)(2,1)S(1)}, u32[]{:S(2)}, u32[]{:S(2)}) collective-permute-start(bf16[128,4096]{1,0:T(8,128)(2,1)S(1)} %multiply_convert_fusion.refs_4_), channel_id=1, source_target_pairs={{0,1},{1,2},{2,3},{3,4},{4,5},{5,6},{6,7},{7,8},{8,9},{9,10},{10,1... | collective-permute-start | bytes 3145736 | tf_op jit(solution)/shard_map/ppermute | solution.py:14
  5.5 1.9 %collective-permute-start.2 = (bf16[128,4096]{1,0:T(8,128)(2,1)S(1)}, bf16[128,4096]{1,0:T(8,128)(2,1)}, u32[]{:S(2)}, u32[]{:S(2)}) collective-permute-start(bf16[128,4096]{1,0:T(8,128)(2,1)S(1)} %multiply_convert_fusion.refs_4_), channel_id=1, source_target_pairs={{0,2},{1,3},{2,4},{3,5},{4,6},{5,7},{6,8},{7,9},{8,10},{9,11},{10,... | collective-permute-start | bytes 3145736 | tf_op jit(solution)/shard_map/ppermute | solution.py:14
  7.5 1.3 collective-permute-start.1
  8.8 1.3 collective-permute-start
  10.1 1.3 collective-permute-start.4
  11.4 83.8 %all_gather.3 = bf16[512,256]{1,0:T(8,128)(2,1)S(1)} all-gather(bf16[32,256]{1,0:T(8,128)(2,1)S(1)} %copy-done.2), channel_id=1, replica_groups=mesh['dp'=2,'ctx'=16] {'ctx'}, dimensions={0}, use_global_device_ids=true | all-gather | bytes 278528 | tf_op jit(solution)/shard_map/all_gather | solution.py:57
  95.3 0.1 pad.2.clone
  95.3 0.1 copy.7
  95.5 0.8 rev.3
  96.3 0.1 convert_element_type.18
  96.4 1.2 maximum_maximum_fusion.refs_5_
  97.6 1.3 collective-permute-start.5
  98.9 4.4 %collective-permute-done.5 = s32[128]{0:T(128)S(1)} collective-permute-done((s32[128]{0:T(128)S(1)}, s32[128]{0:T(128)S(1)}, u32[]{:S(2)}, u32[]{:S(2)}) %collective-permute-start.5) | collective-permute-done | bytes 544 | tf_op jit(solution)/shard_map/ppermute | solution.py:14
  103.3 1.9 %collective-permute-start.6 = (s32[128]{0:T(128)S(1)}, s32[128]{0:T(128)S(1)}, u32[]{:S(2)}, u32[]{:S(2)}) collective-permute-start(s32[128]{0:T(128)S(1)} %copy-done.3), channel_id=1, source_target_pairs={{0,2},{1,3},{2,4},{3,5},{4,6},{5,7},{6,8},{7,9},{8,10},{9,11},{10,... | collective-permute-start | bytes 1544 | tf_op jit(solution)/shard_map/ppermute | solution.py:14
  105.2 3.2 %collective-permute-done.6 = s32[128]{0:T(128)S(1)} collective-permute-done((s32[128]{0:T(128)S(1)}, s32[128]{0:T(128)S(1)}, u32[]{:S(2)}, u32[]{:S(2)}) %collective-permute-start.6) | collective-permute-done | bytes 544 | tf_op jit(solution)/shard_map/ppermute | solution.py:14
  108.5 1.9 %collective-permute-start.7 = (s32[128]{0:T(128)S(1)}, s32[128]{0:T(128)S(1)}, u32[]{:S(2)}, u32[]{:S(2)}) collective-permute-start(s32[128]{0:T(128)S(1)} %copy-done.3), channel_id=1, source_target_pairs={{0,1},{1,2},{2,3},{3,4},{4,5},{5,6},{6,7},{7,8},{8,9},{9,10},{10,1... | collective-permute-start | bytes 1544 | tf_op jit(solution)/shard_map/ppermute | solution.py:14
  110.4 1.1 collective-permute-done.7
  111.5 0.8 compare_convert_fusion.refs_6_
  112.3 0.0 collective-permute-done.3.refs_3_
  112.3 0.0 collective-permute-done.2.refs_2_
  112.3 0.0 collective-permute-done.refs_0_
  112.4 1.0 copy-done.1
  113.3 42.8 %shard_map.55 = bf16[128,4096]{1,0:T(8,128)(2,1)} custom-call(bf16[128,4096]{1,0:T(8,128)(2,1)} %collective-permute-done.refs_0_, bf16[128,4096]{1,0:T(8,128)(2,1)} %collective-permute-done.1.refs_1_, bf16[128,4096]{1,0:T(8,128)(2,1)} %collective-permute-done.2.refs_2_, bf16[128,4096]{1,0:T(8,128)(2,1)} %copy-done.1, bf16[128,4096]{1,0:T(8,128)(2,1)} %copy-done, ...), custom_call_target="tpu_custom_call" | custom-call | tf_op jit(solution)/shard_map/pallas_call | solution.py:79
  (18 shorter events, 0.1 us)
Async XLA Ops:
  0.0 10.1 %copy-start.3 = (s32[128]{0:T(128)S(1)}, s32[128]{0:T(128)}, u32[]{:S(2)}) copy-start(s32[128]{0:T(128)} %param.9) | copy-start | bytes 1540
  0.0 11.4 %copy-start.2 = (bf16[32,256]{1,0:T(8,128)(2,1)S(1)}, bf16[32,256]{1,0:T(8,128)(2,1)}, u32[]{:S(2)}) copy-start(bf16[32,256]{1,0:T(8,128)(2,1)} %param.8) | copy-start | bytes 49156
  1.8 94.6 %copy-start = (bf16[128,4096]{1,0:T(8,128)(2,1)}, bf16[128,4096]{1,0:T(8,128)(2,1)S(1)}, u32[]{:S(2)}) copy-start(bf16[128,4096]{1,0:T(8,128)(2,1)S(1)} %multiply_convert_fusion.refs_4_) | copy-start | bytes 3145732
  1.8 110.5 %collective-permute-start.3 = (bf16[128,4096]{1,0:T(8,128)(2,1)S(1)}, bf16[128,4096]{1,0:T(8,128)(2,1)S(1)}, u32[]{:S(2)}, u32[]{:S(2)}) collective-permute-start(bf16[128,4096]{1,0:T(8,128)(2,1)S(1)} %multiply_convert_fusion.refs_4_), channel_id=1, source_target_pairs={{0,1},{1,2},{2,3},{3,4},{4,5},{5,6},{6,7},{7,8},{8,9},{9,10},{10,1... | collective-permute-start | bytes 3145736 | tf_op jit(solution)/shard_map/ppermute | solution.py:14
  5.5 106.8 %collective-permute-start.2 = (bf16[128,4096]{1,0:T(8,128)(2,1)S(1)}, bf16[128,4096]{1,0:T(8,128)(2,1)}, u32[]{:S(2)}, u32[]{:S(2)}) collective-permute-start(bf16[128,4096]{1,0:T(8,128)(2,1)S(1)} %multiply_convert_fusion.refs_4_), channel_id=1, source_target_pairs={{0,2},{1,3},{2,4},{3,5},{4,6},{5,7},{6,8},{7,9},{8,10},{9,11},{10,... | collective-permute-start | bytes 3145736 | tf_op jit(solution)/shard_map/ppermute | solution.py:14
  7.5 104.9 %collective-permute-start.1 = (bf16[128,4096]{1,0:T(8,128)(2,1)S(1)}, bf16[128,4096]{1,0:T(8,128)(2,1)}, u32[]{:S(2)}, u32[]{:S(2)}) collective-permute-start(bf16[128,4096]{1,0:T(8,128)(2,1)S(1)} %multiply_convert_fusion.refs_4_), channel_id=1, source_target_pairs={{0,3},{1,4},{2,5},{3,6},{4,7},{5,8},{6,9},{7,10},{8,11},{9,12},{10... | collective-permute-start | bytes 3145736 | tf_op jit(solution)/shard_map/ppermute | solution.py:14
  8.8 103.6 %collective-permute-start = (bf16[128,4096]{1,0:T(8,128)(2,1)S(1)}, bf16[128,4096]{1,0:T(8,128)(2,1)}, u32[]{:S(2)}, u32[]{:S(2)}) collective-permute-start(bf16[128,4096]{1,0:T(8,128)(2,1)S(1)} %multiply_convert_fusion.refs_4_), channel_id=1, source_target_pairs={{0,4},{1,5},{2,6},{3,7},{4,8},{5,9},{6,10},{7,11},{8,12},{9,13},{1... | collective-permute-start | bytes 3145736 | tf_op jit(solution)/shard_map/ppermute | solution.py:14
  10.1 87.5 %collective-permute-start.4 = (s32[128]{0:T(128)S(1)}, s32[128]{0:T(128)S(1)}, u32[]{:S(2)}, u32[]{:S(2)}) collective-permute-start(s32[128]{0:T(128)S(1)} %copy-done.3), channel_id=1, source_target_pairs={{0,4},{1,5},{2,6},{3,7},{4,8},{5,9},{6,10},{7,11},{8,12},{9,13},{1... | collective-permute-start | bytes 1544 | tf_op jit(solution)/shard_map/ppermute | solution.py:14
  97.6 5.7 %collective-permute-start.5 = (s32[128]{0:T(128)S(1)}, s32[128]{0:T(128)S(1)}, u32[]{:S(2)}, u32[]{:S(2)}) collective-permute-start(s32[128]{0:T(128)S(1)} %copy-done.3), channel_id=1, source_target_pairs={{0,3},{1,4},{2,5},{3,6},{4,7},{5,8},{6,9},{7,10},{8,11},{9,12},{10... | collective-permute-start | bytes 1544 | tf_op jit(solution)/shard_map/ppermute | solution.py:14
  103.3 5.2 %collective-permute-start.6 = (s32[128]{0:T(128)S(1)}, s32[128]{0:T(128)S(1)}, u32[]{:S(2)}, u32[]{:S(2)}) collective-permute-start(s32[128]{0:T(128)S(1)} %copy-done.3), channel_id=1, source_target_pairs={{0,2},{1,3},{2,4},{3,5},{4,6},{5,7},{6,8},{7,9},{8,10},{9,11},{10,... | collective-permute-start | bytes 1544 | tf_op jit(solution)/shard_map/ppermute | solution.py:14
  108.5 3.0 %collective-permute-start.7 = (s32[128]{0:T(128)S(1)}, s32[128]{0:T(128)S(1)}, u32[]{:S(2)}, u32[]{:S(2)}) collective-permute-start(s32[128]{0:T(128)S(1)} %copy-done.3), channel_id=1, source_target_pairs={{0,1},{1,2},{2,3},{3,4},{4,5},{5,6},{6,7},{7,8},{8,9},{9,10},{10,1... | collective-permute-start | bytes 1544 | tf_op jit(solution)/shard_map/ppermute | solution.py:14
  112.3 1.0 copy-start.1

commit v2 on v1

v2 whole, which is shorter than its diff:
```python
import functools

import jax
import jax.numpy as jnp
from jax import lax
from jax.experimental import pallas as pl
from jax.experimental.pallas import tpu as pltpu
from jax.sharding import PartitionSpec as P


def shifted(value, axis, steps):
    count = lax.axis_size(axis)
    first, last = (max(0, -steps), min(count, count - steps))
    return lax.ppermute(value, axis, [(source, source + steps) for source in range(first, last)])


def swapped(value, axis):
    count = lax.axis_size(axis)
    return lax.ppermute(value, axis, [(source, source ^ 1) for source in range(count)])


def conv_kernel(core_ref, *refs, lags, rows, group_size):
    g_refs = list(refs[:lags + 1])
    p_ref, m_ref, q_ref, o_ref, lhs_ref, rhs_ref = refs[lags + 1:]
    lane_chunk = q_ref.shape[1]
    per_chunk = lane_chunk // group_size
    row = lax.broadcasted_iota(jnp.int32, (rows, rows), 0)
    upper = lax.broadcasted_iota(jnp.int32, (rows, rows), 1) >= row
    owner = lax.broadcasted_iota(jnp.int32, (rows, lane_chunk), 1) // group_size
    for k in range(per_chunk):
        tap_row = p_ref[k : k + 1, :]
        rolled = [
            pltpu.roll(
                jnp.broadcast_to(tap_row[:, rows * m : rows * (m + 1)], (rows, rows)),
                0,
                1,
                stride=1,
                stride_axis=0,
            )
            for m in range(lags + 2)
        ]
        for n in range(lags + 1):
            tile = jnp.where(upper, rolled[n + 1], rolled[n]) * m_ref[:, rows * n : rows * (n + 1)]
            lhs_ref[n, :, rows * k : rows * (k + 1)] = tile.astype(jnp.bfloat16)
    even = core_ref[0] == 0
    near, far = g_refs[lags - 1][...], g_refs[lags - 3][...]
    blocks = [g[...] for g in g_refs]
    blocks[lags - 1] = jnp.where(even, near, far)
    blocks[lags - 3] = jnp.where(even, far, near)
    acc = jnp.zeros((rows, lane_chunk), jnp.float32)
    for n in range(lags + 1):
        source = blocks[n]
        for k in range(per_chunk):
            rhs_ref[rows * k : rows * (k + 1), :] = jnp.where(owner == k, source, jnp.zeros_like(source))
        term = jnp.dot(lhs_ref[n], rhs_ref[...], preferred_element_type=jnp.float32)
        if n < lags:
            term = term.astype(jnp.bfloat16).astype(jnp.float32)
        acc = acc + term
    o_ref[...] = (q_ref[...].astype(jnp.float32) * acc).astype(o_ref.dtype)


def shards(queries, keys, values, taps, segment_ids):
    rows = queries.shape[0]
    channels = queries.shape[1]
    filters = taps.shape[1]
    group_size = channels // filters
    ctx_count = lax.axis_size("ctx")
    own_index = lax.axis_index("ctx")
    core = own_index % 2
    tap_rows = taps.shape[0]
    filt_len = tap_rows * ctx_count
    lags = filt_len // rows
    packed = jnp.zeros((filt_len + ctx_count, filters), jnp.float32)
    packed = lax.dynamic_update_slice(packed, taps.astype(jnp.float32), (own_index * tap_rows, 0))
    seg_row = jnp.zeros((1, filters), jnp.float32).at[0, :rows].set(segment_ids.astype(jnp.float32))
    packed = lax.dynamic_update_slice(packed, seg_row, (filt_len + own_index, 0))
    packed = lax.psum(packed, "ctx")
    all_taps = packed[:filt_len]
    all_segs = packed[filt_len:, :rows].astype(jnp.int32)
    gated = (keys.astype(jnp.float32) * values.astype(jnp.float32)).astype(jnp.bfloat16)
    padded = jnp.concatenate(
        [
            jnp.zeros((filters, rows + 1), jnp.float32),
            all_taps.T[:, ::-1],
            jnp.zeros((filters, rows - 1), jnp.float32),
        ],
        axis=1,
    )
    seg_sources = [
        lax.dynamic_index_in_dim(all_segs, jnp.maximum(own_index - lag, 0), 0, keepdims=False)
        for lag in range(lags, -1, -1)
    ]
    mask = (segment_ids[:, None] == jnp.concatenate(seg_sources)[None, :]).astype(jnp.float32)
    two_back = shifted(gated, "ctx", 2)
    four_back = shifted(gated, "ctx", 4)
    swap_a = swapped(two_back, "ctx")
    swap_b = swapped(jnp.where(core == 1, four_back, gated), "ctx")
    sources = [four_back, swap_b, two_back, swap_a, gated]
    lane_chunk = 128
    per_chunk = lane_chunk // group_size
    span = (lags + 1) * rows
    kernel = functools.partial(conv_kernel, lags=lags, rows=rows, group_size=group_size)
    block = pl.BlockSpec((rows, lane_chunk), lambda j, c: (0, j))
    return pl.pallas_call(
        kernel,
        grid_spec=pltpu.PrefetchScalarGridSpec(
            num_scalar_prefetch=1,
            grid=(channels // lane_chunk,),
            in_specs=[block] * (lags + 1)
            + [
                pl.BlockSpec((per_chunk, (lags + 2) * rows), lambda j, c: (j, 0)),
                pl.BlockSpec((rows, span), lambda j, c: (0, 0)),
                block,
            ],
            out_specs=block,
            scratch_shapes=[
                pltpu.VMEM((lags + 1, rows, rows * per_chunk), jnp.bfloat16),
                pltpu.VMEM((rows * per_chunk, lane_chunk), jnp.bfloat16),
            ],
        ),
        out_shape=jax.ShapeDtypeStruct((rows, channels), jnp.bfloat16),
    )(jnp.reshape(core, (1,)).astype(jnp.int32), *sources, padded, mask, queries)


def solution(mesh):
    return jax.shard_map(
        shards,
        mesh=mesh,
        in_specs=(
            P(("dp", "ctx"), None),
            P(("dp", "ctx"), None),
            P(("dp", "ctx"), None),
            P("ctx", None),
            P(("dp", "ctx")),
        ),
        out_specs=P(("dp", "ctx"), None),
        check_vma=False,
    )
```

time: 159 us -> 172 us (1.082)
  waiting for transfers between devices: 8.77 us -> 93.1 us
  blocking collectives: 83.8 us -> 0 us
  between operations: 0.18 us -> 13.6 us
  starting transfers between devices: 14.6 us -> 6.78 us
  local copies, waits for them, and re-layouts: 2.09 us -> 6.42 us
  other arithmetic: 3.84 us -> 7.09 us
    psum x0 -> x1, waiting for transfers between devices: none -> 93.1 us  [shards(): packed = lax.psum(packed, 'ctx')]
    all_gather x1 -> x0, blocking collectives: 83.8 us -> none  [shards(): all_taps = lax.all_gather(taps, 'ctx', axis=0, tiled=True)]
    ppermute x8 -> x2, starting transfers between devices: 14.6 us -> 4.44 us  [shifted(): lax.ppermute(value, axis, [(source, source + steps) for source in range(f...]
    ppermute x8 -> x2, waiting for transfers between devices: 8.77 us -> 0.01 us  [shifted(): lax.ppermute(value, axis, [(source, source + steps) for source in range(f...]
    ppermute x0 -> x2, starting transfers between devices: none -> 2.34 us  [swapped(): lax.ppermute(value, axis, [(source, source ^ 1) for source in range(count)])]
    dynamic_update_slice x0 -> x2, local copies, waits for them, and re-layouts: none -> 1.95 us  [the longest x1 1.33 us: shards(): lax.dynamic_update_slice(packed, taps.astype(jnp.float32), (own_index * t...]
  transfers between devices with their start and end apart: 8 -> 5, of which waited for: 3 -> 1; matrix products, arithmetic and copies ran while one was open for 2% -> 6% of each run, Pallas kernels for 0% -> 0%
where the time goes in v2:
time: 172 us; the launch traced here: 170 us
  waiting for transfers between devices  93.1 us (54%)
  Pallas kernels  42.9 us (25%)
  between operations  13.6 us (8%)
  other arithmetic  7.09 us (4%)
  starting transfers between devices  6.78 us (4%)
  local copies, waits for them, and re-layouts  6.42 us (4%)
    psum x1, waiting for transfers between devices, shards(): packed = lax.psum(packed, 'ctx')  93.1 us
    pallas_call x1, Pallas kernels, shards(): pl.pallas_call(kernel, grid_spec=pltpu.PrefetchScalarGridSpec(num_scalar_...  42.9 us
    ppermute x2, starting transfers between devices, shifted(): lax.ppermute(value, axis, [(source, source + steps) for source in range(f...  4.44 us
  transfers between devices with their start and end apart: 5, of which 1 were waited for; matrix products, arithmetic and copies ran while one was open for 6% of the time, Pallas kernels for 0%

profile of v2, /device:TPU:25, one launch (start us, length us, event | category | flops | bytes accessed | tf_op | source)
XLA Modules:
  0.0 169.9 jit_solution(2721525278713102072)
XLA Ops:
  6.5 1.8 %multiply_convert_fusion.refs_4_ = bf16[128,4096]{1,0:T(8,128)(2,1)S(1)} fusion(bf16[128,4096]{1,0:T(8,128)(2,1)} %param.9, bf16[128,4096]{1,0:T(8,128)(2,1)} %param.8), kind=kLoop, calls=%fused_computation | loop fusion | flops 2097152 | bytes 3145728 | tf_op jit(solution)/shard_map/convert_element_type | solution.py:80
  8.4 1.3 collective-permute-start
  9.7 0.1 copy.10
  9.8 0.6 compare_reduce_fusion
  10.4 0.6 fusion
  11.1 0.1 copy.11
  11.3 1.3 dynamic_update_slice.6
  12.6 0.6 dynamic_update_slice.7
  13.2 0.8 copy-done.2
  14.1 3.1 %collective-permute-start.2 = (bf16[128,4096]{1,0:T(8,128)(2,1)S(1)}, bf16[128,4096]{1,0:T(8,128)(2,1)}, u32[]{:S(2)}, u32[]{:S(2)}) collective-permute-start(bf16[128,4096]{1,0:T(8,128)(2,1)S(1)} %multiply_convert_fusion.refs_4_), channel_id=1, source_target_pairs={{0,2},{1,3},{2,4},{3,5},{4,6},{5,7},{6,8},{7,9},{8,10},{9,11},{10,... | collective-permute-start | bytes 3145736 | tf_op jit(solution)/shard_map/ppermute | solution.py:14
  17.3 0.1 pad.7.clone
  17.4 93.1 %all-reduce.3.cloned.1.call-done = f32[528,256]{0,1:T(8,128)} async-done(((f32[528,256]{0,1:T(8,128)}), f32[528,256]{0,1:T(8,128)}) %all-reduce.3.cloned.1.call-update) | async-done | bytes 540688 | tf_op jit(solution)/shard_map/psum | solution.py:77
  110.5 1.1 slice_bitcast_fusion
  111.6 1.2 broadcast_select_fusion
  112.7 0.1 copy-done.1
  112.9 2.3 %collective-permute-start.1 = (bf16[128,4096]{1,0:T(8,128)(2,1)}, bf16[128,4096]{1,0:T(8,128)(2,1)}, u32[]{:S(2)}, u32[]{:S(2)}) collective-permute-start(bf16[128,4096]{1,0:T(8,128)(2,1)} %broadcast_select_fusion), channel_id=1, source_target_pairs={{0,1},{1,0},{2,3},{3,2},{4,5},{5,4},{6,7},{7,6},{8,9},{9,8},{10,11... | collective-permute-start | bytes 3145736 | tf_op jit(solution)/shard_map/ppermute | solution.py:19
  115.2 0.8 slice_convert_fusion
  116.1 0.7 rev.3
  116.8 0.3 dynamic-slice_reduce_fusion
  117.2 0.8 compare_convert_fusion.refs_6_
  118.0 1.1 maximum_maximum_fusion.refs_5_
  119.2 0.0 collective-permute-done.3.refs_3_
  119.2 1.0 copy-done.3
  120.2 42.9 %shard_map.55 = bf16[128,4096]{1,0:T(8,128)(2,1)} custom-call(s32[1]{0:T(128)} %bitcast.core_ref, bf16[128,4096]{1,0:T(8,128)(2,1)} %copy-done.1, bf16[128,4096]{1,0:T(8,128)(2,1)} %collective-permute-done.1.refs_1_, bf16[128,4096]{1,0:T(8,128)(2,1)} %collective-permute-done.2.refs_2_, bf16[128,4096]{1,0:T(8,128)(2,1)} %copy-done.3, ...), custom_call_target="tpu_custom_call" | custom-call | tf_op jit(solution)/shard_map/pallas_call | solution.py:104
  (26 shorter events, 0.1 us)
Async XLA Ops:
  6.5 3.1 %copy-start.4 = (bf16[32,256]{1,0:T(8,128)(2,1)S(1)}, bf16[32,256]{1,0:T(8,128)(2,1)}, u32[]{:S(2)}) copy-start(bf16[32,256]{1,0:T(8,128)(2,1)} %param.10) | copy-start | bytes 49156
  6.5 3.9 %copy-start.5 = (s32[128]{0:T(128)S(1)}, s32[128]{0:T(128)}, u32[]{:S(2)}) copy-start(s32[128]{0:T(128)} %param.11) | copy-start | bytes 1540
  6.5 103.9 %all-reduce.3.cloned.1.call-start = ((), (), s32[]{:S(2)}) async-start(), calls=%async_computation | async-start | bytes 1310720 | tf_op jit(solution)/shard_map/psum | solution.py:77
  8.4 103.2 %copy-start = (bf16[128,4096]{1,0:T(8,128)(2,1)}, bf16[128,4096]{1,0:T(8,128)(2,1)S(1)}, u32[]{:S(2)}) copy-start(bf16[128,4096]{1,0:T(8,128)(2,1)S(1)} %multiply_convert_fusion.refs_4_) | copy-start | bytes 3145732
  8.4 103.2 %collective-permute-start = (bf16[128,4096]{1,0:T(8,128)(2,1)S(1)}, bf16[128,4096]{1,0:T(8,128)(2,1)S(1)}, u32[]{:S(2)}, u32[]{:S(2)}) collective-permute-start(bf16[128,4096]{1,0:T(8,128)(2,1)S(1)} %multiply_convert_fusion.refs_4_), channel_id=1, source_target_pairs={{0,4},{1,5},{2,6},{3,7},{4,8},{5,9},{6,10},{7,11},{8,12},{9,13},{1... | collective-permute-start | bytes 3145736 | tf_op jit(solution)/shard_map/ppermute | solution.py:14
  13.2 0.8 copy-start.2
  14.1 101.1 %collective-permute-start.2 = (bf16[128,4096]{1,0:T(8,128)(2,1)S(1)}, bf16[128,4096]{1,0:T(8,128)(2,1)}, u32[]{:S(2)}, u32[]{:S(2)}) collective-permute-start(bf16[128,4096]{1,0:T(8,128)(2,1)S(1)} %multiply_convert_fusion.refs_4_), channel_id=1, source_target_pairs={{0,2},{1,3},{2,4},{3,5},{4,6},{5,7},{6,8},{7,9},{8,10},{9,11},{10,... | collective-permute-start | bytes 3145736 | tf_op jit(solution)/shard_map/ppermute | solution.py:14
  111.6 1.3 copy-start.1
  112.9 6.3 %collective-permute-start.1 = (bf16[128,4096]{1,0:T(8,128)(2,1)}, bf16[128,4096]{1,0:T(8,128)(2,1)}, u32[]{:S(2)}, u32[]{:S(2)}) collective-permute-start(bf16[128,4096]{1,0:T(8,128)(2,1)} %broadcast_select_fusion), channel_id=1, source_target_pairs={{0,1},{1,0},{2,3},{3,2},{4,5},{5,4},{6,7},{7,6},{8,9},{9,8},{10,11... | collective-permute-start | bytes 3145736 | tf_op jit(solution)/shard_map/ppermute | solution.py:19
  115.2 4.0 %collective-permute-start.3 = (bf16[128,4096]{1,0:T(8,128)(2,1)}, bf16[128,4096]{1,0:T(8,128)(2,1)S(1)}, u32[]{:S(2)}, u32[]{:S(2)}) collective-permute-start(bf16[128,4096]{1,0:T(8,128)(2,1)} %collective-permute-done.2.refs_2_), channel_id=1, source_target_pairs={{0,1},{1,0},{2,3},{3,2},{4,5},{5,4},{6,7},{7,6},{8,9},{9,8},{10,11... | collective-permute-start | bytes 3145736 | tf_op jit(solution)/shard_map/ppermute | solution.py:19
  119.2 1.0 copy-start.3
Sparse Core Ops, SparseCore 0:
  14.2 96.1 all-reduce.2

commit v3 on v2

--- a/solution.py
+++ b/solution.py
@@ -70,13 +70,12 @@
     tap_rows = taps.shape[0]
     filt_len = tap_rows * ctx_count
     lags = filt_len // rows
-    packed = jnp.zeros((filt_len + ctx_count, filters), jnp.float32)
-    packed = lax.dynamic_update_slice(packed, taps.astype(jnp.float32), (own_index * tap_rows, 0))
     seg_row = jnp.zeros((1, filters), jnp.float32).at[0, :rows].set(segment_ids.astype(jnp.float32))
-    packed = lax.dynamic_update_slice(packed, seg_row, (filt_len + own_index, 0))
-    packed = lax.psum(packed, "ctx")
-    all_taps = packed[:filt_len]
-    all_segs = packed[filt_len:, :rows].astype(jnp.int32)
+    packed = jnp.concatenate([taps.astype(jnp.float32), seg_row], axis=0)
+    packed = lax.all_gather(packed, "ctx", axis=0, tiled=False)
+    packed, keys, values = lax.optimization_barrier((packed, keys, values))
+    all_taps = packed[:, :tap_rows].reshape(filt_len, filters)
+    all_segs = packed[:, tap_rows, :rows].astype(jnp.int32)
     gated = (keys.astype(jnp.float32) * values.astype(jnp.float32)).astype(jnp.bfloat16)
     padded = jnp.concatenate(
         [

time: 172 us -> 121 us (0.70); the launches traced: 170 us -> 121 us
  waiting for transfers between devices: 93.1 us -> 43.1 us
  blocking collectives: 0 us -> 19.1 us
  between operations: 13.6 us -> 0.16 us
  local copies, waits for them, and re-layouts: 6.42 us -> 2.26 us
    psum x1 -> x0, waiting for transfers between devices: 93.1 us -> none  [shards(): packed = lax.psum(packed, 'ctx')]
    ppermute x2, waiting for transfers between devices: 0.01 us -> 43.1 us  [shifted(): lax.ppermute(value, axis, [(source, source + steps) for source in range(f...]
    all_gather x0 -> x1, blocking collectives: none -> 19.1 us  [shards(): packed = lax.all_gather(packed, 'ctx', axis=0, tiled=False)]
    dynamic_update_slice x2 -> x0, local copies, waits for them, and re-layouts: 1.95 us -> none  [the longest x1 1.33 us: shards(): lax.dynamic_update_slice(packed, taps.astype(jnp.float32), (own_index * t...]
  transfers between devices with their start and end apart: 5 -> 4, of which waited for: 1 -> 2; matrix products, arithmetic and copies ran while one was open for 6% -> 4% of each run, Pallas kernels for 0% -> 0%
where the time goes in v3:
time: 121 us
  waiting for transfers between devices  43.1 us (36%)
  Pallas kernels  42.9 us (35%)
  blocking collectives  19.1 us (16%)
  other arithmetic  7.61 us (6%)
  starting transfers between devices  6.03 us (5%)
  local copies, waits for them, and re-layouts  2.26 us (2%)
    ppermute x2, waiting for transfers between devices, shifted(): lax.ppermute(value, axis, [(source, source + steps) for source in range(f...  43.1 us
    pallas_call x1, Pallas kernels, shards(): pl.pallas_call(kernel, grid_spec=pltpu.PrefetchScalarGridSpec(num_scalar_...  42.9 us
    all_gather x1, blocking collectives, shards(): packed = lax.all_gather(packed, 'ctx', axis=0, tiled=False)  19.1 us
    ppermute x2, starting transfers between devices, shifted(): lax.ppermute(value, axis, [(source, source + steps) for source in range(f...  3.89 us
  transfers between devices with their start and end apart: 4, of which 2 were waited for; matrix products, arithmetic and copies ran while one was open for 4% of the time, Pallas kernels for 0%

profile of v3, /device:TPU:25, one launch (start us, length us, event | category | flops | bytes accessed | tf_op | source)
XLA Modules:
  0.0 121.1 jit_solution(13208157183624874055)
XLA Ops:
  0.0 0.6 compare_reduce_fusion
  0.6 0.7 convert_element_type.22
  1.4 1.3 %fusion.1 = f32[1,128]{1,0:T(1,128)S(1)} fusion(pred[]{:T(512)} %compare_reduce_fusion, s32[128]{0:T(128)} %param.11), kind=kLoop, calls=%fused_computation.20 | loop fusion | flops 256 | bytes 1025 | tf_op jit(solution)/shard_map/reshape.29
  2.7 19.1 %all-gather.1 = f32[16,33,256]{2,1,0:T(8,128)S(1)} all-gather(f32[1,33,256]{2,1,0:T(8,128)S(1)} %fusion), channel_id=2, replica_groups=mesh['dp'=2,'ctx'=16] {'ctx'}, dimensions={0}, use_global_device_ids=true | all-gather | bytes 574464 | tf_op jit(solution)/shard_map/all_gather | solution.py:75
  21.8 1.8 %multiply_convert_fusion.refs_4_ = bf16[128,4096]{1,0:T(8,128)(2,1)S(1)} fusion(bf16[128,4096]{1,0:T(8,128)(2,1)} %param.9, bf16[128,4096]{1,0:T(8,128)(2,1)} %param.8), kind=kLoop, calls=%fused_computation | loop fusion | flops 2097152 | bytes 3145728 | tf_op jit(solution)/shard_map/convert_element_type | solution.py:79
  23.6 0.0 copy-start
  23.6 1.3 %collective-permute-start = (bf16[128,4096]{1,0:T(8,128)(2,1)S(1)}, bf16[128,4096]{1,0:T(8,128)(2,1)S(1)}, u32[]{:S(2)}, u32[]{:S(2)}) collective-permute-start(bf16[128,4096]{1,0:T(8,128)(2,1)S(1)} %multiply_convert_fusion.refs_4_), channel_id=1, source_target_pairs={{0,4},{1,5},{2,6},{3,7},{4,8},{5,9},{6,10},{7,11},{8,12},{9,13},{1... | collective-permute-start | bytes 3145736 | tf_op jit(solution)/shard_map/ppermute | solution.py:14
  24.9 2.6 %collective-permute-start.2 = (bf16[128,4096]{1,0:T(8,128)(2,1)S(1)}, bf16[128,4096]{1,0:T(8,128)(2,1)}, u32[]{:S(2)}, u32[]{:S(2)}) collective-permute-start(bf16[128,4096]{1,0:T(8,128)(2,1)S(1)} %multiply_convert_fusion.refs_4_), channel_id=1, source_target_pairs={{0,2},{1,3},{2,4},{3,5},{4,6},{5,7},{6,8},{7,9},{8,10},{9,11},{10,... | collective-permute-start | bytes 3145736 | tf_op jit(solution)/shard_map/ppermute | solution.py:14
  27.5 22.6 %collective-permute-done.refs_0_ = bf16[128,4096]{1,0:T(8,128)(2,1)S(1)} collective-permute-done((bf16[128,4096]{1,0:T(8,128)(2,1)S(1)}, bf16[128,4096]{1,0:T(8,128)(2,1)S(1)}, u32[]{:S(2)}, u32[]{:S(2)}) %collective-permute-start) | collective-permute-done | bytes 1048608 | tf_op jit(solution)/shard_map/ppermute | solution.py:14
  50.1 1.2 broadcast_select_fusion
  51.3 0.1 copy-done.1
  51.4 1.0 collective-permute-start.1
  52.4 20.5 %collective-permute-done.2.refs_2_ = bf16[128,4096]{1,0:T(8,128)(2,1)} collective-permute-done((bf16[128,4096]{1,0:T(8,128)(2,1)S(1)}, bf16[128,4096]{1,0:T(8,128)(2,1)}, u32[]{:S(2)}, u32[]{:S(2)}) %collective-permute-start.2) | collective-permute-done | bytes 1048608 | tf_op jit(solution)/shard_map/ppermute | solution.py:14
  72.8 1.2 collective-permute-start.3
  74.1 0.0 copy-start.3
  74.1 0.2 copy.8
  74.3 0.8 rev.3
  75.1 0.1 pad.7.clone
  75.3 0.8 compare_convert_fusion.refs_6_
  76.1 1.2 maximum_maximum_fusion.refs_5_
  77.2 0.0 collective-permute-done.1.refs_1_
  77.2 0.0 collective-permute-done.3.refs_3_
  77.2 1.0 copy-done.2
  78.2 42.9 %shard_map.55 = bf16[128,4096]{1,0:T(8,128)(2,1)} custom-call(s32[1]{0:T(128)} %bitcast.core_ref, bf16[128,4096]{1,0:T(8,128)(2,1)} %copy-done.1, bf16[128,4096]{1,0:T(8,128)(2,1)} %collective-permute-done.1.refs_1_, bf16[128,4096]{1,0:T(8,128)(2,1)} %collective-permute-done.2.refs_2_, bf16[128,4096]{1,0:T(8,128)(2,1)} %copy-done.2, ...), custom_call_target="tpu_custom_call" | custom-call | tf_op jit(solution)/shard_map/pallas_call | solution.py:103
  (16 shorter events, 0.1 us)
Async XLA Ops:
  23.6 27.7 %copy-start = (bf16[128,4096]{1,0:T(8,128)(2,1)}, bf16[128,4096]{1,0:T(8,128)(2,1)S(1)}, u32[]{:S(2)}) copy-start(bf16[128,4096]{1,0:T(8,128)(2,1)S(1)} %multiply_convert_fusion.refs_4_) | copy-start | bytes 3145732
  23.6 26.5 %collective-permute-start = (bf16[128,4096]{1,0:T(8,128)(2,1)S(1)}, bf16[128,4096]{1,0:T(8,128)(2,1)S(1)}, u32[]{:S(2)}, u32[]{:S(2)}) collective-permute-start(bf16[128,4096]{1,0:T(8,128)(2,1)S(1)} %multiply_convert_fusion.refs_4_), channel_id=1, source_target_pairs={{0,4},{1,5},{2,6},{3,7},{4,8},{5,9},{6,10},{7,11},{8,12},{9,13},{1... | collective-permute-start | bytes 3145736 | tf_op jit(solution)/shard_map/ppermute | solution.py:14
  24.9 48.0 %collective-permute-start.2 = (bf16[128,4096]{1,0:T(8,128)(2,1)S(1)}, bf16[128,4096]{1,0:T(8,128)(2,1)}, u32[]{:S(2)}, u32[]{:S(2)}) collective-permute-start(bf16[128,4096]{1,0:T(8,128)(2,1)S(1)} %multiply_convert_fusion.refs_4_), channel_id=1, source_target_pairs={{0,2},{1,3},{2,4},{3,5},{4,6},{5,7},{6,8},{7,9},{8,10},{9,11},{10,... | collective-permute-start | bytes 3145736 | tf_op jit(solution)/shard_map/ppermute | solution.py:14
  50.1 1.3 %copy-start.1 = (bf16[128,4096]{1,0:T(8,128)(2,1)}, bf16[128,4096]{1,0:T(8,128)(2,1)S(1)}, u32[]{:S(2)}) copy-start(bf16[128,4096]{1,0:T(8,128)(2,1)S(1)} %collective-permute-done.refs_0_) | copy-start | bytes 3145732
  51.4 25.8 %collective-permute-start.1 = (bf16[128,4096]{1,0:T(8,128)(2,1)}, bf16[128,4096]{1,0:T(8,128)(2,1)}, u32[]{:S(2)}, u32[]{:S(2)}) collective-permute-start(bf16[128,4096]{1,0:T(8,128)(2,1)} %broadcast_select_fusion), channel_id=1, source_target_pairs={{0,1},{1,0},{2,3},{3,2},{4,5},{5,4},{6,7},{7,6},{8,9},{9,8},{10,11... | collective-permute-start | bytes 3145736 | tf_op jit(solution)/shard_map/ppermute | solution.py:19
  72.8 4.4 %collective-permute-start.3 = (bf16[128,4096]{1,0:T(8,128)(2,1)}, bf16[128,4096]{1,0:T(8,128)(2,1)S(1)}, u32[]{:S(2)}, u32[]{:S(2)}) collective-permute-start(bf16[128,4096]{1,0:T(8,128)(2,1)} %collective-permute-done.2.refs_2_), channel_id=1, source_target_pairs={{0,1},{1,0},{2,3},{3,2},{4,5},{5,4},{6,7},{7,6},{8,9},{9,8},{10,11... | collective-permute-start | bytes 3145736 | tf_op jit(solution)/shard_map/ppermute | solution.py:19
  74.1 1.2 copy-start.3
  77.2 1.0 copy-start.2

commit v4 on v3

--- a/solution.py
+++ b/solution.py
@@ -22,41 +22,43 @@
 def conv_kernel(core_ref, *refs, lags, rows, group_size):
     g_refs = list(refs[:lags + 1])
     p_ref, m_ref, q_ref, o_ref, lhs_ref, rhs_ref = refs[lags + 1:]
-    lane_chunk = q_ref.shape[1]
+    lane_chunk = rhs_ref.shape[1]
     per_chunk = lane_chunk // group_size
     row = lax.broadcasted_iota(jnp.int32, (rows, rows), 0)
     upper = lax.broadcasted_iota(jnp.int32, (rows, rows), 1) >= row
     owner = lax.broadcasted_iota(jnp.int32, (rows, lane_chunk), 1) // group_size
-    for k in range(per_chunk):
-        tap_row = p_ref[k : k + 1, :]
-        rolled = [
-            pltpu.roll(
-                jnp.broadcast_to(tap_row[:, rows * m : rows * (m + 1)], (rows, rows)),
-                0,
-                1,
-                stride=1,
-                stride_axis=0,
-            )
-            for m in range(lags + 2)
-        ]
+    even = core_ref[0] == 0
+    for u in range(q_ref.shape[1] // lane_chunk):
+        lanes = slice(lane_chunk * u, lane_chunk * (u + 1))
+        for k in range(per_chunk):
+            tap_row = p_ref[u * per_chunk + k : u * per_chunk + k + 1, :]
+            rolled = [
+                pltpu.roll(
+                    jnp.broadcast_to(tap_row[:, rows * m : rows * (m + 1)], (rows, rows)),
+                    0,
+                    1,
+                    stride=1,
+                    stride_axis=0,
+                )
+                for m in range(lags + 2)
+            ]
+            for n in range(lags + 1):
+                tile = jnp.where(upper, rolled[n + 1], rolled[n]) * m_ref[:, rows * n : rows * (n + 1)]
+                lhs_ref[n, :, rows * k : rows * (k + 1)] = tile.astype(jnp.bfloat16)
+        blocks = [g[:, lanes] for g in g_refs]
+        near, far = blocks[lags - 1], blocks[lags - 3]
+        blocks[lags - 1] = jnp.where(even, near, far)
+        blocks[lags - 3] = jnp.where(even, far, near)
+        acc = jnp.zeros((rows, lane_chunk), jnp.float32)
         for n in range(lags + 1):
-            tile = jnp.where(upper, rolled[n + 1], rolled[n]) * m_ref[:, rows * n : rows * (n + 1)]
-            lhs_ref[n, :, rows * k : rows * (k + 1)] = tile.astype(jnp.bfloat16)
-    even = core_ref[0] == 0
-    near, far = g_refs[lags - 1][...], g_refs[lags - 3][...]
-    blocks = [g[...] for g in g_refs]
-    blocks[lags - 1] = jnp.where(even, near, far)
-    blocks[lags - 3] = jnp.where(even, far, near)
-    acc = jnp.zeros((rows, lane_chunk), jnp.float32)
-    for n in range(lags + 1):
-        source = blocks[n]
-        for k in range(per_chunk):
-            rhs_ref[rows * k : rows * (k + 1), :] = jnp.where(owner == k, source, jnp.zeros_like(source))
-        term = jnp.dot(lhs_ref[n], rhs_ref[...], preferred_element_type=jnp.float32)
-        if n < lags:
-            term = term.astype(jnp.bfloat16).astype(jnp.float32)
-        acc = acc + term
-    o_ref[...] = (q_ref[...].astype(jnp.float32) * acc).astype(o_ref.dtype)
+            source = blocks[n]
+            for k in range(per_chunk):
+                rhs_ref[rows * k : rows * (k + 1), :] = jnp.where(owner == k, source, jnp.zeros_like(source))
+            term = jnp.dot(lhs_ref[n], rhs_ref[...], preferred_element_type=jnp.float32)
+            if n < lags:
+                term = term.astype(jnp.bfloat16).astype(jnp.float32)
+            acc = acc + term
+        o_ref[:, lanes] = (q_ref[:, lanes].astype(jnp.float32) * acc).astype(o_ref.dtype)
 
 
 def shards(queries, keys, values, taps, segment_ids):
@@ -70,11 +72,11 @@
     tap_rows = taps.shape[0]
     filt_len = tap_rows * ctx_count
     lags = filt_len // rows
-    seg_row = jnp.zeros((1, filters), jnp.float32).at[0, :rows].set(segment_ids.astype(jnp.float32))
-    packed = jnp.concatenate([taps.astype(jnp.float32), seg_row], axis=0)
+    seg_row = jnp.zeros((1, filters), jnp.bfloat16).at[0, :rows].set(segment_ids.astype(jnp.bfloat16))
+    packed = jnp.concatenate([taps, seg_row], axis=0)
     packed = lax.all_gather(packed, "ctx", axis=0, tiled=False)
     packed, keys, values = lax.optimization_barrier((packed, keys, values))
-    all_taps = packed[:, :tap_rows].reshape(filt_len, filters)
+    all_taps = packed[:, :tap_rows].reshape(filt_len, filters).astype(jnp.float32)
     all_segs = packed[:, tap_rows, :rows].astype(jnp.int32)
     gated = (keys.astype(jnp.float32) * values.astype(jnp.float32)).astype(jnp.bfloat16)
     padded = jnp.concatenate(
@@ -97,17 +99,18 @@
     sources = [four_back, swap_b, two_back, swap_a, gated]
     lane_chunk = 128
     per_chunk = lane_chunk // group_size
+    step_lanes = lane_chunk * 4 if channels % (lane_chunk * 4) == 0 else lane_chunk
     span = (lags + 1) * rows
     kernel = functools.partial(conv_kernel, lags=lags, rows=rows, group_size=group_size)
-    block = pl.BlockSpec((rows, lane_chunk), lambda j, c: (0, j))
+    block = pl.BlockSpec((rows, step_lanes), lambda j, c: (0, j))
     return pl.pallas_call(
         kernel,
         grid_spec=pltpu.PrefetchScalarGridSpec(
             num_scalar_prefetch=1,
-            grid=(channels // lane_chunk,),
+            grid=(channels // step_lanes,),
             in_specs=[block] * (lags + 1)
             + [
-                pl.BlockSpec((per_chunk, (lags + 2) * rows), lambda j, c: (j, 0)),
+                pl.BlockSpec((step_lanes // group_size, (lags + 2) * rows), lambda j, c: (j, 0)),
                 pl.BlockSpec((rows, span), lambda j, c: (0, 0)),
                 block,
             ],

time: 121 us -> 112 us (0.926)
  Pallas kernels: 42.9 us -> 34.3 us
    pallas_call x1, Pallas kernels: 42.9 us -> 34.3 us  [shards(): pl.pallas_call(kernel, grid_spec=pltpu.PrefetchScalarGridSpec(num_scalar_...]
where the time goes in v4:
time: 112 us; the launch traced here: 111 us
  waiting for transfers between devices  43 us (38%)
  Pallas kernels  34.3 us (31%)
  blocking collectives  18.2 us (16%)
  other arithmetic  7.67 us (7%)
  starting transfers between devices  5.97 us (5%)
  local copies, waits for them, and re-layouts  2.23 us (2%)
    ppermute x2, waiting for transfers between devices, shifted(): lax.ppermute(value, axis, [(source, source + steps) for source in range(f...  43 us
    pallas_call x1, Pallas kernels, shards(): pl.pallas_call(kernel, grid_spec=pltpu.PrefetchScalarGridSpec(num_scalar_...  34.3 us
    all_gather x1, blocking collectives, shards(): packed = lax.all_gather(packed, 'ctx', axis=0, tiled=False)  18.2 us
    ppermute x2, starting transfers between devices, shifted(): lax.ppermute(value, axis, [(source, source + steps) for source in range(f...  3.84 us
  transfers between devices with their start and end apart: 4, of which 2 were waited for; matrix products, arithmetic and copies ran while one was open for 4% of the time, Pallas kernels for 0%

profile of v4, /device:TPU:25, one launch (start us, length us, event | category | flops | bytes accessed | tf_op | source)
XLA Modules:
  0.0 111.5 jit_solution(8625614804037929507)
XLA Ops:
  0.0 0.6 compare_reduce_fusion
  0.6 1.3 %fusion.3 = bf16[1,128]{1,0:T(2,128)(2,1)S(1)} fusion(pred[]{:T(512)} %compare_reduce_fusion, s32[128]{0:T(128)} %param.11), kind=kLoop, calls=%fused_computation.22 | loop fusion | flops 256 | bytes 769 | tf_op jit(solution)/shard_map/reshape.29
  1.9 0.7 fusion.2
  2.7 18.2 %all-gather.1 = bf16[16,33,256]{2,1,0:T(8,128)(2,1)S(1)} all-gather(bf16[1,33,256]{2,1,0:T(8,128)(2,1)S(1)} %fusion.2), channel_id=2, replica_groups=mesh['dp'=2,'ctx'=16] {'ctx'}, dimensions={0}, use_global_device_ids=true | all-gather | bytes 287232 | tf_op jit(solution)/shard_map/all_gather | solution.py:77
  20.9 1.8 %multiply_convert_fusion.refs_4_ = bf16[128,4096]{1,0:T(8,128)(2,1)S(1)} fusion(bf16[128,4096]{1,0:T(8,128)(2,1)} %param.9, bf16[128,4096]{1,0:T(8,128)(2,1)} %param.8), kind=kLoop, calls=%fused_computation | loop fusion | flops 2097152 | bytes 3145728 | tf_op jit(solution)/shard_map/convert_element_type | solution.py:81
  22.7 1.3 %collective-permute-start = (bf16[128,4096]{1,0:T(8,128)(2,1)S(1)}, bf16[128,4096]{1,0:T(8,128)(2,1)S(1)}, u32[]{:S(2)}, u32[]{:S(2)}) collective-permute-start(bf16[128,4096]{1,0:T(8,128)(2,1)S(1)} %multiply_convert_fusion.refs_4_), channel_id=1, source_target_pairs={{0,4},{1,5},{2,6},{3,7},{4,8},{5,9},{6,10},{7,11},{8,12},{9,13},{1... | collective-permute-start | bytes 3145736 | tf_op jit(solution)/shard_map/ppermute | solution.py:14
  24.0 2.5 %collective-permute-start.2 = (bf16[128,4096]{1,0:T(8,128)(2,1)S(1)}, bf16[128,4096]{1,0:T(8,128)(2,1)}, u32[]{:S(2)}, u32[]{:S(2)}) collective-permute-start(bf16[128,4096]{1,0:T(8,128)(2,1)S(1)} %multiply_convert_fusion.refs_4_), channel_id=1, source_target_pairs={{0,2},{1,3},{2,4},{3,5},{4,6},{5,7},{6,8},{7,9},{8,10},{9,11},{10,... | collective-permute-start | bytes 3145736 | tf_op jit(solution)/shard_map/ppermute | solution.py:14
  26.5 0.1 bitcast_convert_fusion
  26.6 22.5 %collective-permute-done.refs_0_ = bf16[128,4096]{1,0:T(8,128)(2,1)S(1)} collective-permute-done((bf16[128,4096]{1,0:T(8,128)(2,1)S(1)}, bf16[128,4096]{1,0:T(8,128)(2,1)S(1)}, u32[]{:S(2)}, u32[]{:S(2)}) %collective-permute-start) | collective-permute-done | bytes 1048608 | tf_op jit(solution)/shard_map/ppermute | solution.py:14
  49.2 1.2 %broadcast_select_fusion = bf16[128,4096]{1,0:T(8,128)(2,1)} fusion(bf16[128,4096]{1,0:T(8,128)(2,1)S(1)} %collective-permute-done.refs_0_, bf16[128,4096]{1,0:T(8,128)(2,1)S(1)} %multiply_convert_fusion.refs_4_, pred[]{:T(512)S(6)} %eq.18), kind=kLoop, calls=%fused_computation.1 | loop fusion | flops 524288 | bytes 3145729 | tf_op jit(solution)/shard_map/jit(_where)/select_n | solution.py:98
  50.4 0.1 copy-done.1
  50.5 1.0 collective-permute-start.1
  51.5 20.4 %collective-permute-done.2.refs_2_ = bf16[128,4096]{1,0:T(8,128)(2,1)} collective-permute-done((bf16[128,4096]{1,0:T(8,128)(2,1)S(1)}, bf16[128,4096]{1,0:T(8,128)(2,1)}, u32[]{:S(2)}, u32[]{:S(2)}) %collective-permute-start.2) | collective-permute-done | bytes 1048608 | tf_op jit(solution)/shard_map/ppermute | solution.py:14
  71.9 1.2 %collective-permute-start.3 = (bf16[128,4096]{1,0:T(8,128)(2,1)}, bf16[128,4096]{1,0:T(8,128)(2,1)S(1)}, u32[]{:S(2)}, u32[]{:S(2)}) collective-permute-start(bf16[128,4096]{1,0:T(8,128)(2,1)} %collective-permute-done.2.refs_2_), channel_id=1, source_target_pairs={{0,1},{1,0},{2,3},{3,2},{4,5},{5,4},{6,7},{7,6},{8,9},{9,8},{10,11... | collective-permute-start | bytes 3145736 | tf_op jit(solution)/shard_map/ppermute | solution.py:19
  73.1 0.0 copy-start.3
  73.1 0.2 copy.8
  73.3 0.8 rev.3
  74.1 0.1 pad.7.clone
  74.3 0.8 compare_convert_fusion.refs_6_
  75.1 1.2 %maximum_maximum_fusion.refs_5_ = f32[256,768]{1,0:T(8,128)} fusion(f32[256,512]{1,0:T(8,128)S(1)} %rev.3, f32[768]{0:T(1024)S(1)} %pad.7.clone, f32[768]{0:T(1024)S(1)} %pad.5.clone), kind=kLoop, calls=%fused_computation.2 | loop fusion | flops 393216 | bytes 1316864 | tf_op jit(solution)/shard_map/concatenate | solution.py:82
  76.2 0.0 collective-permute-done.1.refs_1_
  76.2 0.0 collective-permute-done.3.refs_3_
  76.2 1.0 copy-done.2
  77.2 34.3 %shard_map.55 = bf16[128,4096]{1,0:T(8,128)(2,1)} custom-call(s32[1]{0:T(128)} %bitcast.core_ref, bf16[128,4096]{1,0:T(8,128)(2,1)} %copy-done.1, bf16[128,4096]{1,0:T(8,128)(2,1)} %collective-permute-done.1.refs_1_, bf16[128,4096]{1,0:T(8,128)(2,1)} %collective-permute-done.2.refs_2_, bf16[128,4096]{1,0:T(8,128)(2,1)} %copy-done.2, ...), custom_call_target="tpu_custom_call" | custom-call | tf_op jit(solution)/shard_map/pallas_call | solution.py:106
  (16 shorter events, 0.1 us)
Async XLA Ops:
  22.7 27.7 %copy-start = (bf16[128,4096]{1,0:T(8,128)(2,1)}, bf16[128,4096]{1,0:T(8,128)(2,1)S(1)}, u32[]{:S(2)}) copy-start(bf16[128,4096]{1,0:T(8,128)(2,1)S(1)} %multiply_convert_fusion.refs_4_) | copy-start | bytes 3145732
  22.7 26.5 %collective-permute-start = (bf16[128,4096]{1,0:T(8,128)(2,1)S(1)}, bf16[128,4096]{1,0:T(8,128)(2,1)S(1)}, u32[]{:S(2)}, u32[]{:S(2)}) collective-permute-start(bf16[128,4096]{1,0:T(8,128)(2,1)S(1)} %multiply_convert_fusion.refs_4_), channel_id=1, source_target_pairs={{0,4},{1,5},{2,6},{3,7},{4,8},{5,9},{6,10},{7,11},{8,12},{9,13},{1... | collective-permute-start | bytes 3145736 | tf_op jit(solution)/shard_map/ppermute | solution.py:14
  24.0 47.9 %collective-permute-start.2 = (bf16[128,4096]{1,0:T(8,128)(2,1)S(1)}, bf16[128,4096]{1,0:T(8,128)(2,1)}, u32[]{:S(2)}, u32[]{:S(2)}) collective-permute-start(bf16[128,4096]{1,0:T(8,128)(2,1)S(1)} %multiply_convert_fusion.refs_4_), channel_id=1, source_target_pairs={{0,2},{1,3},{2,4},{3,5},{4,6},{5,7},{6,8},{7,9},{8,10},{9,11},{10,... | collective-permute-start | bytes 3145736 | tf_op jit(solution)/shard_map/ppermute | solution.py:14
  49.2 1.3 %copy-start.1 = (bf16[128,4096]{1,0:T(8,128)(2,1)}, bf16[128,4096]{1,0:T(8,128)(2,1)S(1)}, u32[]{:S(2)}) copy-start(bf16[128,4096]{1,0:T(8,128)(2,1)S(1)} %collective-permute-done.refs_0_) | copy-start | bytes 3145732
  50.5 25.7 %collective-permute-start.1 = (bf16[128,4096]{1,0:T(8,128)(2,1)}, bf16[128,4096]{1,0:T(8,128)(2,1)}, u32[]{:S(2)}, u32[]{:S(2)}) collective-permute-start(bf16[128,4096]{1,0:T(8,128)(2,1)} %broadcast_select_fusion), channel_id=1, source_target_pairs={{0,1},{1,0},{2,3},{3,2},{4,5},{5,4},{6,7},{7,6},{8,9},{9,8},{10,11... | collective-permute-start | bytes 3145736 | tf_op jit(solution)/shard_map/ppermute | solution.py:19
  71.9 4.3 %collective-permute-start.3 = (bf16[128,4096]{1,0:T(8,128)(2,1)}, bf16[128,4096]{1,0:T(8,128)(2,1)S(1)}, u32[]{:S(2)}, u32[]{:S(2)}) collective-permute-start(bf16[128,4096]{1,0:T(8,128)(2,1)} %collective-permute-done.2.refs_2_), channel_id=1, source_target_pairs={{0,1},{1,0},{2,3},{3,2},{4,5},{5,4},{6,7},{7,6},{8,9},{9,8},{10,11... | collective-permute-start | bytes 3145736 | tf_op jit(solution)/shard_map/ppermute | solution.py:19
  73.1 1.2 %copy-start.3 = (s32[128]{0:T(128)S(1)}, s32[128]{0:T(128)}, u32[]{:S(2)}) copy-start(s32[128]{0:T(128)} %param.11) | copy-start | bytes 1540
  76.2 1.0 copy-start.2

commit v5 on v4

--- a/solution.py
+++ b/solution.py
@@ -17,6 +17,20 @@
 def swapped(value, axis):
     count = lax.axis_size(axis)
     return lax.ppermute(value, axis, [(source, source ^ 1) for source in range(count)])
+
+
+def two_back_relayed(value, axis, own_index):
+    count = lax.axis_size(axis)
+    half = value.shape[0] // 2
+    relay = [s for s in range(count) if s % 4 >= 2 and s + 2 < count]
+    direct = [(s, s + 2) for s in range(count - 2) if s not in relay]
+    plain = lax.ppermute(value, axis, direct)
+    top = lax.ppermute(value[:half], axis, [(s, s + 4) for s in relay])
+    top = lax.ppermute(top, axis, [(s + 4, s + 2) for s in relay])
+    bottom = lax.ppermute(value[half:], axis, [(s, s - 2) for s in relay])
+    bottom = lax.ppermute(bottom, axis, [(s - 2, s + 2) for s in relay])
+    relayed = jnp.isin(own_index, jnp.array([s + 2 for s in relay] or [-1], jnp.int32))
+    return jnp.where(relayed, jnp.concatenate([top, bottom], axis=0), plain)
 
 
 def conv_kernel(core_ref, *refs, lags, rows, group_size):
@@ -92,7 +106,7 @@
         for lag in range(lags, -1, -1)
     ]
     mask = (segment_ids[:, None] == jnp.concatenate(seg_sources)[None, :]).astype(jnp.float32)
-    two_back = shifted(gated, "ctx", 2)
+    two_back = two_back_relayed(gated, "ctx", own_index)
     four_back = shifted(gated, "ctx", 4)
     swap_a = swapped(two_back, "ctx")
     swap_b = swapped(jnp.where(core == 1, four_back, gated), "ctx")

time: 112 us -> 114 us (1.018)
  starting transfers between devices: 5.97 us -> 13.7 us
  waiting for transfers between devices: 43 us -> 36 us
  other arithmetic: 7.67 us -> 9.34 us
    ppermute x2 -> x1, waiting for transfers between devices: 43 us -> 14.5 us  [shifted(): lax.ppermute(value, axis, [(source, source + steps) for source in range(f...]
    ppermute x0 -> x5, waiting for transfers between devices: none -> 21.5 us  [the longest x1 21.5 us: two_back_relayed(): top = lax.ppermute(top, axis, [(s + 4, s + 2) for s in relay])]
    ppermute x0 -> x5, starting transfers between devices: none -> 8.99 us  [the longest x1 3.36 us: two_back_relayed(): plain = lax.ppermute(value, axis, direct)]
    ppermute x2 -> x1, starting transfers between devices: 3.84 us -> 1.29 us  [shifted(): lax.ppermute(value, axis, [(source, source + steps) for source in range(f...]
    ppermute x2, starting transfers between devices: 2.14 us -> 3.4 us  [swapped(): lax.ppermute(value, axis, [(source, source ^ 1) for source in range(count)])]
  transfers between devices with their start and end apart: 4 -> 8, of which waited for: 2 -> 2; matrix products, arithmetic and copies ran while one was open for 4% -> 6% of each run, Pallas kernels for 0% -> 0%
where the time goes in v5:
time: 114 us
  waiting for transfers between devices  36 us (32%)
  Pallas kernels  34.3 us (30%)
  blocking collectives  18.2 us (16%)
  starting transfers between devices  13.7 us (12%)
  other arithmetic  9.34 us (8%)
  local copies, waits for them, and re-layouts  2.13 us (2%)
    pallas_call x1, Pallas kernels, shards(): pl.pallas_call(kernel, grid_spec=pltpu.PrefetchScalarGridSpec(num_scalar_...  34.3 us
    ppermute x1, waiting for transfers between devices, two_back_relayed(): top = lax.ppermute(top, axis, [(s + 4, s + 2) for s in relay])  21.5 us
    all_gather x1, blocking collectives, shards(): packed = lax.all_gather(packed, 'ctx', axis=0, tiled=False)  18.2 us
    ppermute x1, waiting for transfers between devices, shifted(): lax.ppermute(value, axis, [(source, source + steps) for source in range(f...  14.5 us
    ppermute x2, starting transfers between devices, swapped(): lax.ppermute(value, axis, [(source, source ^ 1) for source in range(count)])  3.4 us
    ppermute x1, starting transfers between devices, two_back_relayed(): plain = lax.ppermute(value, axis, direct)  3.36 us
  transfers between devices with their start and end apart: 8, of which 2 were waited for; matrix products, arithmetic and copies ran while one was open for 6% of the time, Pallas kernels for 0%

profile of v5, /device:TPU:25, one launch (start us, length us, event | category | flops | bytes accessed | tf_op | source)
XLA Modules:
  0.0 113.8 jit_solution(12869885693298798135)
XLA Ops:
  0.0 0.6 compare_reduce_fusion.1
  0.6 1.3 %fusion.3 = bf16[1,128]{1,0:T(2,128)(2,1)S(1)} fusion(pred[]{:T(512)} %compare_reduce_fusion.1, s32[128]{0:T(128)} %param.12), kind=kLoop, calls=%fused_computation.24 | loop fusion | flops 256 | bytes 769 | tf_op jit(solution)/shard_map/reshape.31
  1.9 0.7 fusion.2
  2.7 18.2 %all-gather.1 = bf16[16,33,256]{2,1,0:T(8,128)(2,1)S(1)} all-gather(bf16[1,33,256]{2,1,0:T(8,128)(2,1)S(1)} %fusion.2), channel_id=2, replica_groups=mesh['dp'=2,'ctx'=16] {'ctx'}, dimensions={0}, use_global_device_ids=true | all-gather | bytes 287232 | tf_op jit(solution)/shard_map/all_gather | solution.py:91
  20.9 1.8 %multiply_convert_fusion.refs_4_ = bf16[128,4096]{1,0:T(8,128)(2,1)S(1)} fusion(bf16[128,4096]{1,0:T(8,128)(2,1)} %param.10, bf16[128,4096]{1,0:T(8,128)(2,1)} %param.9), kind=kLoop, calls=%fused_computation | loop fusion | flops 2097152 | bytes 3145728 | tf_op jit(solution)/shard_map/convert_element_type | solution.py:95
  22.7 1.3 %collective-permute-start = (bf16[128,4096]{1,0:T(8,128)(2,1)S(1)}, bf16[128,4096]{1,0:T(8,128)(2,1)S(1)}, u32[]{:S(2)}, u32[]{:S(2)}) collective-permute-start(bf16[128,4096]{1,0:T(8,128)(2,1)S(1)} %multiply_convert_fusion.refs_4_), channel_id=1, source_target_pairs={{0,4},{1,5},{2,6},{3,7},{4,8},{5,9},{6,10},{7,11},{8,12},{9,13},{1... | collective-permute-start | bytes 3145736 | tf_op jit(solution)/shard_map/ppermute | solution.py:14
  24.0 0.9 fusion.9
  24.8 1.6 %collective-permute-start.2 = (bf16[64,4096]{1,0:T(8,128)(2,1)}, bf16[64,4096]{1,0:T(8,128)(2,1)}, u32[]{:S(2)}, u32[]{:S(2)}) collective-permute-start(bf16[64,4096]{1,0:T(8,128)(2,1)} %get-tuple-element.23), channel_id=1, source_target_pairs={{2,6},{3,7},{6,10},{7,11},{10,14},{11,15},{18,22},{19,23},{22,26},... | collective-permute-start | bytes 1572872 | tf_op jit(solution)/shard_map/ppermute | solution.py:28
  26.4 1.5 %collective-permute-start.4 = (bf16[64,4096]{1,0:T(8,128)(2,1)S(1)}, bf16[64,4096]{1,0:T(8,128)(2,1)}, u32[]{:S(2)}, u32[]{:S(2)}) collective-permute-start(bf16[64,4096]{1,0:T(8,128)(2,1)S(1)} %get-tuple-element.24), channel_id=1, source_target_pairs={{2,0},{3,1},{6,4},{7,5},{10,8},{11,9},{18,16},{19,17},{22,20},{23,... | collective-permute-start | bytes 1572872 | tf_op jit(solution)/shard_map/ppermute | solution.py:30
  27.9 3.4 %collective-permute-start.6 = (bf16[128,4096]{1,0:T(8,128)(2,1)S(1)}, bf16[128,4096]{1,0:T(8,128)(2,1)}, u32[]{:S(2)}, u32[]{:S(2)}) collective-permute-start(bf16[128,4096]{1,0:T(8,128)(2,1)S(1)} %multiply_convert_fusion.refs_4_), channel_id=1, source_target_pairs={{0,2},{1,3},{4,6},{5,7},{8,10},{9,11},{12,14},{13,15},{16,18},{17,... | collective-permute-start | bytes 3145736 | tf_op jit(solution)/shard_map/ppermute | solution.py:27
  31.4 0.7 compare_reduce_fusion
  32.1 1.3 %collective-permute-start.3 = (bf16[64,4096]{1,0:T(8,128)(2,1)}, bf16[64,4096]{1,0:T(8,128)(2,1)S(1)}, u32[]{:S(2)}, u32[]{:S(2)}) collective-permute-start(bf16[64,4096]{1,0:T(8,128)(2,1)} %collective-permute-done.2), channel_id=1, source_target_pairs={{6,4},{7,5},{10,8},{11,9},{14,12},{15,13},{22,20},{23,21},{26,24},... | collective-permute-start | bytes 1572872 | tf_op jit(solution)/shard_map/ppermute | solution.py:29
  33.4 1.3 %collective-permute-start.5 = (bf16[64,4096]{1,0:T(8,128)(2,1)}, bf16[64,4096]{1,0:T(8,128)(2,1)S(1)}, u32[]{:S(2)}, u32[]{:S(2)}) collective-permute-start(bf16[64,4096]{1,0:T(8,128)(2,1)} %collective-permute-done.4), channel_id=1, source_target_pairs={{0,4},{1,5},{4,8},{5,9},{8,12},{9,13},{16,20},{17,21},{20,24},{21,... | collective-permute-start | bytes 1572872 | tf_op jit(solution)/shard_map/ppermute | solution.py:31
  34.7 14.5 %collective-permute-done.refs_0_ = bf16[128,4096]{1,0:T(8,128)(2,1)S(1)} collective-permute-done((bf16[128,4096]{1,0:T(8,128)(2,1)S(1)}, bf16[128,4096]{1,0:T(8,128)(2,1)S(1)}, u32[]{:S(2)}, u32[]{:S(2)}) %collective-permute-start) | collective-permute-done | bytes 1048608 | tf_op jit(solution)/shard_map/ppermute | solution.py:14
  49.2 1.2 %broadcast_select_fusion = bf16[128,4096]{1,0:T(8,128)(2,1)} fusion(bf16[128,4096]{1,0:T(8,128)(2,1)S(1)} %collective-permute-done.refs_0_, bf16[128,4096]{1,0:T(8,128)(2,1)S(1)} %multiply_convert_fusion.refs_4_, pred[]{:T(512)S(6)} %eq.31), kind=kLoop, calls=%fused_computation.2 | loop fusion | flops 524288 | bytes 3145729 | tf_op jit(solution)/shard_map/jit(_where)/select_n | solution.py:112
  50.5 1.5 %collective-permute-start.1 = (bf16[128,4096]{1,0:T(8,128)(2,1)}, bf16[128,4096]{1,0:T(8,128)(2,1)}, u32[]{:S(2)}, u32[]{:S(2)}) collective-permute-start(bf16[128,4096]{1,0:T(8,128)(2,1)} %broadcast_select_fusion), channel_id=1, source_target_pairs={{0,1},{1,0},{2,3},{3,2},{4,5},{5,4},{6,7},{7,6},{8,9},{9,8},{10,11... | collective-permute-start | bytes 3145736 | tf_op jit(solution)/shard_map/ppermute | solution.py:19
  52.0 21.5 %collective-permute-done.3 = bf16[64,4096]{1,0:T(8,128)(2,1)S(1)} collective-permute-done((bf16[64,4096]{1,0:T(8,128)(2,1)}, bf16[64,4096]{1,0:T(8,128)(2,1)S(1)}, u32[]{:S(2)}, u32[]{:S(2)}) %collective-permute-start.3) | collective-permute-done | bytes 524320 | tf_op jit(solution)/shard_map/ppermute | solution.py:29
  73.5 1.0 maximum_select_fusion.refs_2_
  74.5 1.9 %collective-permute-start.7 = (bf16[128,4096]{1,0:T(8,128)(2,1)S(1)}, bf16[128,4096]{1,0:T(8,128)(2,1)}, u32[]{:S(2)}, u32[]{:S(2)}) collective-permute-start(bf16[128,4096]{1,0:T(8,128)(2,1)S(1)} %maximum_select_fusion.refs_2_), channel_id=1, source_target_pairs={{0,1},{1,0},{2,3},{3,2},{4,5},{5,4},{6,7},{7,6},{8,9},{9,8},{10,11... | collective-permute-start | bytes 3145736 | tf_op jit(solution)/shard_map/ppermute | solution.py:19
  76.4 0.2 copy.9
  76.6 0.8 rev.3
  77.6 0.8 compare_convert_fusion.refs_6_
  78.4 1.2 %maximum_maximum_fusion.refs_5_ = f32[256,768]{1,0:T(8,128)} fusion(f32[256,512]{1,0:T(8,128)S(1)} %rev.3, f32[768]{0:T(1024)S(1)} %pad.7.clone, f32[768]{0:T(1024)S(1)} %pad.5.clone), kind=kLoop, calls=%fused_computation.3 | loop fusion | flops 393216 | bytes 1316864 | tf_op jit(solution)/shard_map/concatenate | solution.py:96
  79.5 34.3 %shard_map.64 = bf16[128,4096]{1,0:T(8,128)(2,1)} custom-call(s32[1]{0:T(128)} %bitcast.core_ref, bf16[128,4096]{1,0:T(8,128)(2,1)} %copy-done.1, bf16[128,4096]{1,0:T(8,128)(2,1)} %collective-permute-done.1.refs_1_, bf16[128,4096]{1,0:T(8,128)(2,1)} %copy-done.2, bf16[128,4096]{1,0:T(8,128)(2,1)} %collective-permute-done.7.refs_3_, ...), custom_call_target="tpu_custom_call" | custom-call | tf_op jit(solution)/shard_map/pallas_call | solution.py:120
  (29 shorter events, 0.4 us)
Async XLA Ops:
  22.7 26.5 %copy-start = (bf16[128,4096]{1,0:T(8,128)(2,1)}, bf16[128,4096]{1,0:T(8,128)(2,1)S(1)}, u32[]{:S(2)}) copy-start(bf16[128,4096]{1,0:T(8,128)(2,1)S(1)} %multiply_convert_fusion.refs_4_) | copy-start | bytes 3145732
  22.7 26.5 %collective-permute-start = (bf16[128,4096]{1,0:T(8,128)(2,1)S(1)}, bf16[128,4096]{1,0:T(8,128)(2,1)S(1)}, u32[]{:S(2)}, u32[]{:S(2)}) collective-permute-start(bf16[128,4096]{1,0:T(8,128)(2,1)S(1)} %multiply_convert_fusion.refs_4_), channel_id=1, source_target_pairs={{0,4},{1,5},{2,6},{3,7},{4,8},{5,9},{6,10},{7,11},{8,12},{9,13},{1... | collective-permute-start | bytes 3145736 | tf_op jit(solution)/shard_map/ppermute | solution.py:14
  24.8 6.5 %copy-start.4 = (s32[6]{0:T(128)S(1)}, s32[6]{0:T(128)}, u32[]{:S(2)}) copy-start(s32[6]{0:T(128)} %constant.89.clone) | copy-start | bytes 76
  24.8 7.2 %collective-permute-start.2 = (bf16[64,4096]{1,0:T(8,128)(2,1)}, bf16[64,4096]{1,0:T(8,128)(2,1)}, u32[]{:S(2)}, u32[]{:S(2)}) collective-permute-start(bf16[64,4096]{1,0:T(8,128)(2,1)} %get-tuple-element.23), channel_id=1, source_target_pairs={{2,6},{3,7},{6,10},{7,11},{10,14},{11,15},{18,22},{19,23},{22,26},... | collective-permute-start | bytes 1572872 | tf_op jit(solution)/shard_map/ppermute | solution.py:28
  26.4 6.9 %collective-permute-start.4 = (bf16[64,4096]{1,0:T(8,128)(2,1)S(1)}, bf16[64,4096]{1,0:T(8,128)(2,1)}, u32[]{:S(2)}, u32[]{:S(2)}) collective-permute-start(bf16[64,4096]{1,0:T(8,128)(2,1)S(1)} %get-tuple-element.24), channel_id=1, source_target_pairs={{2,0},{3,1},{6,4},{7,5},{10,8},{11,9},{18,16},{19,17},{22,20},{23,... | collective-permute-start | bytes 1572872 | tf_op jit(solution)/shard_map/ppermute | solution.py:30
  27.9 45.6 %collective-permute-start.6 = (bf16[128,4096]{1,0:T(8,128)(2,1)S(1)}, bf16[128,4096]{1,0:T(8,128)(2,1)}, u32[]{:S(2)}, u32[]{:S(2)}) collective-permute-start(bf16[128,4096]{1,0:T(8,128)(2,1)S(1)} %multiply_convert_fusion.refs_4_), channel_id=1, source_target_pairs={{0,2},{1,3},{4,6},{5,7},{8,10},{9,11},{12,14},{13,15},{16,18},{17,... | collective-permute-start | bytes 3145736 | tf_op jit(solution)/shard_map/ppermute | solution.py:27
  32.1 41.4 %collective-permute-start.3 = (bf16[64,4096]{1,0:T(8,128)(2,1)}, bf16[64,4096]{1,0:T(8,128)(2,1)S(1)}, u32[]{:S(2)}, u32[]{:S(2)}) collective-permute-start(bf16[64,4096]{1,0:T(8,128)(2,1)} %collective-permute-done.2), channel_id=1, source_target_pairs={{6,4},{7,5},{10,8},{11,9},{14,12},{15,13},{22,20},{23,21},{26,24},... | collective-permute-start | bytes 1572872 | tf_op jit(solution)/shard_map/ppermute | solution.py:29
  33.4 40.1 %collective-permute-start.5 = (bf16[64,4096]{1,0:T(8,128)(2,1)}, bf16[64,4096]{1,0:T(8,128)(2,1)S(1)}, u32[]{:S(2)}, u32[]{:S(2)}) collective-permute-start(bf16[64,4096]{1,0:T(8,128)(2,1)} %collective-permute-done.4), channel_id=1, source_target_pairs={{0,4},{1,5},{4,8},{5,9},{8,12},{9,13},{16,20},{17,21},{20,24},{21,... | collective-permute-start | bytes 1572872 | tf_op jit(solution)/shard_map/ppermute | solution.py:31
  49.2 1.3 %copy-start.1 = (bf16[128,4096]{1,0:T(8,128)(2,1)}, bf16[128,4096]{1,0:T(8,128)(2,1)S(1)}, u32[]{:S(2)}) copy-start(bf16[128,4096]{1,0:T(8,128)(2,1)S(1)} %collective-permute-done.refs_0_) | copy-start | bytes 3145732
  50.5 29.0 %collective-permute-start.1 = (bf16[128,4096]{1,0:T(8,128)(2,1)}, bf16[128,4096]{1,0:T(8,128)(2,1)}, u32[]{:S(2)}, u32[]{:S(2)}) collective-permute-start(bf16[128,4096]{1,0:T(8,128)(2,1)} %broadcast_select_fusion), channel_id=1, source_target_pairs={{0,1},{1,0},{2,3},{3,2},{4,5},{5,4},{6,7},{7,6},{8,9},{9,8},{10,11... | collective-permute-start | bytes 3145736 | tf_op jit(solution)/shard_map/ppermute | solution.py:19
  74.5 2.9 %copy-start.2 = (bf16[128,4096]{1,0:T(8,128)(2,1)}, bf16[128,4096]{1,0:T(8,128)(2,1)S(1)}, u32[]{:S(2)}) copy-start(bf16[128,4096]{1,0:T(8,128)(2,1)S(1)} %maximum_select_fusion.refs_2_) | copy-start | bytes 3145732
  74.5 5.0 %collective-permute-start.7 = (bf16[128,4096]{1,0:T(8,128)(2,1)S(1)}, bf16[128,4096]{1,0:T(8,128)(2,1)}, u32[]{:S(2)}, u32[]{:S(2)}) collective-permute-start(bf16[128,4096]{1,0:T(8,128)(2,1)S(1)} %maximum_select_fusion.refs_2_), channel_id=1, source_target_pairs={{0,1},{1,0},{2,3},{3,2},{4,5},{5,4},{6,7},{7,6},{8,9},{9,8},{10,11... | collective-permute-start | bytes 3145736 | tf_op jit(solution)/shard_map/ppermute | solution.py:19
  76.4 1.2 %copy-start.3 = (s32[128]{0:T(128)S(1)}, s32[128]{0:T(128)}, u32[]{:S(2)}) copy-start(s32[128]{0:T(128)} %param.12) | copy-start | bytes 1540

commit v6 on v4

v6 whole, which is shorter than its diff:
```python
import functools

import jax
import jax.numpy as jnp
from jax import lax
from jax.experimental import pallas as pl
from jax.experimental.pallas import tpu as pltpu
from jax.sharding import PartitionSpec as P


def shifted(value, axis, steps):
    count = lax.axis_size(axis)
    first, last = (max(0, -steps), min(count, count - steps))
    return lax.ppermute(value, axis, [(source, source + steps) for source in range(first, last)])


def swapped(value, axis):
    count = lax.axis_size(axis)
    return lax.ppermute(value, axis, [(source, source ^ 1) for source in range(count)])


def conv_kernel(*refs, count, rows, group_size, rounded, first, final):
    g_refs = refs[:count]
    w_refs = refs[count : 2 * count]
    rest = list(refs[2 * count :])
    m_ref = rest.pop(0)
    acc_ref = None if first else rest.pop(0)
    q_ref = rest.pop(0) if final else None
    o_ref, lhs_ref, rhs_ref = rest
    lane_chunk = rhs_ref.shape[1]
    per_chunk = lane_chunk // group_size
    row = lax.broadcasted_iota(jnp.int32, (rows, rows), 0)
    upper = lax.broadcasted_iota(jnp.int32, (rows, rows), 1) >= row
    owner = lax.broadcasted_iota(jnp.int32, (rows, lane_chunk), 1) // group_size
    for u in range(o_ref.shape[1] // lane_chunk):
        lanes = slice(lane_chunk * u, lane_chunk * (u + 1))
        for n in range(count):
            for k in range(per_chunk):
                window = w_refs[n][u * per_chunk + k : u * per_chunk + k + 1, :]
                lo, hi = [
                    pltpu.roll(
                        jnp.broadcast_to(window[:, rows * m : rows * (m + 1)], (rows, rows)),
                        0,
                        1,
                        stride=1,
                        stride_axis=0,
                    )
                    for m in range(2)
                ]
                tile = jnp.where(upper, hi, lo) * m_ref[:, rows * n : rows * (n + 1)]
                lhs_ref[n, :, rows * k : rows * (k + 1)] = tile.astype(jnp.bfloat16)
        acc = jnp.zeros((rows, lane_chunk), jnp.float32) if first else acc_ref[:, lanes]
        for n in range(count):
            source = g_refs[n][:, lanes]
            for k in range(per_chunk):
                rhs_ref[rows * k : rows * (k + 1), :] = jnp.where(owner == k, source, jnp.zeros_like(source))
            term = jnp.dot(lhs_ref[n], rhs_ref[...], preferred_element_type=jnp.float32)
            if rounded[n]:
                term = term.astype(jnp.bfloat16).astype(jnp.float32)
            acc = acc + term
        if final:
            o_ref[:, lanes] = (q_ref[:, lanes].astype(jnp.float32) * acc).astype(o_ref.dtype)
        else:
            o_ref[:, lanes] = acc


def conv_terms(sources, windows, mask, rounded, acc, queries, group_size):
    rows, channels = sources[0].shape
    count = len(sources)
    first = acc is None
    final = queries is not None
    lane_chunk = 128
    step_lanes = lane_chunk * 4 if channels % (lane_chunk * 4) == 0 else lane_chunk
    block = pl.BlockSpec((rows, step_lanes), lambda j: (0, j))
    window_spec = pl.BlockSpec((step_lanes // group_size, 2 * rows), lambda j: (j, 0))
    in_specs = [block] * count + [window_spec] * count + [pl.BlockSpec((rows, count * rows), lambda j: (0, 0))]
    operands = list(sources) + list(windows) + [mask]
    if not first:
        in_specs.append(block)
        operands.append(acc)
    if final:
        in_specs.append(block)
        operands.append(queries)
    kernel = functools.partial(
        conv_kernel, count=count, rows=rows, group_size=group_size, rounded=tuple(rounded), first=first, final=final
    )
    return pl.pallas_call(
        kernel,
        grid=(channels // step_lanes,),
        in_specs=in_specs,
        out_specs=block,
        scratch_shapes=[
            pltpu.VMEM((count, rows, rows * (lane_chunk // group_size)), jnp.bfloat16),
            pltpu.VMEM((rows * (lane_chunk // group_size), lane_chunk), jnp.bfloat16),
        ],
        out_shape=jax.ShapeDtypeStruct((rows, channels), jnp.bfloat16 if final else jnp.float32),
    )(*operands)


def shards(queries, keys, values, taps, segment_ids):
    rows = queries.shape[0]
    channels = queries.shape[1]
    filters = taps.shape[1]
    group_size = channels // filters
    ctx_count = lax.axis_size("ctx")
    own_index = lax.axis_index("ctx")
    core = own_index % 2
    tap_rows = taps.shape[0]
    filt_len = tap_rows * ctx_count
    lags = filt_len // rows
    seg_row = jnp.zeros((1, filters), jnp.bfloat16).at[0, :rows].set(segment_ids.astype(jnp.bfloat16))
    packed = jnp.concatenate([taps, seg_row], axis=0)
    packed = lax.all_gather(packed, "ctx", axis=0, tiled=False)
    packed, keys, values = lax.optimization_barrier((packed, keys, values))
    all_taps = packed[:, :tap_rows].reshape(filt_len, filters).astype(jnp.float32)
    all_segs = packed[:, tap_rows, :rows].astype(jnp.int32)
    gated = (keys.astype(jnp.float32) * values.astype(jnp.float32)).astype(jnp.bfloat16)
    padded = jnp.concatenate(
        [
            jnp.zeros((filters, rows + 1), jnp.float32),
            all_taps.T[:, ::-1],
            jnp.zeros((filters, rows - 1), jnp.float32),
        ],
        axis=1,
    )

    def window(lag):
        return lax.dynamic_slice_in_dim(padded, (lags - lag) * rows, 2 * rows, 1)

    def mask_for(lags_here):
        segs = [
            lax.dynamic_index_in_dim(all_segs, jnp.maximum(own_index - lag, 0), 0, keepdims=False)
            for lag in lags_here
        ]
        return (segment_ids[:, None] == jnp.concatenate(segs)[None, :]).astype(jnp.float32)

    two_back = shifted(gated, "ctx", 2)
    four_back = shifted(gated, "ctx", 4)
    swap_a = swapped(two_back, "ctx")
    swap_b = swapped(jnp.where(core == 1, four_back, gated), "ctx")
    lag_a = 1 + 2 * core
    lag_b = 3 - 2 * core
    first_lags = [jnp.int32(0), jnp.int32(2), lag_a]
    acc = conv_terms(
        [gated, two_back, swap_a], [window(lag) for lag in first_lags], mask_for(first_lags),
        [False, True, True], None, None, group_size,
    )
    last_lags = [jnp.int32(4), lag_b]
    return conv_terms(
        [four_back, swap_b], [window(lag) for lag in last_lags], mask_for(last_lags),
        [True, True], acc, queries, group_size,
    )


def solution(mesh):
    return jax.shard_map(
        shards,
        mesh=mesh,
        in_specs=(
            P(("dp", "ctx"), None),
            P(("dp", "ctx"), None),
            P(("dp", "ctx"), None),
            P("ctx", None),
            P(("dp", "ctx")),
        ),
        out_specs=P(("dp", "ctx"), None),
        check_vma=False,
    )
```

time: 112 us -> 134 us (1.20)
  Pallas kernels: 34.3 us -> 57.1 us
  waiting for transfers between devices: 43 us -> 38 us
  local copies, waits for them, and re-layouts: 2.23 us -> 6.21 us
    pallas_call x1 -> x2, Pallas kernels: 34.3 us -> 57.1 us  [conv_terms(): pl.pallas_call(kernel, grid=(channels // step_lanes,), in_specs=in_specs,...]
    dynamic_slice x0 -> x3, local copies, waits for them, and re-layouts: none -> 5.13 us  [window(): return lax.dynamic_slice_in_dim(padded, (lags - lag) * rows, 2 * rows, 1)]
    ppermute x2, waiting for transfers between devices: 43 us -> 38 us  [shifted(): lax.ppermute(value, axis, [(source, source + steps) for source in range(f...]
  transfers between devices with their start and end apart: 4 -> 4, of which waited for: 2 -> 2; matrix products, arithmetic and copies ran while one was open for 4% -> 7% of each run, Pallas kernels for 0% -> 25%
where the time goes in v6:
time: 134 us; the launch traced here: 133 us
  Pallas kernels  57.1 us (43%)
  waiting for transfers between devices  38 us (28%)
  blocking collectives  18.2 us (14%)
  other arithmetic  7.45 us (6%)
  local copies, waits for them, and re-layouts  6.21 us (5%)
  starting transfers between devices  5.97 us (4%)
    pallas_call x2, Pallas kernels, conv_terms(): pl.pallas_call(kernel, grid=(channels // step_lanes,), in_specs=in_specs,...  57.1 us
    ppermute x2, waiting for transfers between devices, shifted(): lax.ppermute(value, axis, [(source, source + steps) for source in range(f...  38 us
    all_gather x1, blocking collectives, shards(): packed = lax.all_gather(packed, 'ctx', axis=0, tiled=False)  18.2 us
    dynamic_slice x3, local copies, waits for them, and re-layouts, window(): return lax.dynamic_slice_in_dim(padded, (lags - lag) * rows, 2 * rows, 1)  5.13 us
    ppermute x2, starting transfers between devices, shifted(): lax.ppermute(value, axis, [(source, source + steps) for source in range(f...  3.84 us
  transfers between devices with their start and end apart: 4, of which 2 were waited for; matrix products, arithmetic and copies ran while one was open for 7% of the time, Pallas kernels for 25%

profile of v6, /device:TPU:25, one launch (start us, length us, event | category | flops | bytes accessed | tf_op | source)
XLA Modules:
  0.0 133.1 jit_solution(14330537684519765519)
XLA Ops:
  0.0 0.6 compare_reduce_fusion
  0.6 1.3 fusion.3
  1.9 0.7 fusion.2
  2.7 18.2 %all-gather.1 = bf16[16,33,256]{2,1,0:T(8,128)(2,1)S(1)} all-gather(bf16[1,33,256]{2,1,0:T(8,128)(2,1)S(1)} %fusion.2), channel_id=2, replica_groups=mesh['dp'=2,'ctx'=16] {'ctx'}, dimensions={0}, use_global_device_ids=true | all-gather | bytes 287232 | tf_op jit(solution)/shard_map/all_gather | solution.py:113
  20.9 1.8 %multiply_convert_fusion.refs_0_ = bf16[128,4096]{1,0:T(8,128)(2,1)S(1)} fusion(bf16[128,4096]{1,0:T(8,128)(2,1)} %param.9, bf16[128,4096]{1,0:T(8,128)(2,1)} %param.8), kind=kLoop, calls=%fused_computation | loop fusion | flops 2097152 | bytes 3145728 | tf_op jit(solution)/shard_map/convert_element_type | solution.py:117
  22.7 1.3 collective-permute-start
  24.0 2.5 %collective-permute-start.2 = (bf16[128,4096]{1,0:T(8,128)(2,1)S(1)}, bf16[128,4096]{1,0:T(8,128)(2,1)}, u32[]{:S(2)}, u32[]{:S(2)}) collective-permute-start(bf16[128,4096]{1,0:T(8,128)(2,1)S(1)} %multiply_convert_fusion.refs_0_), channel_id=1, source_target_pairs={{0,2},{1,3},{2,4},{3,5},{4,6},{5,7},{6,8},{7,9},{8,10},{9,11},{10,... | collective-permute-start | bytes 3145736 | tf_op jit(solution)/shard_map/ppermute | solution.py:14
  26.6 0.1 bitcast_convert_fusion
  26.6 0.2 copy.8
  26.8 0.8 rev.3
  27.6 0.9 dynamic_slice.44
  28.5 0.1 pad.14.clone
  28.5 3.1 %dynamic_slice.39.refs_4_ = f32[256,256]{1,0:T(8,128)} reverse(f32[256,256]{1,0:T(8,128)} %dynamic_slice.44), dimensions={1} | reverse | bytes 524288 | tf_op jit(solution)/shard_map/dynamic_slice | solution.py:128
  31.7 17.5 %collective-permute-done.refs_0_ = bf16[128,4096]{1,0:T(8,128)(2,1)S(1)} collective-permute-done((bf16[128,4096]{1,0:T(8,128)(2,1)S(1)}, bf16[128,4096]{1,0:T(8,128)(2,1)S(1)}, u32[]{:S(2)}, u32[]{:S(2)}) %collective-permute-start) | collective-permute-done | bytes 1048608 | tf_op jit(solution)/shard_map/ppermute | solution.py:14
  49.2 1.2 broadcast_select_fusion
  50.4 1.0 collective-permute-start.1
  51.3 20.5 %collective-permute-done.2.refs_1_ = bf16[128,4096]{1,0:T(8,128)(2,1)} collective-permute-done((bf16[128,4096]{1,0:T(8,128)(2,1)S(1)}, bf16[128,4096]{1,0:T(8,128)(2,1)}, u32[]{:S(2)}, u32[]{:S(2)}) %collective-permute-start.2) | collective-permute-done | bytes 1048608 | tf_op jit(solution)/shard_map/ppermute | solution.py:14
  71.9 1.2 collective-permute-start.3
  73.1 0.2 maximum_maximum_fusion
  73.3 1.2 pad_slice_fusion.1
  74.5 0.7 compare_convert_fusion.1.refs_4_
  75.2 0.8 compare_convert_fusion.refs_6_
  76.0 33.5 %shard_map.55.refs_5_ = f32[128,4096]{1,0:T(8,128)} custom-call(bf16[128,4096]{1,0:T(8,128)(2,1)} %copy-done, bf16[128,4096]{1,0:T(8,128)(2,1)} %collective-permute-done.2.refs_1_, bf16[128,4096]{1,0:T(8,128)(2,1)} %collective-permute-done.3.refs_2_, f32[256,256]{1,0:T(8,128)} %get-tuple-element.25.refs_3_, f32[256,256]{1,0:T(8,128)} %dynamic_slice.39.refs_4_, ...), custom_call_target="tpu_custom_call" | custom-call | tf_op jit(solution)/shard_map/pallas_call | solution.py:87
  109.5 23.6 %shard_map.56 = bf16[128,4096]{1,0:T(8,128)(2,1)} custom-call(bf16[128,4096]{1,0:T(8,128)(2,1)} %copy-done.1, bf16[128,4096]{1,0:T(8,128)(2,1)} %collective-permute-done.1.refs_1_, f32[256,256]{1,0:T(8,128)} %get-tuple-element.26.refs_2_, f32[256,256]{1,0:T(8,128)} %get-tuple-element.32.refs_3_, f32[128,256]{1,0:T(8,128)} %compare_convert_fusion.1.refs_4_, ...), custom_call_target="tpu_custom_call" | custom-call | tf_op jit(solution)/shard_map/pallas_call | solution.py:87
  (16 shorter events, 0.1 us)
Async XLA Ops:
  22.7 26.5 %copy-start = (bf16[128,4096]{1,0:T(8,128)(2,1)}, bf16[128,4096]{1,0:T(8,128)(2,1)S(1)}, u32[]{:S(2)}) copy-start(bf16[128,4096]{1,0:T(8,128)(2,1)S(1)} %multiply_convert_fusion.refs_0_) | copy-start | bytes 3145732
  22.7 26.5 %collective-permute-start = (bf16[128,4096]{1,0:T(8,128)(2,1)S(1)}, bf16[128,4096]{1,0:T(8,128)(2,1)S(1)}, u32[]{:S(2)}, u32[]{:S(2)}) collective-permute-start(bf16[128,4096]{1,0:T(8,128)(2,1)S(1)} %multiply_convert_fusion.refs_0_), channel_id=1, source_target_pairs={{0,4},{1,5},{2,6},{3,7},{4,8},{5,9},{6,10},{7,11},{8,12},{9,13},{1... | collective-permute-start | bytes 3145736 | tf_op jit(solution)/shard_map/ppermute | solution.py:14
  24.0 47.9 %collective-permute-start.2 = (bf16[128,4096]{1,0:T(8,128)(2,1)S(1)}, bf16[128,4096]{1,0:T(8,128)(2,1)}, u32[]{:S(2)}, u32[]{:S(2)}) collective-permute-start(bf16[128,4096]{1,0:T(8,128)(2,1)S(1)} %multiply_convert_fusion.refs_0_), channel_id=1, source_target_pairs={{0,2},{1,3},{2,4},{3,5},{4,6},{5,7},{6,8},{7,9},{8,10},{9,11},{10,... | collective-permute-start | bytes 3145736 | tf_op jit(solution)/shard_map/ppermute | solution.py:14
  49.2 24.2 %copy-start.1 = (bf16[128,4096]{1,0:T(8,128)(2,1)}, bf16[128,4096]{1,0:T(8,128)(2,1)S(1)}, u32[]{:S(2)}) copy-start(bf16[128,4096]{1,0:T(8,128)(2,1)S(1)} %collective-permute-done.refs_0_) | copy-start | bytes 3145732
  50.4 24.1 %copy-start.2 = (s32[128]{0:T(128)S(1)}, s32[128]{0:T(128)}, u32[]{:S(2)}) copy-start(s32[128]{0:T(128)} %param.11) | copy-start | bytes 1540
  50.4 59.1 %collective-permute-start.1 = (bf16[128,4096]{1,0:T(8,128)(2,1)}, bf16[128,4096]{1,0:T(8,128)(2,1)}, u32[]{:S(2)}, u32[]{:S(2)}) collective-permute-start(bf16[128,4096]{1,0:T(8,128)(2,1)} %broadcast_select_fusion), channel_id=1, source_target_pairs={{0,1},{1,0},{2,3},{3,2},{4,5},{5,4},{6,7},{7,6},{8,9},{9,8},{10,11... | collective-permute-start | bytes 3145736 | tf_op jit(solution)/shard_map/ppermute | solution.py:19
  71.9 4.1 %collective-permute-start.3 = (bf16[128,4096]{1,0:T(8,128)(2,1)}, bf16[128,4096]{1,0:T(8,128)(2,1)}, u32[]{:S(2)}, u32[]{:S(2)}) collective-permute-start(bf16[128,4096]{1,0:T(8,128)(2,1)} %collective-permute-done.2.refs_1_), channel_id=1, source_target_pairs={{0,1},{1,0},{2,3},{3,2},{4,5},{5,4},{6,7},{7,6},{8,9},{9,8},{10,11... | collective-permute-start | bytes 3145736 | tf_op jit(solution)/shard_map/ppermute | solution.py:19

commit v7 on v4

--- a/solution.py
+++ b/solution.py
@@ -74,11 +74,13 @@
     lags = filt_len // rows
     seg_row = jnp.zeros((1, filters), jnp.bfloat16).at[0, :rows].set(segment_ids.astype(jnp.bfloat16))
     packed = jnp.concatenate([taps, seg_row], axis=0)
+    gated = (keys.astype(jnp.float32) * values.astype(jnp.float32)).astype(jnp.bfloat16)
+    packed, gated = lax.optimization_barrier((packed, gated))
+    two_back = shifted(gated, "ctx", 2)
+    four_back = shifted(gated, "ctx", 4)
     packed = lax.all_gather(packed, "ctx", axis=0, tiled=False)
-    packed, keys, values = lax.optimization_barrier((packed, keys, values))
     all_taps = packed[:, :tap_rows].reshape(filt_len, filters).astype(jnp.float32)
     all_segs = packed[:, tap_rows, :rows].astype(jnp.int32)
-    gated = (keys.astype(jnp.float32) * values.astype(jnp.float32)).astype(jnp.bfloat16)
     padded = jnp.concatenate(
         [
             jnp.zeros((filters, rows + 1), jnp.float32),
@@ -92,8 +94,6 @@
         for lag in range(lags, -1, -1)
     ]
     mask = (segment_ids[:, None] == jnp.concatenate(seg_sources)[None, :]).astype(jnp.float32)
-    two_back = shifted(gated, "ctx", 2)
-    four_back = shifted(gated, "ctx", 4)
     swap_a = swapped(two_back, "ctx")
     swap_b = swapped(jnp.where(core == 1, four_back, gated), "ctx")
     sources = [four_back, swap_b, two_back, swap_a, gated]

time: 112 us -> 108 us (0.964)
  the two profiles are of different devices: /device:TPU:25 before, /device:TPU:7 now
where the time goes in v7:
time: 108 us; the launch traced here: 107 us
  blocking collectives  56.8 us (53%)
  Pallas kernels  34.3 us (32%)
  starting transfers between devices  6.86 us (6%)
  other arithmetic  6.36 us (6%)
  local copies, waits for them, and re-layouts  2.21 us (2%)
    all_gather x1, blocking collectives, shards(): packed = lax.all_gather(packed, 'ctx', axis=0, tiled=False)  56.8 us
    pallas_call x1, Pallas kernels, shards(): pl.pallas_call(kernel, grid_spec=pltpu.PrefetchScalarGridSpec(num_scalar_...  34.3 us
    ppermute x2, starting transfers between devices, shifted(): lax.ppermute(value, axis, [(source, source + steps) for source in range(f...  6.35 us
  transfers between devices with their start and end apart: 4, of which 1 were waited for; matrix products, arithmetic and copies ran while one was open for 4% of the time, Pallas kernels for 0%

profile of v7, /device:TPU:7, one launch (start us, length us, event | category | flops | bytes accessed | tf_op | source)
XLA Modules:
  0.0 107.5 jit_solution(9838948410132857259)
XLA Ops:
  0.0 0.6 compare_reduce_fusion
  0.6 1.8 %multiply_convert_fusion.refs_4_ = bf16[128,4096]{1,0:T(8,128)(2,1)S(1)} fusion(bf16[128,4096]{1,0:T(8,128)(2,1)} %param.9, bf16[128,4096]{1,0:T(8,128)(2,1)} %param.8), kind=kLoop, calls=%fused_computation | loop fusion | flops 2097152 | bytes 3145728 | tf_op jit(solution)/shard_map/convert_element_type | solution.py:77
  2.5 0.0 copy-done.4
  2.5 0.7 fusion.2
  3.2 3.3 %collective-permute-start = (bf16[128,4096]{1,0:T(8,128)(2,1)S(1)}, bf16[128,4096]{1,0:T(8,128)(2,1)S(1)}, u32[]{:S(2)}, u32[]{:S(2)}) collective-permute-start(bf16[128,4096]{1,0:T(8,128)(2,1)S(1)} %multiply_convert_fusion.refs_4_), channel_id=1, source_target_pairs={{0,4},{1,5},{2,6},{3,7},{4,8},{5,9},{6,10},{7,11},{8,12},{9,13},{1... | collective-permute-start | bytes 3145736 | tf_op jit(solution)/shard_map/ppermute | solution.py:14
  6.5 3.1 %collective-permute-start.2 = (bf16[128,4096]{1,0:T(8,128)(2,1)S(1)}, bf16[128,4096]{1,0:T(8,128)(2,1)}, u32[]{:S(2)}, u32[]{:S(2)}) collective-permute-start(bf16[128,4096]{1,0:T(8,128)(2,1)S(1)} %multiply_convert_fusion.refs_4_), channel_id=1, source_target_pairs={{0,2},{1,3},{2,4},{3,5},{4,6},{5,7},{6,8},{7,9},{8,10},{9,11},{10,... | collective-permute-start | bytes 3145736 | tf_op jit(solution)/shard_map/ppermute | solution.py:14
  9.6 56.8 %all-gather.1 = bf16[16,33,256]{2,1,0:T(8,128)(2,1)S(1)} all-gather(bf16[1,33,256]{2,1,0:T(8,128)(2,1)S(1)} %bitcast.29), channel_id=2, replica_groups=mesh['dp'=2,'ctx'=16] {'ctx'}, dimensions={0}, use_global_device_ids=true | all-gather | bytes 287232 | tf_op jit(solution)/shard_map/all_gather | solution.py:81
  66.4 0.1 bitcast_convert_fusion
  66.5 0.0 collective-permute-done.refs_0_
  66.5 0.0 copy-start.1
  66.5 1.2 %broadcast_select_fusion = bf16[128,4096]{1,0:T(8,128)(2,1)} fusion(bf16[128,4096]{1,0:T(8,128)(2,1)S(1)} %collective-permute-done.refs_0_, bf16[128,4096]{1,0:T(8,128)(2,1)S(1)} %multiply_convert_fusion.refs_4_, pred[]{:T(512)S(6)} %eq.18), kind=kLoop, calls=%fused_computation.1 | loop fusion | flops 524288 | bytes 3145729 | tf_op jit(solution)/shard_map/jit(_where)/select_n | solution.py:98
  67.7 0.1 copy-done.1
  67.8 0.2 collective-permute-start.1
  68.0 0.0 collective-permute-done.2.refs_2_
  68.0 0.3 collective-permute-start.3
  68.4 0.2 copy.8
  68.6 0.8 rev.3
  69.4 0.1 pad.7.clone
  69.5 0.8 compare_convert_fusion.refs_6_
  70.3 1.2 %maximum_maximum_fusion.refs_5_ = f32[256,768]{1,0:T(8,128)} fusion(f32[256,512]{1,0:T(8,128)S(1)} %rev.3, f32[768]{0:T(1024)S(1)} %pad.7.clone, f32[768]{0:T(1024)S(1)} %pad.5.clone), kind=kLoop, calls=%fused_computation.2 | loop fusion | flops 393216 | bytes 1316864 | tf_op jit(solution)/shard_map/concatenate | solution.py:84
  71.5 0.0 collective-permute-done.1.refs_1_
  71.5 0.7 collective-permute-done.3.refs_3_
  72.2 1.0 copy-done.2
  73.2 34.3 %shard_map.55 = bf16[128,4096]{1,0:T(8,128)(2,1)} custom-call(s32[1]{0:T(128)} %bitcast.core_ref, bf16[128,4096]{1,0:T(8,128)(2,1)} %copy-done.1, bf16[128,4096]{1,0:T(8,128)(2,1)} %collective-permute-done.1.refs_1_, bf16[128,4096]{1,0:T(8,128)(2,1)} %collective-permute-done.2.refs_2_, bf16[128,4096]{1,0:T(8,128)(2,1)} %copy-done.2, ...), custom_call_target="tpu_custom_call" | custom-call | tf_op jit(solution)/shard_map/pallas_call | solution.py:106
  (18 shorter events, 0.1 us)
Async XLA Ops:
  0.6 1.8 %copy-start.4 = (s32[128]{0:T(128)S(1)}, s32[128]{0:T(128)}, u32[]{:S(2)}) copy-start(s32[128]{0:T(128)} %param.11) | copy-start | bytes 1540
  0.6 2.5 %copy-start.3 = (bf16[32,256]{1,0:T(8,128)(2,1)S(1)}, bf16[32,256]{1,0:T(8,128)(2,1)}, u32[]{:S(2)}) copy-start(bf16[32,256]{1,0:T(8,128)(2,1)} %param.10) | copy-start | bytes 49156
  2.5 65.2 %copy-start = (bf16[128,4096]{1,0:T(8,128)(2,1)}, bf16[128,4096]{1,0:T(8,128)(2,1)S(1)}, u32[]{:S(2)}) copy-start(bf16[128,4096]{1,0:T(8,128)(2,1)S(1)} %multiply_convert_fusion.refs_4_) | copy-start | bytes 3145732
  3.2 63.3 %collective-permute-start = (bf16[128,4096]{1,0:T(8,128)(2,1)S(1)}, bf16[128,4096]{1,0:T(8,128)(2,1)S(1)}, u32[]{:S(2)}, u32[]{:S(2)}) collective-permute-start(bf16[128,4096]{1,0:T(8,128)(2,1)S(1)} %multiply_convert_fusion.refs_4_), channel_id=1, source_target_pairs={{0,4},{1,5},{2,6},{3,7},{4,8},{5,9},{6,10},{7,11},{8,12},{9,13},{1... | collective-permute-start | bytes 3145736 | tf_op jit(solution)/shard_map/ppermute | solution.py:14
  6.5 61.5 %collective-permute-start.2 = (bf16[128,4096]{1,0:T(8,128)(2,1)S(1)}, bf16[128,4096]{1,0:T(8,128)(2,1)}, u32[]{:S(2)}, u32[]{:S(2)}) collective-permute-start(bf16[128,4096]{1,0:T(8,128)(2,1)S(1)} %multiply_convert_fusion.refs_4_), channel_id=1, source_target_pairs={{0,2},{1,3},{2,4},{3,5},{4,6},{5,7},{6,8},{7,9},{8,10},{9,11},{10,... | collective-permute-start | bytes 3145736 | tf_op jit(solution)/shard_map/ppermute | solution.py:14
  66.5 1.3 %copy-start.1 = (bf16[128,4096]{1,0:T(8,128)(2,1)}, bf16[128,4096]{1,0:T(8,128)(2,1)S(1)}, u32[]{:S(2)}) copy-start(bf16[128,4096]{1,0:T(8,128)(2,1)S(1)} %collective-permute-done.refs_0_) | copy-start | bytes 3145732
  67.8 3.7 %collective-permute-start.1 = (bf16[128,4096]{1,0:T(8,128)(2,1)}, bf16[128,4096]{1,0:T(8,128)(2,1)}, u32[]{:S(2)}, u32[]{:S(2)}) collective-permute-start(bf16[128,4096]{1,0:T(8,128)(2,1)} %broadcast_select_fusion), channel_id=1, source_target_pairs={{0,1},{1,0},{2,3},{3,2},{4,5},{5,4},{6,7},{7,6},{8,9},{9,8},{10,11... | collective-permute-start | bytes 3145736 | tf_op jit(solution)/shard_map/ppermute | solution.py:19
  68.0 4.2 %collective-permute-start.3 = (bf16[128,4096]{1,0:T(8,128)(2,1)}, bf16[128,4096]{1,0:T(8,128)(2,1)S(1)}, u32[]{:S(2)}, u32[]{:S(2)}) collective-permute-start(bf16[128,4096]{1,0:T(8,128)(2,1)} %collective-permute-done.2.refs_2_), channel_id=1, source_target_pairs={{0,1},{1,0},{2,3},{3,2},{4,5},{5,4},{6,7},{7,6},{8,9},{9,8},{10,11... | collective-permute-start | bytes 3145736 | tf_op jit(solution)/shard_map/ppermute | solution.py:19
  72.2 1.0 copy-start.2

commit v8 on v4

--- a/solution.py
+++ b/solution.py
@@ -19,32 +19,35 @@
     return lax.ppermute(value, axis, [(source, source ^ 1) for source in range(count)])
 
 
+def weight_kernel(p_ref, m_ref, w_ref, *, lags, rows):
+    row = lax.broadcasted_iota(jnp.int32, (rows, rows), 0)
+    upper = lax.broadcasted_iota(jnp.int32, (rows, rows), 1) >= row
+    for k in range(p_ref.shape[0]):
+        tap_row = p_ref[k : k + 1, :]
+        rolled = [
+            pltpu.roll(
+                jnp.broadcast_to(tap_row[:, rows * m : rows * (m + 1)], (rows, rows)),
+                0,
+                1,
+                stride=1,
+                stride_axis=0,
+            )
+            for m in range(lags + 2)
+        ]
+        for n in range(lags + 1):
+            tile = jnp.where(upper, rolled[n + 1], rolled[n]) * m_ref[:, rows * n : rows * (n + 1)]
+            w_ref[n, :, rows * k : rows * (k + 1)] = tile.astype(jnp.bfloat16)
+
+
 def conv_kernel(core_ref, *refs, lags, rows, group_size):
     g_refs = list(refs[:lags + 1])
-    p_ref, m_ref, q_ref, o_ref, lhs_ref, rhs_ref = refs[lags + 1:]
+    w_ref, q_ref, o_ref, rhs_ref = refs[lags + 1:]
     lane_chunk = rhs_ref.shape[1]
     per_chunk = lane_chunk // group_size
-    row = lax.broadcasted_iota(jnp.int32, (rows, rows), 0)
-    upper = lax.broadcasted_iota(jnp.int32, (rows, rows), 1) >= row
     owner = lax.broadcasted_iota(jnp.int32, (rows, lane_chunk), 1) // group_size
     even = core_ref[0] == 0
     for u in range(q_ref.shape[1] // lane_chunk):
         lanes = slice(lane_chunk * u, lane_chunk * (u + 1))
-        for k in range(per_chunk):
-            tap_row = p_ref[u * per_chunk + k : u * per_chunk + k + 1, :]
-            rolled = [
-                pltpu.roll(
-                    jnp.broadcast_to(tap_row[:, rows * m : rows * (m + 1)], (rows, rows)),
-                    0,
-                    1,
-                    stride=1,
-                    stride_axis=0,
-                )
-                for m in range(lags + 2)
-            ]
-            for n in range(lags + 1):
-                tile = jnp.where(upper, rolled[n + 1], rolled[n]) * m_ref[:, rows * n : rows * (n + 1)]
-                lhs_ref[n, :, rows * k : rows * (k + 1)] = tile.astype(jnp.bfloat16)
         blocks = [g[:, lanes] for g in g_refs]
         near, far = blocks[lags - 1], blocks[lags - 3]
         blocks[lags - 1] = jnp.where(even, near, far)
@@ -54,7 +57,8 @@
             source = blocks[n]
             for k in range(per_chunk):
                 rhs_ref[rows * k : rows * (k + 1), :] = jnp.where(owner == k, source, jnp.zeros_like(source))
-            term = jnp.dot(lhs_ref[n], rhs_ref[...], preferred_element_type=jnp.float32)
+            weights = w_ref[n, :, rows * per_chunk * u : rows * per_chunk * (u + 1)]
+            term = jnp.dot(weights, rhs_ref[...], preferred_element_type=jnp.float32)
             if n < lags:
                 term = term.astype(jnp.bfloat16).astype(jnp.float32)
             acc = acc + term
@@ -94,13 +98,29 @@
     mask = (segment_ids[:, None] == jnp.concatenate(seg_sources)[None, :]).astype(jnp.float32)
     two_back = shifted(gated, "ctx", 2)
     four_back = shifted(gated, "ctx", 4)
+    lane_chunk = 128
+    step_lanes = lane_chunk * 4 if channels % (lane_chunk * 4) == 0 else lane_chunk
+    span = (lags + 1) * rows
+    step_filters = step_lanes // group_size
+    weights = pl.pallas_call(
+        functools.partial(weight_kernel, lags=lags, rows=rows),
+        grid=(channels // step_lanes,),
+        in_specs=[
+            pl.BlockSpec((step_filters, (lags + 2) * rows), lambda j: (j, 0)),
+            pl.BlockSpec((rows, span), lambda j: (0, 0)),
+        ],
+        out_specs=pl.BlockSpec((lags + 1, rows, step_filters * rows), lambda j: (0, 0, j)),
+        out_shape=jax.ShapeDtypeStruct((lags + 1, rows, filters * rows), jnp.bfloat16),
+        cost_estimate=pl.CostEstimate(
+            flops=8 * (lags + 1) * rows * rows * filters,
+            transcendentals=0,
+            bytes_accessed=2 * (lags + 1) * rows * rows * filters,
+        ),
+    )(padded, mask)
+    weights, two_back, four_back = lax.optimization_barrier((weights, two_back, four_back))
     swap_a = swapped(two_back, "ctx")
     swap_b = swapped(jnp.where(core == 1, four_back, gated), "ctx")
     sources = [four_back, swap_b, two_back, swap_a, gated]
-    lane_chunk = 128
-    per_chunk = lane_chunk // group_size
-    step_lanes = lane_chunk * 4 if channels % (lane_chunk * 4) == 0 else lane_chunk
-    span = (lags + 1) * rows
     kernel = functools.partial(conv_kernel, lags=lags, rows=rows, group_size=group_size)
     block = pl.BlockSpec((rows, step_lanes), lambda j, c: (0, j))
     return pl.pallas_call(
@@ -110,18 +130,14 @@
             grid=(channels // step_lanes,),
             in_specs=[block] * (lags + 1)
             + [
-                pl.BlockSpec((step_lanes // group_size, (lags + 2) * rows), lambda j, c: (j, 0)),
-                pl.BlockSpec((rows, span), lambda j, c: (0, 0)),
+                pl.BlockSpec((lags + 1, rows, step_filters * rows), lambda j, c: (0, 0, j)),
                 block,
             ],
             out_specs=block,
-            scratch_shapes=[
-                pltpu.VMEM((lags + 1, rows, rows * per_chunk), jnp.bfloat16),
-                pltpu.VMEM((rows * per_chunk, lane_chunk), jnp.bfloat16),
-            ],
+            scratch_shapes=[pltpu.VMEM((rows * (lane_chunk // group_size), lane_chunk), jnp.bfloat16)],
         ),
         out_shape=jax.ShapeDtypeStruct((rows, channels), jnp.bfloat16),
-    )(jnp.reshape(core, (1,)).astype(jnp.int32), *sources, padded, mask, queries)
+    )(jnp.reshape(core, (1,)).astype(jnp.int32), *sources, weights, queries)
 
 
 def solution(mesh):

time: 112 us -> 98.7 us (0.88)
  waiting for transfers between devices: 43 us -> 16.2 us
  Pallas kernels: 34.3 us -> 49.9 us
    ppermute x2, waiting for transfers between devices: 43 us -> 12.3 us  [shifted(): lax.ppermute(value, axis, [(source, source + steps) for source in range(f...]
    pallas_call x0 -> x1, Pallas kernels: none -> 29.8 us  [shards(): pl.pallas_call(functools.partial(weight_kernel, lags=lags, rows=rows), gr...]
    pallas_call x1, Pallas kernels: 34.3 us -> 20 us  [shards(): pl.pallas_call(kernel, grid_spec=pltpu.PrefetchScalarGridSpec(num_scalar_...]
    ppermute x2, waiting for transfers between devices: 0.01 us -> 3.92 us  [swapped(): lax.ppermute(value, axis, [(source, source ^ 1) for source in range(count)])]
  transfers between devices with their start and end apart: 4 -> 4, of which waited for: 2 -> 3; matrix products, arithmetic and copies ran while one was open for 4% -> 3% of each run, Pallas kernels for 0% -> 30%
where the time goes in v8:
time: 98.7 us; the launch traced here: 98.4 us
  Pallas kernels  49.9 us (51%)
  blocking collectives  18.2 us (18%)
  waiting for transfers between devices  16.2 us (16%)
  other arithmetic  6.57 us (7%)
  starting transfers between devices  5.28 us (5%)
  local copies, waits for them, and re-layouts  2.08 us (2%)
    pallas_call x1, Pallas kernels, shards(): pl.pallas_call(functools.partial(weight_kernel, lags=lags, rows=rows), gr...  29.8 us
    pallas_call x1, Pallas kernels, shards(): pl.pallas_call(kernel, grid_spec=pltpu.PrefetchScalarGridSpec(num_scalar_...  20 us
    all_gather x1, blocking collectives, shards(): packed = lax.all_gather(packed, 'ctx', axis=0, tiled=False)  18.2 us
    ppermute x2, waiting for transfers between devices, shifted(): lax.ppermute(value, axis, [(source, source + steps) for source in range(f...  12.3 us
    ppermute x2, starting transfers between devices, shifted(): lax.ppermute(value, axis, [(source, source + steps) for source in range(f...  3.97 us
    ppermute x2, waiting for transfers between devices, swapped(): lax.ppermute(value, axis, [(source, source ^ 1) for source in range(count)])  3.92 us
  transfers between devices with their start and end apart: 4, of which 3 were waited for; matrix products, arithmetic and copies ran while one was open for 3% of the time, Pallas kernels for 30%

profile of v8, /device:TPU:25, one launch (start us, length us, event | category | flops | bytes accessed | tf_op | source)
XLA Modules:
  0.0 98.4 jit_solution(10699240061274133719)
XLA Ops:
  0.0 0.6 compare_reduce_fusion
  0.6 1.3 %fusion.3 = bf16[1,128]{1,0:T(2,128)(2,1)S(1)} fusion(pred[]{:T(512)} %compare_reduce_fusion, s32[128]{0:T(128)} %param.11), kind=kLoop, calls=%fused_computation.22 | loop fusion | flops 256 | bytes 769 | tf_op jit(solution)/shard_map/reshape.29
  1.9 0.7 fusion.2
  2.7 18.2 %all-gather.1 = bf16[16,33,256]{2,1,0:T(8,128)(2,1)S(1)} all-gather(bf16[1,33,256]{2,1,0:T(8,128)(2,1)S(1)} %fusion.2), channel_id=2, replica_groups=mesh['dp'=2,'ctx'=16] {'ctx'}, dimensions={0}, use_global_device_ids=true | all-gather | bytes 287232 | tf_op jit(solution)/shard_map/all_gather | solution.py:81
  20.9 1.8 %multiply_convert_fusion.refs_4_ = bf16[128,4096]{1,0:T(8,128)(2,1)S(1)} fusion(bf16[128,4096]{1,0:T(8,128)(2,1)} %param.9, bf16[128,4096]{1,0:T(8,128)(2,1)} %param.8), kind=kLoop, calls=%fused_computation | loop fusion | flops 2097152 | bytes 3145728 | tf_op jit(solution)/shard_map/convert_element_type | solution.py:85
  22.7 0.0 copy-start.4
  22.7 1.4 %collective-permute-start.1 = (bf16[128,4096]{1,0:T(8,128)(2,1)S(1)}, bf16[128,4096]{1,0:T(8,128)(2,1)S(1)}, u32[]{:S(2)}, u32[]{:S(2)}) collective-permute-start(bf16[128,4096]{1,0:T(8,128)(2,1)S(1)} %multiply_convert_fusion.refs_4_), channel_id=1, source_target_pairs={{0,4},{1,5},{2,6},{3,7},{4,8},{5,9},{6,10},{7,11},{8,12},{9,13},{1... | collective-permute-start | bytes 3145736 | tf_op jit(solution)/shard_map/ppermute | solution.py:14
  24.1 2.5 %collective-permute-start = (bf16[128,4096]{1,0:T(8,128)(2,1)S(1)}, bf16[128,4096]{1,0:T(8,128)(2,1)}, u32[]{:S(2)}, u32[]{:S(2)}) collective-permute-start(bf16[128,4096]{1,0:T(8,128)(2,1)S(1)} %multiply_convert_fusion.refs_4_), channel_id=1, source_target_pairs={{0,2},{1,3},{2,4},{3,5},{4,6},{5,7},{6,8},{7,9},{8,10},{9,11},{10,... | collective-permute-start | bytes 3145736 | tf_op jit(solution)/shard_map/ppermute | solution.py:14
  26.8 0.1 pad.7.clone
  26.9 0.1 bitcast_convert_fusion
  26.9 0.2 copy.8
  27.1 0.8 rev.3
  28.0 0.8 compare_convert_fusion.m_ref
  28.8 1.1 %maximum_maximum_fusion.p_ref = f32[256,768]{1,0:T(8,128)} fusion(f32[256,512]{1,0:T(8,128)S(1)} %rev.3, f32[768]{0:T(1024)S(1)} %pad.7.clone, f32[768]{0:T(1024)S(1)} %pad.5.clone), kind=kLoop, calls=%fused_computation.2 | loop fusion | flops 393216 | bytes 1316864 | tf_op jit(solution)/shard_map/concatenate | solution.py:86
  29.9 29.8 %shard_map.55.refs_5_ = bf16[5,128,32768]{2,1,0:T(8,128)(2,1)} custom-call(f32[256,768]{1,0:T(8,128)} %maximum_maximum_fusion.p_ref, f32[128,640]{1,0:T(8,128)} %compare_convert_fusion.m_ref), custom_call_target="tpu_custom_call" | custom-call | flops 167772160 | bytes 41943040 | tf_op jit(solution)/shard_map/pallas_call | solution.py:105
  59.8 0.0 collective-permute-done.1.refs_0_
  59.8 12.3 %collective-permute-done.refs_2_ = bf16[128,4096]{1,0:T(8,128)(2,1)} collective-permute-done((bf16[128,4096]{1,0:T(8,128)(2,1)S(1)}, bf16[128,4096]{1,0:T(8,128)(2,1)}, u32[]{:S(2)}, u32[]{:S(2)}) %collective-permute-start) | collective-permute-done | bytes 1048608 | tf_op jit(solution)/shard_map/ppermute | solution.py:14
  72.0 0.1 broadcast_select_fusion
  72.1 1.2 %collective-permute-start.2 = (bf16[128,4096]{1,0:T(8,128)(2,1)S(1)}, bf16[128,4096]{1,0:T(8,128)(2,1)S(1)}, u32[]{:S(2)}, u32[]{:S(2)}) collective-permute-start(bf16[128,4096]{1,0:T(8,128)(2,1)S(1)} %broadcast_select_fusion), channel_id=1, source_target_pairs={{0,1},{1,0},{2,3},{3,2},{4,5},{5,4},{6,7},{7,6},{8,9},{9,8},{10,11... | collective-permute-start | bytes 3145736 | tf_op jit(solution)/shard_map/ppermute | solution.py:19
  73.4 0.1 collective-permute-start.3
  73.5 2.9 %collective-permute-done.2.refs_1_ = bf16[128,4096]{1,0:T(8,128)(2,1)S(1)} collective-permute-done((bf16[128,4096]{1,0:T(8,128)(2,1)S(1)}, bf16[128,4096]{1,0:T(8,128)(2,1)S(1)}, u32[]{:S(2)}, u32[]{:S(2)}) %collective-permute-start.2) | collective-permute-done | bytes 1048608 | tf_op jit(solution)/shard_map/ppermute | solution.py:19
  76.4 1.0 %collective-permute-done.3.refs_3_ = bf16[128,4096]{1,0:T(8,128)(2,1)S(1)} collective-permute-done((bf16[128,4096]{1,0:T(8,128)(2,1)}, bf16[128,4096]{1,0:T(8,128)(2,1)S(1)}, u32[]{:S(2)}, u32[]{:S(2)}) %collective-permute-start.3) | collective-permute-done | bytes 1048608 | tf_op jit(solution)/shard_map/ppermute | solution.py:19
  77.4 0.9 copy-done.3
  78.3 20.0 %shard_map.56 = bf16[128,4096]{1,0:T(8,128)(2,1)} custom-call(s32[1]{0:T(128)} %bitcast.core_ref, bf16[128,4096]{1,0:T(8,128)(2,1)} %copy-done.1, bf16[128,4096]{1,0:T(8,128)(2,1)} %copy-done.2, bf16[128,4096]{1,0:T(8,128)(2,1)} %collective-permute-done.refs_2_, bf16[128,4096]{1,0:T(8,128)(2,1)} %copy-done.3, bf16[128,4096]{1,0:T(8,128)(2,1)} %copy-done, ...), custom_call_target="tpu_custom_call" | custom-call | tf_op jit(solution)/shard_map/pallas_call | solution.py:126
  (19 shorter events, 0.1 us)
Async XLA Ops:
  22.7 49.4 %copy-start = (bf16[128,4096]{1,0:T(8,128)(2,1)}, bf16[128,4096]{1,0:T(8,128)(2,1)S(1)}, u32[]{:S(2)}) copy-start(bf16[128,4096]{1,0:T(8,128)(2,1)S(1)} %multiply_convert_fusion.refs_4_) | copy-start | bytes 3145732
  22.7 5.3 %copy-start.4 = (s32[128]{0:T(128)S(1)}, s32[128]{0:T(128)}, u32[]{:S(2)}) copy-start(s32[128]{0:T(128)} %param.11) | copy-start | bytes 1540
  22.7 37.1 %collective-permute-start.1 = (bf16[128,4096]{1,0:T(8,128)(2,1)S(1)}, bf16[128,4096]{1,0:T(8,128)(2,1)S(1)}, u32[]{:S(2)}, u32[]{:S(2)}) collective-permute-start(bf16[128,4096]{1,0:T(8,128)(2,1)S(1)} %multiply_convert_fusion.refs_4_), channel_id=1, source_target_pairs={{0,4},{1,5},{2,6},{3,7},{4,8},{5,9},{6,10},{7,11},{8,12},{9,13},{1... | collective-permute-start | bytes 3145736 | tf_op jit(solution)/shard_map/ppermute | solution.py:14
  24.1 47.9 %collective-permute-start = (bf16[128,4096]{1,0:T(8,128)(2,1)S(1)}, bf16[128,4096]{1,0:T(8,128)(2,1)}, u32[]{:S(2)}, u32[]{:S(2)}) collective-permute-start(bf16[128,4096]{1,0:T(8,128)(2,1)S(1)} %multiply_convert_fusion.refs_4_), channel_id=1, source_target_pairs={{0,2},{1,3},{2,4},{3,5},{4,6},{5,7},{6,8},{7,9},{8,10},{9,11},{10,... | collective-permute-start | bytes 3145736 | tf_op jit(solution)/shard_map/ppermute | solution.py:14
  59.8 17.6 %copy-start.1 = (bf16[128,4096]{1,0:T(8,128)(2,1)}, bf16[128,4096]{1,0:T(8,128)(2,1)S(1)}, u32[]{:S(2)}) copy-start(bf16[128,4096]{1,0:T(8,128)(2,1)S(1)} %collective-permute-done.1.refs_0_) | copy-start | bytes 3145732
  72.1 4.2 %collective-permute-start.2 = (bf16[128,4096]{1,0:T(8,128)(2,1)S(1)}, bf16[128,4096]{1,0:T(8,128)(2,1)S(1)}, u32[]{:S(2)}, u32[]{:S(2)}) collective-permute-start(bf16[128,4096]{1,0:T(8,128)(2,1)S(1)} %broadcast_select_fusion), channel_id=1, source_target_pairs={{0,1},{1,0},{2,3},{3,2},{4,5},{5,4},{6,7},{7,6},{8,9},{9,8},{10,11... | collective-permute-start | bytes 3145736 | tf_op jit(solution)/shard_map/ppermute | solution.py:19
  73.4 4.0 %collective-permute-start.3 = (bf16[128,4096]{1,0:T(8,128)(2,1)}, bf16[128,4096]{1,0:T(8,128)(2,1)S(1)}, u32[]{:S(2)}, u32[]{:S(2)}) collective-permute-start(bf16[128,4096]{1,0:T(8,128)(2,1)} %collective-permute-done.refs_2_), channel_id=1, source_target_pairs={{0,1},{1,0},{2,3},{3,2},{4,5},{5,4},{6,7},{7,6},{8,9},{9,8},{10,11... | collective-permute-start | bytes 3145736 | tf_op jit(solution)/shard_map/ppermute | solution.py:19
  76.4 1.0 %copy-start.2 = (bf16[128,4096]{1,0:T(8,128)(2,1)}, bf16[128,4096]{1,0:T(8,128)(2,1)S(1)}, u32[]{:S(2)}) copy-start(bf16[128,4096]{1,0:T(8,128)(2,1)S(1)} %collective-permute-done.2.refs_1_) | copy-start | bytes 3145732
  77.4 1.0 copy-start.3

commit v9 on v4

--- a/solution.py
+++ b/solution.py
@@ -19,19 +19,16 @@
     return lax.ppermute(value, axis, [(source, source ^ 1) for source in range(count)])
 
 
-def conv_kernel(core_ref, *refs, lags, rows, group_size):
-    g_refs = list(refs[:lags + 1])
-    p_ref, m_ref, q_ref, o_ref, lhs_ref, rhs_ref = refs[lags + 1:]
+def weight_kernel(p_ref, m_ref, g_ref, w_ref, a_ref, lhs_ref, rhs_ref, *, lags, rows, group_size):
+    row = lax.broadcasted_iota(jnp.int32, (rows, rows), 0)
+    upper = lax.broadcasted_iota(jnp.int32, (rows, rows), 1) >= row
     lane_chunk = rhs_ref.shape[1]
     per_chunk = lane_chunk // group_size
-    row = lax.broadcasted_iota(jnp.int32, (rows, rows), 0)
-    upper = lax.broadcasted_iota(jnp.int32, (rows, rows), 1) >= row
     owner = lax.broadcasted_iota(jnp.int32, (rows, lane_chunk), 1) // group_size
-    even = core_ref[0] == 0
-    for u in range(q_ref.shape[1] // lane_chunk):
-        lanes = slice(lane_chunk * u, lane_chunk * (u + 1))
-        for k in range(per_chunk):
-            tap_row = p_ref[u * per_chunk + k : u * per_chunk + k + 1, :]
+    for u in range(g_ref.shape[1] // lane_chunk):
+        for j in range(per_chunk):
+            k = u * per_chunk + j
+            tap_row = p_ref[k : k + 1, :]
             rolled = [
                 pltpu.roll(
                     jnp.broadcast_to(tap_row[:, rows * m : rows * (m + 1)], (rows, rows)),
@@ -44,20 +41,38 @@
             ]
             for n in range(lags + 1):
                 tile = jnp.where(upper, rolled[n + 1], rolled[n]) * m_ref[:, rows * n : rows * (n + 1)]
-                lhs_ref[n, :, rows * k : rows * (k + 1)] = tile.astype(jnp.bfloat16)
+                if n < lags:
+                    w_ref[n, :, rows * k : rows * (k + 1)] = tile.astype(jnp.bfloat16)
+                else:
+                    lhs_ref[:, rows * j : rows * (j + 1)] = tile.astype(jnp.bfloat16)
+        lanes = slice(lane_chunk * u, lane_chunk * (u + 1))
+        source = g_ref[:, lanes]
+        for j in range(per_chunk):
+            rhs_ref[rows * j : rows * (j + 1), :] = jnp.where(owner == j, source, jnp.zeros_like(source))
+        a_ref[:, lanes] = jnp.dot(lhs_ref[...], rhs_ref[...], preferred_element_type=jnp.float32)
+
+
+def conv_kernel(core_ref, *refs, lags, rows, group_size):
+    g_refs = list(refs[:lags])
+    w_ref, a_ref, q_ref, o_ref, rhs_ref = refs[lags:]
+    lane_chunk = rhs_ref.shape[1]
+    per_chunk = lane_chunk // group_size
+    owner = lax.broadcasted_iota(jnp.int32, (rows, lane_chunk), 1) // group_size
+    even = core_ref[0] == 0
+    for u in range(q_ref.shape[1] // lane_chunk):
+        lanes = slice(lane_chunk * u, lane_chunk * (u + 1))
         blocks = [g[:, lanes] for g in g_refs]
         near, far = blocks[lags - 1], blocks[lags - 3]
         blocks[lags - 1] = jnp.where(even, near, far)
         blocks[lags - 3] = jnp.where(even, far, near)
-        acc = jnp.zeros((rows, lane_chunk), jnp.float32)
-        for n in range(lags + 1):
+        acc = a_ref[:, lanes]
+        for n in range(lags):
             source = blocks[n]
             for k in range(per_chunk):
                 rhs_ref[rows * k : rows * (k + 1), :] = jnp.where(owner == k, source, jnp.zeros_like(source))
-            term = jnp.dot(lhs_ref[n], rhs_ref[...], preferred_element_type=jnp.float32)
-            if n < lags:
-                term = term.astype(jnp.bfloat16).astype(jnp.float32)
-            acc = acc + term
+            weights = w_ref[n, :, rows * per_chunk * u : rows * per_chunk * (u + 1)]
+            term = jnp.dot(weights, rhs_ref[...], preferred_element_type=jnp.float32)
+            acc = acc + term.astype(jnp.bfloat16).astype(jnp.float32)
         o_ref[:, lanes] = (q_ref[:, lanes].astype(jnp.float32) * acc).astype(o_ref.dtype)
 
 
@@ -94,13 +109,35 @@
     mask = (segment_ids[:, None] == jnp.concatenate(seg_sources)[None, :]).astype(jnp.float32)
     two_back = shifted(gated, "ctx", 2)
     four_back = shifted(gated, "ctx", 4)
+    lane_chunk = 128
+    step_lanes = lane_chunk * 4 if channels % (lane_chunk * 4) == 0 else lane_chunk
+    span = (lags + 1) * rows
+    step_filters = step_lanes // group_size
+    weights, own_term = pl.pallas_call(
+        functools.partial(weight_kernel, lags=lags, rows=rows, group_size=group_size),
+        grid=(channels // step_lanes,),
+        in_specs=[
+            pl.BlockSpec((step_filters, (lags + 2) * rows), lambda j: (j, 0)),
+            pl.BlockSpec((rows, span), lambda j: (0, 0)),
+            pl.BlockSpec((rows, step_lanes), lambda j: (0, j)),
+        ],
+        out_specs=[
+            pl.BlockSpec((lags, rows, step_filters * rows), lambda j: (0, 0, j)),
+            pl.BlockSpec((rows, step_lanes), lambda j: (0, j)),
+        ],
+        out_shape=[
+            jax.ShapeDtypeStruct((lags, rows, filters * rows), jnp.bfloat16),
+            jax.ShapeDtypeStruct((rows, channels), jnp.float32),
+        ],
+        scratch_shapes=[
+            pltpu.VMEM((rows, rows * (lane_chunk // group_size)), jnp.bfloat16),
+            pltpu.VMEM((rows * (lane_chunk // group_size), lane_chunk), jnp.bfloat16),
+        ],
+    )(padded, mask, gated)
+    weights, own_term, two_back, four_back = lax.optimization_barrier((weights, own_term, two_back, four_back))
     swap_a = swapped(two_back, "ctx")
     swap_b = swapped(jnp.where(core == 1, four_back, gated), "ctx")
-    sources = [four_back, swap_b, two_back, swap_a, gated]
-    lane_chunk = 128
-    per_chunk = lane_chunk // group_size
-    step_lanes = lane_chunk * 4 if channels % (lane_chunk * 4) == 0 else lane_chunk
-    span = (lags + 1) * rows
+    sources = [four_back, swap_b, two_back, swap_a]
     kernel = functools.partial(conv_kernel, lags=lags, rows=rows, group_size=group_size)
     block = pl.BlockSpec((rows, step_lanes), lambda j, c: (0, j))
     return pl.pallas_call(
@@ -108,20 +145,17 @@
         grid_spec=pltpu.PrefetchScalarGridSpec(
             num_scalar_prefetch=1,
             grid=(channels // step_lanes,),
-            in_specs=[block] * (lags + 1)
+            in_specs=[block] * lags
             + [
-                pl.BlockSpec((step_lanes // group_size, (lags + 2) * rows), lambda j, c: (j, 0)),
-                pl.BlockSpec((rows, span), lambda j, c: (0, 0)),
+                pl.BlockSpec((lags, rows, step_filters * rows), lambda j, c: (0, 0, j)),
+                block,
                 block,
             ],
             out_specs=block,
-            scratch_shapes=[
-                pltpu.VMEM((lags + 1, rows, rows * per_chunk), jnp.bfloat16),
-                pltpu.VMEM((rows * per_chunk, lane_chunk), jnp.bfloat16),
-            ],
+            scratch_shapes=[pltpu.VMEM((rows * (lane_chunk // group_size), lane_chunk), jnp.bfloat16)],
         ),
         out_shape=jax.ShapeDtypeStruct((rows, channels), jnp.bfloat16),
-    )(jnp.reshape(core, (1,)).astype(jnp.int32), *sources, padded, mask, queries)
+    )(jnp.reshape(core, (1,)).astype(jnp.int32), *sources, weights, own_term, queries)
 
 
 def solution(mesh):

time: 112 us -> 98.1 us (0.88)
  waiting for transfers between devices: 43 us -> 14.8 us
  Pallas kernels: 34.3 us -> 49.3 us
    ppermute x2, waiting for transfers between devices: 43 us -> 10.9 us  [shifted(): lax.ppermute(value, axis, [(source, source + steps) for source in range(f...]
    pallas_call x0 -> x1, Pallas kernels: none -> 31.1 us  [shards(): pl.pallas_call(functools.partial(weight_kernel, lags=lags, rows=rows, gro...]
    pallas_call x1, Pallas kernels: 34.3 us -> 18.2 us  [shards(): pl.pallas_call(kernel, grid_spec=pltpu.PrefetchScalarGridSpec(num_scalar_...]
    ppermute x2, waiting for transfers between devices: 0.01 us -> 3.92 us  [swapped(): lax.ppermute(value, axis, [(source, source ^ 1) for source in range(count)])]
  transfers between devices with their start and end apart: 4 -> 4, of which waited for: 2 -> 3; matrix products, arithmetic and copies ran while one was open for 4% -> 3% of each run, Pallas kernels for 0% -> 32%
where the time goes in v9:
time: 98.1 us; the launch traced here: 97.8 us
  Pallas kernels  49.3 us (50%)
  blocking collectives  18.2 us (19%)
  waiting for transfers between devices  14.8 us (15%)
  other arithmetic  6.61 us (7%)
  starting transfers between devices  6.51 us (7%)
  local copies, waits for them, and re-layouts  2.07 us (2%)
    pallas_call x1, Pallas kernels, shards(): pl.pallas_call(functools.partial(weight_kernel, lags=lags, rows=rows, gro...  31.1 us
    pallas_call x1, Pallas kernels, shards(): pl.pallas_call(kernel, grid_spec=pltpu.PrefetchScalarGridSpec(num_scalar_...  18.2 us
    all_gather x1, blocking collectives, shards(): packed = lax.all_gather(packed, 'ctx', axis=0, tiled=False)  18.2 us
    ppermute x2, waiting for transfers between devices, shifted(): lax.ppermute(value, axis, [(source, source + steps) for source in range(f...  10.9 us
    ppermute x2, starting transfers between devices, shifted(): lax.ppermute(value, axis, [(source, source + steps) for source in range(f...  3.97 us
    ppermute x2, waiting for transfers between devices, swapped(): lax.ppermute(value, axis, [(source, source ^ 1) for source in range(count)])  3.92 us
    ppermute x2, starting transfers between devices, swapped(): lax.ppermute(value, axis, [(source, source ^ 1) for source in range(count)])  2.54 us
  transfers between devices with their start and end apart: 4, of which 3 were waited for; matrix products, arithmetic and copies ran while one was open for 3% of the time, Pallas kernels for 32%

profile of v9, /device:TPU:25, one launch (start us, length us, event | category | flops | bytes accessed | tf_op | source)
XLA Modules:
  0.0 97.8 jit_solution(4351814953584064881)
XLA Ops:
  0.0 0.6 compare_reduce_fusion
  0.6 1.3 %fusion.3 = bf16[1,128]{1,0:T(2,128)(2,1)S(1)} fusion(pred[]{:T(512)} %compare_reduce_fusion, s32[128]{0:T(128)} %param.11), kind=kLoop, calls=%fused_computation.22 | loop fusion | flops 256 | bytes 769 | tf_op jit(solution)/shard_map/reshape.29
  1.9 0.7 fusion.2
  2.7 18.2 %all-gather.1 = bf16[16,33,256]{2,1,0:T(8,128)(2,1)S(1)} all-gather(bf16[1,33,256]{2,1,0:T(8,128)(2,1)S(1)} %fusion.2), channel_id=2, replica_groups=mesh['dp'=2,'ctx'=16] {'ctx'}, dimensions={0}, use_global_device_ids=true | all-gather | bytes 287232 | tf_op jit(solution)/shard_map/all_gather | solution.py:92
  20.9 1.8 %multiply_convert_fusion.g_ref = bf16[128,4096]{1,0:T(8,128)(2,1)S(1)} fusion(bf16[128,4096]{1,0:T(8,128)(2,1)} %param.9, bf16[128,4096]{1,0:T(8,128)(2,1)} %param.8), kind=kLoop, calls=%fused_computation | loop fusion | flops 2097152 | bytes 3145728 | tf_op jit(solution)/shard_map/convert_element_type | solution.py:96
  22.7 0.0 copy-start
  22.7 0.0 copy-start.4
  22.7 1.4 %collective-permute-start.1 = (bf16[128,4096]{1,0:T(8,128)(2,1)S(1)}, bf16[128,4096]{1,0:T(8,128)(2,1)S(1)}, u32[]{:S(2)}, u32[]{:S(2)}) collective-permute-start(bf16[128,4096]{1,0:T(8,128)(2,1)S(1)} %multiply_convert_fusion.g_ref), channel_id=1, source_target_pairs={{0,4},{1,5},{2,6},{3,7},{4,8},{5,9},{6,10},{7,11},{8,12},{9,13},{1... | collective-permute-start | bytes 3145736 | tf_op jit(solution)/shard_map/ppermute | solution.py:14
  24.1 2.5 %collective-permute-start = (bf16[128,4096]{1,0:T(8,128)(2,1)S(1)}, bf16[128,4096]{1,0:T(8,128)(2,1)}, u32[]{:S(2)}, u32[]{:S(2)}) collective-permute-start(bf16[128,4096]{1,0:T(8,128)(2,1)S(1)} %multiply_convert_fusion.g_ref), channel_id=1, source_target_pairs={{0,2},{1,3},{2,4},{3,5},{4,6},{5,7},{6,8},{7,9},{8,10},{9,11},{10,... | collective-permute-start | bytes 3145736 | tf_op jit(solution)/shard_map/ppermute | solution.py:14
  26.7 0.1 bitcast_convert_fusion
  26.8 0.1 pad.7.clone
  26.9 0.2 copy.8
  27.1 0.8 rev.3
  28.0 0.8 compare_convert_fusion.m_ref
  28.8 1.2 %maximum_maximum_fusion.p_ref = f32[256,768]{1,0:T(8,128)} fusion(f32[256,512]{1,0:T(8,128)S(1)} %rev.3, f32[768]{0:T(1024)S(1)} %pad.7.clone, f32[768]{0:T(1024)S(1)} %pad.5.clone), kind=kLoop, calls=%fused_computation.2 | loop fusion | flops 393216 | bytes 1316864 | tf_op jit(solution)/shard_map/concatenate | solution.py:97
  30.0 31.1 %shard_map.55 = (bf16[4,128,32768]{2,1,0:T(8,128)(2,1)}, f32[128,4096]{1,0:T(8,128)}) custom-call(f32[256,768]{1,0:T(8,128)} %maximum_maximum_fusion.p_ref, f32[128,640]{1,0:T(8,128)} %compare_convert_fusion.m_ref, bf16[128,4096]{1,0:T(8,128)(2,1)} %copy-done), custom_call_target="tpu_custom_call" | custom-call | tf_op jit(solution)/shard_map/pallas_call | solution.py:116
  61.1 10.9 %collective-permute-done.refs_2_ = bf16[128,4096]{1,0:T(8,128)(2,1)} collective-permute-done((bf16[128,4096]{1,0:T(8,128)(2,1)S(1)}, bf16[128,4096]{1,0:T(8,128)(2,1)}, u32[]{:S(2)}, u32[]{:S(2)}) %collective-permute-start) | collective-permute-done | bytes 1048608 | tf_op jit(solution)/shard_map/ppermute | solution.py:14
  72.0 0.1 broadcast_select_fusion
  72.1 2.5 %collective-permute-start.2 = (bf16[128,4096]{1,0:T(8,128)(2,1)S(1)}, bf16[128,4096]{1,0:T(8,128)(2,1)S(1)}, u32[]{:S(2)}, u32[]{:S(2)}) collective-permute-start(bf16[128,4096]{1,0:T(8,128)(2,1)S(1)} %broadcast_select_fusion), channel_id=1, source_target_pairs={{0,1},{1,0},{2,3},{3,2},{4,5},{5,4},{6,7},{7,6},{8,9},{9,8},{10,11... | collective-permute-start | bytes 3145736 | tf_op jit(solution)/shard_map/ppermute | solution.py:19
  74.6 0.1 collective-permute-start.3
  74.7 2.9 %collective-permute-done.2.refs_1_ = bf16[128,4096]{1,0:T(8,128)(2,1)S(1)} collective-permute-done((bf16[128,4096]{1,0:T(8,128)(2,1)S(1)}, bf16[128,4096]{1,0:T(8,128)(2,1)S(1)}, u32[]{:S(2)}, u32[]{:S(2)}) %collective-permute-start.2) | collective-permute-done | bytes 1048608 | tf_op jit(solution)/shard_map/ppermute | solution.py:19
  77.6 1.0 %collective-permute-done.3.refs_3_ = bf16[128,4096]{1,0:T(8,128)(2,1)S(1)} collective-permute-done((bf16[128,4096]{1,0:T(8,128)(2,1)}, bf16[128,4096]{1,0:T(8,128)(2,1)S(1)}, u32[]{:S(2)}, u32[]{:S(2)}) %collective-permute-start.3) | collective-permute-done | bytes 1048608 | tf_op jit(solution)/shard_map/ppermute | solution.py:19
  78.6 0.9 copy-done.3
  79.5 18.2 %shard_map.56 = bf16[128,4096]{1,0:T(8,128)(2,1)} custom-call(s32[1]{0:T(128)} %bitcast.core_ref, bf16[128,4096]{1,0:T(8,128)(2,1)} %copy-done.1, bf16[128,4096]{1,0:T(8,128)(2,1)} %copy-done.2, bf16[128,4096]{1,0:T(8,128)(2,1)} %collective-permute-done.refs_2_, bf16[128,4096]{1,0:T(8,128)(2,1)} %copy-done.3, ...), custom_call_target="tpu_custom_call" | custom-call | tf_op jit(solution)/shard_map/pallas_call | solution.py:143
  (19 shorter events, 0.1 us)
Async XLA Ops:
  22.7 7.3 %copy-start = (bf16[128,4096]{1,0:T(8,128)(2,1)}, bf16[128,4096]{1,0:T(8,128)(2,1)S(1)}, u32[]{:S(2)}) copy-start(bf16[128,4096]{1,0:T(8,128)(2,1)S(1)} %multiply_convert_fusion.g_ref) | copy-start | bytes 3145732
  22.7 5.3 %copy-start.4 = (s32[128]{0:T(128)S(1)}, s32[128]{0:T(128)}, u32[]{:S(2)}) copy-start(s32[128]{0:T(128)} %param.11) | copy-start | bytes 1540
  22.7 38.4 %collective-permute-start.1 = (bf16[128,4096]{1,0:T(8,128)(2,1)S(1)}, bf16[128,4096]{1,0:T(8,128)(2,1)S(1)}, u32[]{:S(2)}, u32[]{:S(2)}) collective-permute-start(bf16[128,4096]{1,0:T(8,128)(2,1)S(1)} %multiply_convert_fusion.g_ref), channel_id=1, source_target_pairs={{0,4},{1,5},{2,6},{3,7},{4,8},{5,9},{6,10},{7,11},{8,12},{9,13},{1... | collective-permute-start | bytes 3145736 | tf_op jit(solution)/shard_map/ppermute | solution.py:14
  24.1 47.9 %collective-permute-start = (bf16[128,4096]{1,0:T(8,128)(2,1)S(1)}, bf16[128,4096]{1,0:T(8,128)(2,1)}, u32[]{:S(2)}, u32[]{:S(2)}) collective-permute-start(bf16[128,4096]{1,0:T(8,128)(2,1)S(1)} %multiply_convert_fusion.g_ref), channel_id=1, source_target_pairs={{0,2},{1,3},{2,4},{3,5},{4,6},{5,7},{6,8},{7,9},{8,10},{9,11},{10,... | collective-permute-start | bytes 3145736 | tf_op jit(solution)/shard_map/ppermute | solution.py:14
  61.1 17.5 %copy-start.1 = (bf16[128,4096]{1,0:T(8,128)(2,1)}, bf16[128,4096]{1,0:T(8,128)(2,1)S(1)}, u32[]{:S(2)}) copy-start(bf16[128,4096]{1,0:T(8,128)(2,1)S(1)} %collective-permute-done.1.refs_0_) | copy-start | bytes 3145732
  72.1 5.5 %collective-permute-start.2 = (bf16[128,4096]{1,0:T(8,128)(2,1)S(1)}, bf16[128,4096]{1,0:T(8,128)(2,1)S(1)}, u32[]{:S(2)}, u32[]{:S(2)}) collective-permute-start(bf16[128,4096]{1,0:T(8,128)(2,1)S(1)} %broadcast_select_fusion), channel_id=1, source_target_pairs={{0,1},{1,0},{2,3},{3,2},{4,5},{5,4},{6,7},{7,6},{8,9},{9,8},{10,11... | collective-permute-start | bytes 3145736 | tf_op jit(solution)/shard_map/ppermute | solution.py:19
  74.6 4.0 %collective-permute-start.3 = (bf16[128,4096]{1,0:T(8,128)(2,1)}, bf16[128,4096]{1,0:T(8,128)(2,1)S(1)}, u32[]{:S(2)}, u32[]{:S(2)}) collective-permute-start(bf16[128,4096]{1,0:T(8,128)(2,1)} %collective-permute-done.refs_2_), channel_id=1, source_target_pairs={{0,1},{1,0},{2,3},{3,2},{4,5},{5,4},{6,7},{7,6},{8,9},{9,8},{10,11... | collective-permute-start | bytes 3145736 | tf_op jit(solution)/shard_map/ppermute | solution.py:19
  77.6 1.0 %copy-start.2 = (bf16[128,4096]{1,0:T(8,128)(2,1)}, bf16[128,4096]{1,0:T(8,128)(2,1)S(1)}, u32[]{:S(2)}) copy-start(bf16[128,4096]{1,0:T(8,128)(2,1)S(1)} %collective-permute-done.2.refs_1_) | copy-start | bytes 3145732
  78.6 0.9 copy-start.3

commit v10 on v9

--- a/solution.py
+++ b/solution.py
@@ -54,7 +54,7 @@
 
 def conv_kernel(core_ref, *refs, lags, rows, group_size):
     g_refs = list(refs[:lags])
-    w_ref, a_ref, q_ref, o_ref, rhs_ref = refs[lags:]
+    own_ref, w_ref, a_ref, q_ref, o_ref, rhs_ref = refs[lags:]
     lane_chunk = rhs_ref.shape[1]
     per_chunk = lane_chunk // group_size
     owner = lax.broadcasted_iota(jnp.int32, (rows, lane_chunk), 1) // group_size
@@ -62,6 +62,7 @@
     for u in range(q_ref.shape[1] // lane_chunk):
         lanes = slice(lane_chunk * u, lane_chunk * (u + 1))
         blocks = [g[:, lanes] for g in g_refs]
+        blocks[lags - 3] = jnp.where(even, blocks[lags - 3], own_ref[:, lanes])
         near, far = blocks[lags - 1], blocks[lags - 3]
         blocks[lags - 1] = jnp.where(even, near, far)
         blocks[lags - 3] = jnp.where(even, far, near)
@@ -136,8 +137,10 @@
     )(padded, mask, gated)
     weights, own_term, two_back, four_back = lax.optimization_barrier((weights, own_term, two_back, four_back))
     swap_a = swapped(two_back, "ctx")
-    swap_b = swapped(jnp.where(core == 1, four_back, gated), "ctx")
-    sources = [four_back, swap_b, two_back, swap_a]
+    pairs = [(source, source ^ 1) for source in range(ctx_count)]
+    sibling_own = lax.ppermute(gated, "ctx", [(s, d) for s, d in pairs if s % 2 == 0])
+    sibling_four = lax.ppermute(four_back, "ctx", [(s, d) for s, d in pairs if s % 2 == 1])
+    sources = [four_back, sibling_four, two_back, swap_a, sibling_own]
     kernel = functools.partial(conv_kernel, lags=lags, rows=rows, group_size=group_size)
     block = pl.BlockSpec((rows, step_lanes), lambda j, c: (0, j))
     return pl.pallas_call(
@@ -145,7 +148,7 @@
         grid_spec=pltpu.PrefetchScalarGridSpec(
             num_scalar_prefetch=1,
             grid=(channels // step_lanes,),
-            in_specs=[block] * lags
+            in_specs=[block] * (lags + 1)
             + [
                 pl.BlockSpec((lags, rows, step_filters * rows), lambda j, c: (0, 0, j)),
                 block,

time: 98.1 us -> 98.9 us (level)
  starting transfers between devices: 6.51 us -> 9.4 us
    ppermute x0 -> x2, starting transfers between devices: none -> 5.49 us  [the longest x1 4.07 us: shards(): lax.ppermute(four_back, 'ctx', [(s, d) for s, d in pairs if s % 2 == 1])]
    ppermute x2 -> x1, starting transfers between devices: 2.54 us -> 0.07 us  [swapped(): lax.ppermute(value, axis, [(source, source ^ 1) for source in range(count)])]
    ppermute x0 -> x2, waiting for transfers between devices: none -> 2.31 us  [the longest x1 2.3 us: shards(): lax.ppermute(four_back, 'ctx', [(s, d) for s, d in pairs if s % 2 == 1])]
    ppermute x2 -> x1, waiting for transfers between devices: 3.92 us -> 1.63 us  [swapped(): lax.ppermute(value, axis, [(source, source ^ 1) for source in range(count)])]
  transfers between devices with their start and end apart: 4 -> 5, of which waited for: 3 -> 3; matrix products, arithmetic and copies ran while one was open for 3% -> 3% of each run, Pallas kernels for 32% -> 32%
where the time goes in v10:
time: 98.9 us; the launch traced here: 98.6 us
  Pallas kernels  49.2 us (50%)
  blocking collectives  18.2 us (18%)
  waiting for transfers between devices  14 us (14%)
  starting transfers between devices  9.4 us (10%)
  other arithmetic  6.45 us (7%)
  local copies, waits for them, and re-layouts  1.13 us (1%)
    pallas_call x1, Pallas kernels, shards(): pl.pallas_call(functools.partial(weight_kernel, lags=lags, rows=rows, gro...  31.1 us
    all_gather x1, blocking collectives, shards(): packed = lax.all_gather(packed, 'ctx', axis=0, tiled=False)  18.2 us
    pallas_call x1, Pallas kernels, shards(): pl.pallas_call(kernel, grid_spec=pltpu.PrefetchScalarGridSpec(num_scalar_...  18.1 us
    ppermute x2, waiting for transfers between devices, shifted(): lax.ppermute(value, axis, [(source, source + steps) for source in range(f...  10 us
    ppermute x1, starting transfers between devices, shards(): lax.ppermute(four_back, 'ctx', [(s, d) for s, d in pairs if s % 2 == 1])  4.07 us
    ppermute x2, starting transfers between devices, shifted(): lax.ppermute(value, axis, [(source, source + steps) for source in range(f...  3.84 us
    ppermute x1, waiting for transfers between devices, shards(): lax.ppermute(four_back, 'ctx', [(s, d) for s, d in pairs if s % 2 == 1])  2.3 us
  transfers between devices with their start and end apart: 5, of which 3 were waited for; matrix products, arithmetic and copies ran while one was open for 3% of the time, Pallas kernels for 32%

profile of v10, /device:TPU:25, one launch (start us, length us, event | category | flops | bytes accessed | tf_op | source)
XLA Modules:
  0.0 98.6 jit_solution(6335574834827090836)
XLA Ops:
  0.0 0.6 compare_reduce_fusion
  0.6 1.3 %fusion.3 = bf16[1,128]{1,0:T(2,128)(2,1)S(1)} fusion(pred[]{:T(512)} %compare_reduce_fusion, s32[128]{0:T(128)} %param.11), kind=kLoop, calls=%fused_computation.21 | loop fusion | flops 256 | bytes 769 | tf_op jit(solution)/shard_map/reshape.29
  1.9 0.7 fusion.2
  2.7 18.2 %all-gather.1 = bf16[16,33,256]{2,1,0:T(8,128)(2,1)S(1)} all-gather(bf16[1,33,256]{2,1,0:T(8,128)(2,1)S(1)} %fusion.2), channel_id=2, replica_groups=mesh['dp'=2,'ctx'=16] {'ctx'}, dimensions={0}, use_global_device_ids=true | all-gather | bytes 287232 | tf_op jit(solution)/shard_map/all_gather | solution.py:93
  20.9 1.8 %multiply_convert_fusion.g_ref = bf16[128,4096]{1,0:T(8,128)(2,1)S(1)} fusion(bf16[128,4096]{1,0:T(8,128)(2,1)} %param.9, bf16[128,4096]{1,0:T(8,128)(2,1)} %param.8), kind=kLoop, calls=%fused_computation | loop fusion | flops 2097152 | bytes 3145728 | tf_op jit(solution)/shard_map/convert_element_type | solution.py:97
  22.7 0.0 copy-start
  22.7 0.0 copy-start.3
  22.7 1.4 %collective-permute-start.4 = (bf16[128,4096]{1,0:T(8,128)(2,1)S(1)}, bf16[128,4096]{1,0:T(8,128)(2,1)S(1)}, u32[]{:S(2)}, u32[]{:S(2)}) collective-permute-start(bf16[128,4096]{1,0:T(8,128)(2,1)S(1)} %multiply_convert_fusion.g_ref), channel_id=1, source_target_pairs={{0,1},{2,3},{4,5},{6,7},{8,9},{10,11},{12,13},{14,15},{16,17},{18,... | collective-permute-start | bytes 3145736 | tf_op jit(solution)/shard_map/ppermute | solution.py:141
  24.1 1.3 %collective-permute-start.1 = (bf16[128,4096]{1,0:T(8,128)(2,1)S(1)}, bf16[128,4096]{1,0:T(8,128)(2,1)}, u32[]{:S(2)}, u32[]{:S(2)}) collective-permute-start(bf16[128,4096]{1,0:T(8,128)(2,1)S(1)} %multiply_convert_fusion.g_ref), channel_id=1, source_target_pairs={{0,4},{1,5},{2,6},{3,7},{4,8},{5,9},{6,10},{7,11},{8,12},{9,13},{1... | collective-permute-start | bytes 3145736 | tf_op jit(solution)/shard_map/ppermute | solution.py:14
  25.4 2.5 %collective-permute-start = (bf16[128,4096]{1,0:T(8,128)(2,1)S(1)}, bf16[128,4096]{1,0:T(8,128)(2,1)}, u32[]{:S(2)}, u32[]{:S(2)}) collective-permute-start(bf16[128,4096]{1,0:T(8,128)(2,1)S(1)} %multiply_convert_fusion.g_ref), channel_id=1, source_target_pairs={{0,2},{1,3},{2,4},{3,5},{4,6},{5,7},{6,8},{7,9},{8,10},{9,11},{10,... | collective-permute-start | bytes 3145736 | tf_op jit(solution)/shard_map/ppermute | solution.py:14
  28.0 0.1 bitcast_convert_fusion
  28.1 0.1 pad.7.clone
  28.2 0.2 copy.8
  28.4 0.8 rev.3
  29.3 0.8 compare_convert_fusion.m_ref
  30.1 1.1 %maximum_maximum_fusion.p_ref = f32[256,768]{1,0:T(8,128)} fusion(f32[256,512]{1,0:T(8,128)S(1)} %rev.3, f32[768]{0:T(1024)S(1)} %pad.7.clone, f32[768]{0:T(1024)S(1)} %pad.5.clone), kind=kLoop, calls=%fused_computation.1 | loop fusion | flops 393216 | bytes 1316864 | tf_op jit(solution)/shard_map/concatenate | solution.py:98
  31.2 31.1 %shard_map.55 = (bf16[4,128,32768]{2,1,0:T(8,128)(2,1)}, f32[128,4096]{1,0:T(8,128)}) custom-call(f32[256,768]{1,0:T(8,128)} %maximum_maximum_fusion.p_ref, f32[128,640]{1,0:T(8,128)} %compare_convert_fusion.m_ref, bf16[128,4096]{1,0:T(8,128)(2,1)} %copy-done), custom_call_target="tpu_custom_call" | custom-call | tf_op jit(solution)/shard_map/pallas_call | solution.py:117
  62.3 0.0 collective-permute-done.1.refs_0_
  62.3 10.0 %collective-permute-done.refs_2_ = bf16[128,4096]{1,0:T(8,128)(2,1)} collective-permute-done((bf16[128,4096]{1,0:T(8,128)(2,1)S(1)}, bf16[128,4096]{1,0:T(8,128)(2,1)}, u32[]{:S(2)}, u32[]{:S(2)}) %collective-permute-start) | collective-permute-done | bytes 1048608 | tf_op jit(solution)/shard_map/ppermute | solution.py:14
  72.4 4.1 %collective-permute-start.2 = (bf16[128,4096]{1,0:T(8,128)(2,1)}, bf16[128,4096]{1,0:T(8,128)(2,1)S(1)}, u32[]{:S(2)}, u32[]{:S(2)}) collective-permute-start(bf16[128,4096]{1,0:T(8,128)(2,1)} %collective-permute-done.1.refs_0_), channel_id=1, source_target_pairs={{1,0},{3,2},{5,4},{7,6},{9,8},{11,10},{13,12},{15,14},{17,16},{19,... | collective-permute-start | bytes 3145736 | tf_op jit(solution)/shard_map/ppermute | solution.py:142
  76.5 0.1 collective-permute-start.3
  76.6 2.3 %collective-permute-done.2.refs_1_ = bf16[128,4096]{1,0:T(8,128)(2,1)S(1)} collective-permute-done((bf16[128,4096]{1,0:T(8,128)(2,1)}, bf16[128,4096]{1,0:T(8,128)(2,1)S(1)}, u32[]{:S(2)}, u32[]{:S(2)}) %collective-permute-start.2) | collective-permute-done | bytes 1048608 | tf_op jit(solution)/shard_map/ppermute | solution.py:142
  78.9 1.6 %collective-permute-done.3.refs_3_ = bf16[128,4096]{1,0:T(8,128)(2,1)} collective-permute-done((bf16[128,4096]{1,0:T(8,128)(2,1)}, bf16[128,4096]{1,0:T(8,128)(2,1)}, u32[]{:S(2)}, u32[]{:S(2)}) %collective-permute-start.3) | collective-permute-done | bytes 1048608 | tf_op jit(solution)/shard_map/ppermute | solution.py:19
  80.5 18.1 %shard_map.56 = bf16[128,4096]{1,0:T(8,128)(2,1)} custom-call(s32[1]{0:T(128)} %bitcast.core_ref, bf16[128,4096]{1,0:T(8,128)(2,1)} %collective-permute-done.1.refs_0_, bf16[128,4096]{1,0:T(8,128)(2,1)} %copy-done.2, bf16[128,4096]{1,0:T(8,128)(2,1)} %collective-permute-done.refs_2_, bf16[128,4096]{1,0:T(8,128)(2,1)} %collective-permute-done.3.refs_3_, ...), custom_call_target="tpu_custom_call" | custom-call | tf_op jit(solution)/shard_map/pallas_call | solution.py:146
  (18 shorter events, 0.1 us)
Async XLA Ops:
  22.7 8.6 %copy-start = (bf16[128,4096]{1,0:T(8,128)(2,1)}, bf16[128,4096]{1,0:T(8,128)(2,1)S(1)}, u32[]{:S(2)}) copy-start(bf16[128,4096]{1,0:T(8,128)(2,1)S(1)} %multiply_convert_fusion.g_ref) | copy-start | bytes 3145732
  22.7 6.6 %copy-start.3 = (s32[128]{0:T(128)S(1)}, s32[128]{0:T(128)}, u32[]{:S(2)}) copy-start(s32[128]{0:T(128)} %param.11) | copy-start | bytes 1540
  22.7 53.9 %collective-permute-start.4 = (bf16[128,4096]{1,0:T(8,128)(2,1)S(1)}, bf16[128,4096]{1,0:T(8,128)(2,1)S(1)}, u32[]{:S(2)}, u32[]{:S(2)}) collective-permute-start(bf16[128,4096]{1,0:T(8,128)(2,1)S(1)} %multiply_convert_fusion.g_ref), channel_id=1, source_target_pairs={{0,1},{2,3},{4,5},{6,7},{8,9},{10,11},{12,13},{14,15},{16,17},{18,... | collective-permute-start | bytes 3145736 | tf_op jit(solution)/shard_map/ppermute | solution.py:141
  24.1 38.2 %collective-permute-start.1 = (bf16[128,4096]{1,0:T(8,128)(2,1)S(1)}, bf16[128,4096]{1,0:T(8,128)(2,1)}, u32[]{:S(2)}, u32[]{:S(2)}) collective-permute-start(bf16[128,4096]{1,0:T(8,128)(2,1)S(1)} %multiply_convert_fusion.g_ref), channel_id=1, source_target_pairs={{0,4},{1,5},{2,6},{3,7},{4,8},{5,9},{6,10},{7,11},{8,12},{9,13},{1... | collective-permute-start | bytes 3145736 | tf_op jit(solution)/shard_map/ppermute | solution.py:14
  25.4 47.0 %collective-permute-start = (bf16[128,4096]{1,0:T(8,128)(2,1)S(1)}, bf16[128,4096]{1,0:T(8,128)(2,1)}, u32[]{:S(2)}, u32[]{:S(2)}) collective-permute-start(bf16[128,4096]{1,0:T(8,128)(2,1)S(1)} %multiply_convert_fusion.g_ref), channel_id=1, source_target_pairs={{0,2},{1,3},{2,4},{3,5},{4,6},{5,7},{6,8},{7,9},{8,10},{9,11},{10,... | collective-permute-start | bytes 3145736 | tf_op jit(solution)/shard_map/ppermute | solution.py:14
  72.4 6.5 %collective-permute-start.2 = (bf16[128,4096]{1,0:T(8,128)(2,1)}, bf16[128,4096]{1,0:T(8,128)(2,1)S(1)}, u32[]{:S(2)}, u32[]{:S(2)}) collective-permute-start(bf16[128,4096]{1,0:T(8,128)(2,1)} %collective-permute-done.1.refs_0_), channel_id=1, source_target_pairs={{1,0},{3,2},{5,4},{7,6},{9,8},{11,10},{13,12},{15,14},{17,16},{19,... | collective-permute-start | bytes 3145736 | tf_op jit(solution)/shard_map/ppermute | solution.py:142
  76.5 4.0 %collective-permute-start.3 = (bf16[128,4096]{1,0:T(8,128)(2,1)}, bf16[128,4096]{1,0:T(8,128)(2,1)}, u32[]{:S(2)}, u32[]{:S(2)}) collective-permute-start(bf16[128,4096]{1,0:T(8,128)(2,1)} %collective-permute-done.refs_2_), channel_id=1, source_target_pairs={{0,1},{1,0},{2,3},{3,2},{4,5},{5,4},{6,7},{7,6},{8,9},{9,8},{10,11... | collective-permute-start | bytes 3145736 | tf_op jit(solution)/shard_map/ppermute | solution.py:19
  76.6 3.9 %copy-start.1 = (bf16[128,4096]{1,0:T(8,128)(2,1)}, bf16[128,4096]{1,0:T(8,128)(2,1)S(1)}, u32[]{:S(2)}) copy-start(bf16[128,4096]{1,0:T(8,128)(2,1)S(1)} %collective-permute-done.4.refs_4_) | copy-start | bytes 3145732
  78.9 1.6 %copy-start.2 = (bf16[128,4096]{1,0:T(8,128)(2,1)}, bf16[128,4096]{1,0:T(8,128)(2,1)S(1)}, u32[]{:S(2)}) copy-start(bf16[128,4096]{1,0:T(8,128)(2,1)S(1)} %collective-permute-done.2.refs_1_) | copy-start | bytes 3145732

commit v11 on v9

--- a/solution.py
+++ b/solution.py
@@ -17,6 +17,21 @@
 def swapped(value, axis):
     count = lax.axis_size(axis)
     return lax.ppermute(value, axis, [(source, source ^ 1) for source in range(count)])
+
+
+def gathered(value, axis):
+    count = lax.axis_size(axis)
+    if count & (count - 1):
+        return lax.all_gather(value, axis, axis=0, tiled=False)
+    index = lax.axis_index(axis)
+    blocks = value[None]
+    step = 1
+    while step < count:
+        received = lax.ppermute(blocks, axis, [(s, s ^ step) for s in range(count)])
+        later = (index & step) != 0
+        blocks = jnp.where(later, jnp.concatenate([received, blocks]), jnp.concatenate([blocks, received]))
+        step *= 2
+    return blocks
 
 
 def weight_kernel(p_ref, m_ref, g_ref, w_ref, a_ref, lhs_ref, rhs_ref, *, lags, rows, group_size):
@@ -89,7 +104,7 @@
     lags = filt_len // rows
     seg_row = jnp.zeros((1, filters), jnp.bfloat16).at[0, :rows].set(segment_ids.astype(jnp.bfloat16))
     packed = jnp.concatenate([taps, seg_row], axis=0)
-    packed = lax.all_gather(packed, "ctx", axis=0, tiled=False)
+    packed = gathered(packed, "ctx")
     packed, keys, values = lax.optimization_barrier((packed, keys, values))
     all_taps = packed[:, :tap_rows].reshape(filt_len, filters).astype(jnp.float32)
     all_segs = packed[:, tap_rows, :rows].astype(jnp.int32)

time: 98.1 us -> 97.4 us (level)
  blocking collectives: 18.2 us -> 0 us
  waiting for transfers between devices: 14.8 us -> 27.7 us
  starting transfers between devices: 6.51 us -> 11.1 us
    all_gather x1 -> x0, blocking collectives: 18.2 us -> none  [shards(): packed = lax.all_gather(packed, 'ctx', axis=0, tiled=False)]
    ppermute x0 -> x4, waiting for transfers between devices: none -> 14.4 us  [gathered(): received = lax.ppermute(blocks, axis, [(s, s ^ step) for s in range(count)])]
    ppermute x0 -> x4, starting transfers between devices: none -> 2.34 us  [gathered(): received = lax.ppermute(blocks, axis, [(s, s ^ step) for s in range(count)])]
    ppermute x2, starting transfers between devices: 2.54 us -> 4.2 us  [swapped(): lax.ppermute(value, axis, [(source, source ^ 1) for source in range(count)])]
    ppermute x2, waiting for transfers between devices: 10.9 us -> 9.41 us  [shifted(): lax.ppermute(value, axis, [(source, source + steps) for source in range(f...]
  transfers between devices with their start and end apart: 4 -> 8, of which waited for: 3 -> 7; matrix products, arithmetic and copies ran while one was open for 3% -> 3% of each run, Pallas kernels for 32% -> 32%
where the time goes in v11:
time: 97.4 us; the launch traced here: 97.1 us
  Pallas kernels  49.3 us (51%)
  waiting for transfers between devices  27.7 us (28%)
  starting transfers between devices  11.1 us (11%)
  other arithmetic  6.72 us (7%)
  local copies, waits for them, and re-layouts  2.07 us (2%)
    pallas_call x1, Pallas kernels, shards(): pl.pallas_call(functools.partial(weight_kernel, lags=lags, rows=rows, gro...  31.1 us
    pallas_call x1, Pallas kernels, shards(): pl.pallas_call(kernel, grid_spec=pltpu.PrefetchScalarGridSpec(num_scalar_...  18.2 us
    ppermute x4, waiting for transfers between devices, gathered(): received = lax.ppermute(blocks, axis, [(s, s ^ step) for s in range(count)])  14.4 us
    ppermute x2, waiting for transfers between devices, shifted(): lax.ppermute(value, axis, [(source, source + steps) for source in range(f...  9.41 us
    ppermute x2, starting transfers between devices, shifted(): lax.ppermute(value, axis, [(source, source + steps) for source in range(f...  4.57 us
    ppermute x2, starting transfers between devices, swapped(): lax.ppermute(value, axis, [(source, source ^ 1) for source in range(count)])  4.2 us
    ppermute x2, waiting for transfers between devices, swapped(): lax.ppermute(value, axis, [(source, source ^ 1) for source in range(count)])  3.92 us
    ppermute x4, starting transfers between devices, gathered(): received = lax.ppermute(blocks, axis, [(s, s ^ step) for s in range(count)])  2.34 us
  transfers between devices with their start and end apart: 8, of which 7 were waited for; matrix products, arithmetic and copies ran while one was open for 3% of the time, Pallas kernels for 32%

profile of v11, /device:TPU:25, one launch (start us, length us, event | category | flops | bytes accessed | tf_op | source)
XLA Modules:
  0.0 97.1 jit_solution(15319028281783654981)
XLA Ops:
  0.0 0.6 compare_reduce_fusion
  0.6 1.3 %fusion.3 = bf16[1,128]{1,0:T(2,128)(2,1)S(1)} fusion(pred[]{:T(512)} %compare_reduce_fusion, s32[128]{0:T(128)} %param.11), kind=kLoop, calls=%fused_computation.26 | loop fusion | flops 256 | bytes 769 | tf_op jit(solution)/shard_map/reshape.29
  1.9 0.7 fusion.2
  2.7 0.7 collective-permute-start
  3.3 0.8 collective-permute-done
  4.2 1.3 %collective-permute-start.1 = (bf16[2,33,256]{2,1,0:T(8,128)(2,1)S(1)}, bf16[2,33,256]{2,1,0:T(8,128)(2,1)S(1)}, u32[]{:S(2)}, u32[]{:S(2)}) collective-permute-start(bf16[2,33,256]{2,1,0:T(8,128)(2,1)S(1)} %maximum_select_fusion.3), channel_id=1, source_target_pairs={{0,2},{1,3},{2,0},{3,1},{4,6},{5,7},{6,4},{7,5},{8,10},{9,11},{10,... | collective-permute-start | bytes 101384 | tf_op jit(solution)/shard_map/ppermute | solution.py:30
  5.5 1.6 %collective-permute-done.1 = bf16[2,33,256]{2,1,0:T(8,128)(2,1)S(1)} collective-permute-done((bf16[2,33,256]{2,1,0:T(8,128)(2,1)S(1)}, bf16[2,33,256]{2,1,0:T(8,128)(2,1)S(1)}, u32[]{:S(2)}, u32[]{:S(2)}) %collective-permute-start.1) | collective-permute-done | bytes 33824 | tf_op jit(solution)/shard_map/ppermute | solution.py:30
  7.1 0.2 collective-permute-start.2
  7.4 3.1 %collective-permute-done.2 = bf16[4,33,256]{2,1,0:T(8,128)(2,1)S(1)} collective-permute-done((bf16[4,33,256]{2,1,0:T(8,128)(2,1)S(1)}, bf16[4,33,256]{2,1,0:T(8,128)(2,1)S(1)}, u32[]{:S(2)}, u32[]{:S(2)}) %collective-permute-start.2) | collective-permute-done | bytes 67616 | tf_op jit(solution)/shard_map/ppermute | solution.py:30
  10.8 8.8 %collective-permute-done.3 = bf16[8,33,256]{2,1,0:T(8,128)(2,1)S(1)} collective-permute-done((bf16[8,33,256]{2,1,0:T(8,128)(2,1)S(1)}, bf16[8,33,256]{2,1,0:T(8,128)(2,1)S(1)}, u32[]{:S(2)}, u32[]{:S(2)}) %collective-permute-start.3) | collective-permute-done | bytes 135200 | tf_op jit(solution)/shard_map/ppermute | solution.py:30
  19.6 1.8 %multiply_convert_fusion.g_ref = bf16[128,4096]{1,0:T(8,128)(2,1)S(1)} fusion(bf16[128,4096]{1,0:T(8,128)(2,1)} %param.9, bf16[128,4096]{1,0:T(8,128)(2,1)} %param.8), kind=kLoop, calls=%fused_computation | loop fusion | flops 2097152 | bytes 3145728 | tf_op jit(solution)/shard_map/convert_element_type | solution.py:111
  21.4 1.4 %collective-permute-start.5 = (bf16[128,4096]{1,0:T(8,128)(2,1)S(1)}, bf16[128,4096]{1,0:T(8,128)(2,1)S(1)}, u32[]{:S(2)}, u32[]{:S(2)}) collective-permute-start(bf16[128,4096]{1,0:T(8,128)(2,1)S(1)} %multiply_convert_fusion.g_ref), channel_id=1, source_target_pairs={{0,4},{1,5},{2,6},{3,7},{4,8},{5,9},{6,10},{7,11},{8,12},{9,13},{1... | collective-permute-start | bytes 3145736 | tf_op jit(solution)/shard_map/ppermute | solution.py:14
  22.9 3.1 %collective-permute-start.4 = (bf16[128,4096]{1,0:T(8,128)(2,1)S(1)}, bf16[128,4096]{1,0:T(8,128)(2,1)}, u32[]{:S(2)}, u32[]{:S(2)}) collective-permute-start(bf16[128,4096]{1,0:T(8,128)(2,1)S(1)} %multiply_convert_fusion.g_ref), channel_id=1, source_target_pairs={{0,2},{1,3},{2,4},{3,5},{4,6},{5,7},{6,8},{7,9},{8,10},{9,11},{10,... | collective-permute-start | bytes 3145736 | tf_op jit(solution)/shard_map/ppermute | solution.py:14
  26.1 0.2 copy.7
  26.3 0.8 rev.3
  27.2 0.8 compare_convert_fusion.m_ref
  28.0 1.2 %maximum_maximum_fusion.p_ref = f32[256,768]{1,0:T(8,128)} fusion(f32[256,512]{1,0:T(8,128)S(1)} %rev.3, f32[768]{0:T(1024)S(1)} %pad.7.clone, f32[768]{0:T(1024)S(1)} %pad.5.clone), kind=kLoop, calls=%fused_computation.2 | loop fusion | flops 393216 | bytes 1316864 | tf_op jit(solution)/shard_map/concatenate | solution.py:112
  29.2 31.1 %shard_map.55 = (bf16[4,128,32768]{2,1,0:T(8,128)(2,1)}, f32[128,4096]{1,0:T(8,128)}) custom-call(f32[256,768]{1,0:T(8,128)} %maximum_maximum_fusion.p_ref, f32[128,640]{1,0:T(8,128)} %compare_convert_fusion.m_ref, bf16[128,4096]{1,0:T(8,128)(2,1)} %copy-done), custom_call_target="tpu_custom_call" | custom-call | tf_op jit(solution)/shard_map/pallas_call | solution.py:131
  60.3 9.4 %collective-permute-done.4.refs_2_ = bf16[128,4096]{1,0:T(8,128)(2,1)} collective-permute-done((bf16[128,4096]{1,0:T(8,128)(2,1)S(1)}, bf16[128,4096]{1,0:T(8,128)(2,1)}, u32[]{:S(2)}, u32[]{:S(2)}) %collective-permute-start.4) | collective-permute-done | bytes 1048608 | tf_op jit(solution)/shard_map/ppermute | solution.py:14
  69.9 4.1 %collective-permute-start.6 = (bf16[128,4096]{1,0:T(8,128)(2,1)S(1)}, bf16[128,4096]{1,0:T(8,128)(2,1)S(1)}, u32[]{:S(2)}, u32[]{:S(2)}) collective-permute-start(bf16[128,4096]{1,0:T(8,128)(2,1)S(1)} %broadcast_select_fusion), channel_id=1, source_target_pairs={{0,1},{1,0},{2,3},{3,2},{4,5},{5,4},{6,7},{7,6},{8,9},{9,8},{10,11... | collective-permute-start | bytes 3145736 | tf_op jit(solution)/shard_map/ppermute | solution.py:19
  74.1 2.9 %collective-permute-done.6.refs_1_ = bf16[128,4096]{1,0:T(8,128)(2,1)S(1)} collective-permute-done((bf16[128,4096]{1,0:T(8,128)(2,1)S(1)}, bf16[128,4096]{1,0:T(8,128)(2,1)S(1)}, u32[]{:S(2)}, u32[]{:S(2)}) %collective-permute-start.6) | collective-permute-done | bytes 1048608 | tf_op jit(solution)/shard_map/ppermute | solution.py:19
  77.0 1.0 %collective-permute-done.7.refs_3_ = bf16[128,4096]{1,0:T(8,128)(2,1)S(1)} collective-permute-done((bf16[128,4096]{1,0:T(8,128)(2,1)}, bf16[128,4096]{1,0:T(8,128)(2,1)S(1)}, u32[]{:S(2)}, u32[]{:S(2)}) %collective-permute-start.7) | collective-permute-done | bytes 1048608 | tf_op jit(solution)/shard_map/ppermute | solution.py:19
  78.0 0.9 copy-done.3
  78.9 18.2 %shard_map.56 = bf16[128,4096]{1,0:T(8,128)(2,1)} custom-call(s32[1]{0:T(128)} %bitcast.core_ref, bf16[128,4096]{1,0:T(8,128)(2,1)} %copy-done.1, bf16[128,4096]{1,0:T(8,128)(2,1)} %copy-done.2, bf16[128,4096]{1,0:T(8,128)(2,1)} %collective-permute-done.4.refs_2_, bf16[128,4096]{1,0:T(8,128)(2,1)} %copy-done.3, ...), custom_call_target="tpu_custom_call" | custom-call | tf_op jit(solution)/shard_map/pallas_call | solution.py:158
  (30 shorter events, 0.6 us)
Async XLA Ops:
  2.7 1.5 %collective-permute-start = (bf16[1,33,256]{2,1,0:T(8,128)(2,1)S(1)}, bf16[1,33,256]{2,1,0:T(8,128)(2,1)S(1)}, u32[]{:S(2)}, u32[]{:S(2)}) collective-permute-start(bf16[1,33,256]{2,1,0:T(8,128)(2,1)S(1)} %fusion.2), channel_id=1, source_target_pairs={{0,1},{1,0},{2,3},{3,2},{4,5},{5,4},{6,7},{7,6},{8,9},{9,8},{10,11... | collective-permute-start | bytes 50696 | tf_op jit(solution)/shard_map/ppermute | solution.py:30
  4.2 2.9 %collective-permute-start.1 = (bf16[2,33,256]{2,1,0:T(8,128)(2,1)S(1)}, bf16[2,33,256]{2,1,0:T(8,128)(2,1)S(1)}, u32[]{:S(2)}, u32[]{:S(2)}) collective-permute-start(bf16[2,33,256]{2,1,0:T(8,128)(2,1)S(1)} %maximum_select_fusion.3), channel_id=1, source_target_pairs={{0,2},{1,3},{2,0},{3,1},{4,6},{5,7},{6,4},{7,5},{8,10},{9,11},{10,... | collective-permute-start | bytes 101384 | tf_op jit(solution)/shard_map/ppermute | solution.py:30
  7.1 3.4 %collective-permute-start.2 = (bf16[4,33,256]{2,1,0:T(8,128)(2,1)S(1)}, bf16[4,33,256]{2,1,0:T(8,128)(2,1)S(1)}, u32[]{:S(2)}, u32[]{:S(2)}) collective-permute-start(bf16[4,33,256]{2,1,0:T(8,128)(2,1)S(1)} %maximum_select_fusion.2), channel_id=1, source_target_pairs={{0,4},{1,5},{2,6},{3,7},{4,0},{5,1},{6,2},{7,3},{8,12},{9,13},{10,... | collective-permute-start | bytes 202760 | tf_op jit(solution)/shard_map/ppermute | solution.py:30
  10.5 9.1 %collective-permute-start.3 = (bf16[8,33,256]{2,1,0:T(8,128)(2,1)S(1)}, bf16[8,33,256]{2,1,0:T(8,128)(2,1)S(1)}, u32[]{:S(2)}, u32[]{:S(2)}) collective-permute-start(bf16[8,33,256]{2,1,0:T(8,128)(2,1)S(1)} %maximum_select_fusion.1), channel_id=1, source_target_pairs={{0,8},{1,9},{2,10},{3,11},{4,12},{5,13},{6,14},{7,15},{8,0},{9,1},... | collective-permute-start | bytes 405512 | tf_op jit(solution)/shard_map/ppermute | solution.py:30
  21.4 7.8 %copy-start = (bf16[128,4096]{1,0:T(8,128)(2,1)}, bf16[128,4096]{1,0:T(8,128)(2,1)S(1)}, u32[]{:S(2)}) copy-start(bf16[128,4096]{1,0:T(8,128)(2,1)S(1)} %multiply_convert_fusion.g_ref) | copy-start | bytes 3145732
  21.4 5.8 %copy-start.4 = (s32[128]{0:T(128)S(1)}, s32[128]{0:T(128)}, u32[]{:S(2)}) copy-start(s32[128]{0:T(128)} %param.11) | copy-start | bytes 1540
  21.4 38.9 %collective-permute-start.5 = (bf16[128,4096]{1,0:T(8,128)(2,1)S(1)}, bf16[128,4096]{1,0:T(8,128)(2,1)S(1)}, u32[]{:S(2)}, u32[]{:S(2)}) collective-permute-start(bf16[128,4096]{1,0:T(8,128)(2,1)S(1)} %multiply_convert_fusion.g_ref), channel_id=1, source_target_pairs={{0,4},{1,5},{2,6},{3,7},{4,8},{5,9},{6,10},{7,11},{8,12},{9,13},{1... | collective-permute-start | bytes 3145736 | tf_op jit(solution)/shard_map/ppermute | solution.py:14
  22.9 46.9 %collective-permute-start.4 = (bf16[128,4096]{1,0:T(8,128)(2,1)S(1)}, bf16[128,4096]{1,0:T(8,128)(2,1)}, u32[]{:S(2)}, u32[]{:S(2)}) collective-permute-start(bf16[128,4096]{1,0:T(8,128)(2,1)S(1)} %multiply_convert_fusion.g_ref), channel_id=1, source_target_pairs={{0,2},{1,3},{2,4},{3,5},{4,6},{5,7},{6,8},{7,9},{8,10},{9,11},{10,... | collective-permute-start | bytes 3145736 | tf_op jit(solution)/shard_map/ppermute | solution.py:14
  60.3 17.6 %copy-start.1 = (bf16[128,4096]{1,0:T(8,128)(2,1)}, bf16[128,4096]{1,0:T(8,128)(2,1)S(1)}, u32[]{:S(2)}) copy-start(bf16[128,4096]{1,0:T(8,128)(2,1)S(1)} %collective-permute-done.5.refs_0_) | copy-start | bytes 3145732
  69.9 7.1 %collective-permute-start.6 = (bf16[128,4096]{1,0:T(8,128)(2,1)S(1)}, bf16[128,4096]{1,0:T(8,128)(2,1)S(1)}, u32[]{:S(2)}, u32[]{:S(2)}) collective-permute-start(bf16[128,4096]{1,0:T(8,128)(2,1)S(1)} %broadcast_select_fusion), channel_id=1, source_target_pairs={{0,1},{1,0},{2,3},{3,2},{4,5},{5,4},{6,7},{7,6},{8,9},{9,8},{10,11... | collective-permute-start | bytes 3145736 | tf_op jit(solution)/shard_map/ppermute | solution.py:19
  74.0 4.0 %collective-permute-start.7 = (bf16[128,4096]{1,0:T(8,128)(2,1)}, bf16[128,4096]{1,0:T(8,128)(2,1)S(1)}, u32[]{:S(2)}, u32[]{:S(2)}) collective-permute-start(bf16[128,4096]{1,0:T(8,128)(2,1)} %collective-permute-done.4.refs_2_), channel_id=1, source_target_pairs={{0,1},{1,0},{2,3},{3,2},{4,5},{5,4},{6,7},{7,6},{8,9},{9,8},{10,11... | collective-permute-start | bytes 3145736 | tf_op jit(solution)/shard_map/ppermute | solution.py:19
  77.0 1.0 %copy-start.2 = (bf16[128,4096]{1,0:T(8,128)(2,1)}, bf16[128,4096]{1,0:T(8,128)(2,1)S(1)}, u32[]{:S(2)}) copy-start(bf16[128,4096]{1,0:T(8,128)(2,1)S(1)} %collective-permute-done.6.refs_1_) | copy-start | bytes 3145732
  78.0 0.9 copy-start.3

commit v12 on v11

--- a/solution.py
+++ b/solution.py
@@ -104,11 +104,11 @@
     lags = filt_len // rows
     seg_row = jnp.zeros((1, filters), jnp.bfloat16).at[0, :rows].set(segment_ids.astype(jnp.bfloat16))
     packed = jnp.concatenate([taps, seg_row], axis=0)
+    gated = (keys.astype(jnp.float32) * values.astype(jnp.float32)).astype(jnp.bfloat16)
     packed = gathered(packed, "ctx")
-    packed, keys, values = lax.optimization_barrier((packed, keys, values))
+    packed, gated = lax.optimization_barrier((packed, gated))
     all_taps = packed[:, :tap_rows].reshape(filt_len, filters).astype(jnp.float32)
     all_segs = packed[:, tap_rows, :rows].astype(jnp.int32)
-    gated = (keys.astype(jnp.float32) * values.astype(jnp.float32)).astype(jnp.bfloat16)
     padded = jnp.concatenate(
         [
             jnp.zeros((filters, rows + 1), jnp.float32),

time: 97.4 us -> 95.5 us (0.980)
  waiting for transfers between devices: 27.7 us -> 25.9 us
    ppermute x4, waiting for transfers between devices: 14.4 us -> 12.6 us  [gathered(): received = lax.ppermute(blocks, axis, [(s, s ^ step) for s in range(count)])]
  transfers between devices with their start and end apart: 8 -> 8, of which waited for: 7 -> 7; matrix products, arithmetic and copies ran while one was open for 3% -> 5% of each run, Pallas kernels for 32% -> 33%
where the time goes in v12:
time: 95.5 us; the launch traced here: 95.2 us
  Pallas kernels  49.3 us (52%)
  waiting for transfers between devices  25.9 us (27%)
  starting transfers between devices  11 us (12%)
  other arithmetic  6.72 us (7%)
  local copies, waits for them, and re-layouts  2.07 us (2%)
    pallas_call x1, Pallas kernels, shards(): pl.pallas_call(functools.partial(weight_kernel, lags=lags, rows=rows, gro...  31.1 us
    pallas_call x1, Pallas kernels, shards(): pl.pallas_call(kernel, grid_spec=pltpu.PrefetchScalarGridSpec(num_scalar_...  18.2 us
    ppermute x4, waiting for transfers between devices, gathered(): received = lax.ppermute(blocks, axis, [(s, s ^ step) for s in range(count)])  12.6 us
    ppermute x2, waiting for transfers between devices, shifted(): lax.ppermute(value, axis, [(source, source + steps) for source in range(f...  9.41 us
    ppermute x2, starting transfers between devices, shifted(): lax.ppermute(value, axis, [(source, source + steps) for source in range(f...  4.44 us
    ppermute x2, starting transfers between devices, swapped(): lax.ppermute(value, axis, [(source, source ^ 1) for source in range(count)])  4.2 us
    ppermute x2, waiting for transfers between devices, swapped(): lax.ppermute(value, axis, [(source, source ^ 1) for source in range(count)])  3.92 us
    ppermute x4, starting transfers between devices, gathered(): received = lax.ppermute(blocks, axis, [(s, s ^ step) for s in range(count)])  2.34 us
  transfers between devices with their start and end apart: 8, of which 7 were waited for; matrix products, arithmetic and copies ran while one was open for 5% of the time, Pallas kernels for 33%

profile of v12, /device:TPU:25, one launch (start us, length us, event | category | flops | bytes accessed | tf_op | source)
XLA Modules:
  0.0 95.2 jit_solution(14837695679055812742)
XLA Ops:
  0.0 0.6 compare_reduce_fusion
  0.6 1.3 %fusion.3 = bf16[1,128]{1,0:T(2,128)(2,1)S(1)} fusion(pred[]{:T(512)} %compare_reduce_fusion, s32[128]{0:T(128)} %param.11), kind=kLoop, calls=%fused_computation.26 | loop fusion | flops 256 | bytes 769 | tf_op jit(solution)/shard_map/reshape.29
  1.9 0.7 fusion.2
  2.7 0.7 collective-permute-start
  3.3 0.8 collective-permute-done
  4.2 1.3 %collective-permute-start.1 = (bf16[2,33,256]{2,1,0:T(8,128)(2,1)S(1)}, bf16[2,33,256]{2,1,0:T(8,128)(2,1)S(1)}, u32[]{:S(2)}, u32[]{:S(2)}) collective-permute-start(bf16[2,33,256]{2,1,0:T(8,128)(2,1)S(1)} %maximum_select_fusion.3), channel_id=1, source_target_pairs={{0,2},{1,3},{2,0},{3,1},{4,6},{5,7},{6,4},{7,5},{8,10},{9,11},{10,... | collective-permute-start | bytes 101384 | tf_op jit(solution)/shard_map/ppermute | solution.py:30
  5.5 1.6 %collective-permute-done.1 = bf16[2,33,256]{2,1,0:T(8,128)(2,1)S(1)} collective-permute-done((bf16[2,33,256]{2,1,0:T(8,128)(2,1)S(1)}, bf16[2,33,256]{2,1,0:T(8,128)(2,1)S(1)}, u32[]{:S(2)}, u32[]{:S(2)}) %collective-permute-start.1) | collective-permute-done | bytes 33824 | tf_op jit(solution)/shard_map/ppermute | solution.py:30
  7.1 0.2 collective-permute-start.2
  7.4 3.1 %collective-permute-done.2 = bf16[4,33,256]{2,1,0:T(8,128)(2,1)S(1)} collective-permute-done((bf16[4,33,256]{2,1,0:T(8,128)(2,1)S(1)}, bf16[4,33,256]{2,1,0:T(8,128)(2,1)S(1)}, u32[]{:S(2)}, u32[]{:S(2)}) %collective-permute-start.2) | collective-permute-done | bytes 67616 | tf_op jit(solution)/shard_map/ppermute | solution.py:30
  10.6 1.8 %multiply_convert_fusion.g_ref = bf16[128,4096]{1,0:T(8,128)(2,1)S(1)} fusion(bf16[128,4096]{1,0:T(8,128)(2,1)} %param.9, bf16[128,4096]{1,0:T(8,128)(2,1)} %param.8), kind=kLoop, calls=%fused_computation | loop fusion | flops 2097152 | bytes 3145728 | tf_op jit(solution)/shard_map/convert_element_type | solution.py:107
  12.6 7.0 %collective-permute-done.3 = bf16[8,33,256]{2,1,0:T(8,128)(2,1)S(1)} collective-permute-done((bf16[8,33,256]{2,1,0:T(8,128)(2,1)S(1)}, bf16[8,33,256]{2,1,0:T(8,128)(2,1)S(1)}, u32[]{:S(2)}, u32[]{:S(2)}) %collective-permute-start.3) | collective-permute-done | bytes 135200 | tf_op jit(solution)/shard_map/ppermute | solution.py:30
  19.6 1.3 %collective-permute-start.5 = (bf16[128,4096]{1,0:T(8,128)(2,1)S(1)}, bf16[128,4096]{1,0:T(8,128)(2,1)S(1)}, u32[]{:S(2)}, u32[]{:S(2)}) collective-permute-start(bf16[128,4096]{1,0:T(8,128)(2,1)S(1)} %multiply_convert_fusion.g_ref), channel_id=1, source_target_pairs={{0,4},{1,5},{2,6},{3,7},{4,8},{5,9},{6,10},{7,11},{8,12},{9,13},{1... | collective-permute-start | bytes 3145736 | tf_op jit(solution)/shard_map/ppermute | solution.py:14
  20.9 3.1 %collective-permute-start.4 = (bf16[128,4096]{1,0:T(8,128)(2,1)S(1)}, bf16[128,4096]{1,0:T(8,128)(2,1)}, u32[]{:S(2)}, u32[]{:S(2)}) collective-permute-start(bf16[128,4096]{1,0:T(8,128)(2,1)S(1)} %multiply_convert_fusion.g_ref), channel_id=1, source_target_pairs={{0,2},{1,3},{2,4},{3,5},{4,6},{5,7},{6,8},{7,9},{8,10},{9,11},{10,... | collective-permute-start | bytes 3145736 | tf_op jit(solution)/shard_map/ppermute | solution.py:14
  24.2 0.2 copy.7
  24.4 0.8 rev.3
  25.3 0.8 compare_convert_fusion.m_ref
  26.1 1.2 %maximum_maximum_fusion.p_ref = f32[256,768]{1,0:T(8,128)} fusion(f32[256,512]{1,0:T(8,128)S(1)} %rev.3, f32[768]{0:T(1024)S(1)} %pad.7.clone, f32[768]{0:T(1024)S(1)} %pad.5.clone), kind=kLoop, calls=%fused_computation.2 | loop fusion | flops 393216 | bytes 1316864 | tf_op jit(solution)/shard_map/concatenate | solution.py:112
  27.3 31.1 %shard_map.55 = (bf16[4,128,32768]{2,1,0:T(8,128)(2,1)}, f32[128,4096]{1,0:T(8,128)}) custom-call(f32[256,768]{1,0:T(8,128)} %maximum_maximum_fusion.p_ref, f32[128,640]{1,0:T(8,128)} %compare_convert_fusion.m_ref, bf16[128,4096]{1,0:T(8,128)(2,1)} %copy-done), custom_call_target="tpu_custom_call" | custom-call | tf_op jit(solution)/shard_map/pallas_call | solution.py:131
  58.4 9.4 %collective-permute-done.4.refs_2_ = bf16[128,4096]{1,0:T(8,128)(2,1)} collective-permute-done((bf16[128,4096]{1,0:T(8,128)(2,1)S(1)}, bf16[128,4096]{1,0:T(8,128)(2,1)}, u32[]{:S(2)}, u32[]{:S(2)}) %collective-permute-start.4) | collective-permute-done | bytes 1048608 | tf_op jit(solution)/shard_map/ppermute | solution.py:14
  67.9 4.1 %collective-permute-start.6 = (bf16[128,4096]{1,0:T(8,128)(2,1)S(1)}, bf16[128,4096]{1,0:T(8,128)(2,1)S(1)}, u32[]{:S(2)}, u32[]{:S(2)}) collective-permute-start(bf16[128,4096]{1,0:T(8,128)(2,1)S(1)} %broadcast_select_fusion), channel_id=1, source_target_pairs={{0,1},{1,0},{2,3},{3,2},{4,5},{5,4},{6,7},{7,6},{8,9},{9,8},{10,11... | collective-permute-start | bytes 3145736 | tf_op jit(solution)/shard_map/ppermute | solution.py:19
  72.1 2.9 %collective-permute-done.6.refs_1_ = bf16[128,4096]{1,0:T(8,128)(2,1)S(1)} collective-permute-done((bf16[128,4096]{1,0:T(8,128)(2,1)S(1)}, bf16[128,4096]{1,0:T(8,128)(2,1)S(1)}, u32[]{:S(2)}, u32[]{:S(2)}) %collective-permute-start.6) | collective-permute-done | bytes 1048608 | tf_op jit(solution)/shard_map/ppermute | solution.py:19
  75.0 1.0 %collective-permute-done.7.refs_3_ = bf16[128,4096]{1,0:T(8,128)(2,1)S(1)} collective-permute-done((bf16[128,4096]{1,0:T(8,128)(2,1)}, bf16[128,4096]{1,0:T(8,128)(2,1)S(1)}, u32[]{:S(2)}, u32[]{:S(2)}) %collective-permute-start.7) | collective-permute-done | bytes 1048608 | tf_op jit(solution)/shard_map/ppermute | solution.py:19
  76.0 0.9 copy-done.3
  77.0 18.2 %shard_map.56 = bf16[128,4096]{1,0:T(8,128)(2,1)} custom-call(s32[1]{0:T(128)} %bitcast.core_ref, bf16[128,4096]{1,0:T(8,128)(2,1)} %copy-done.1, bf16[128,4096]{1,0:T(8,128)(2,1)} %copy-done.2, bf16[128,4096]{1,0:T(8,128)(2,1)} %collective-permute-done.4.refs_2_, bf16[128,4096]{1,0:T(8,128)(2,1)} %copy-done.3, ...), custom_call_target="tpu_custom_call" | custom-call | tf_op jit(solution)/shard_map/pallas_call | solution.py:158
  (30 shorter events, 0.6 us)
Async XLA Ops:
  2.7 1.5 %collective-permute-start = (bf16[1,33,256]{2,1,0:T(8,128)(2,1)S(1)}, bf16[1,33,256]{2,1,0:T(8,128)(2,1)S(1)}, u32[]{:S(2)}, u32[]{:S(2)}) collective-permute-start(bf16[1,33,256]{2,1,0:T(8,128)(2,1)S(1)} %fusion.2), channel_id=1, source_target_pairs={{0,1},{1,0},{2,3},{3,2},{4,5},{5,4},{6,7},{7,6},{8,9},{9,8},{10,11... | collective-permute-start | bytes 50696 | tf_op jit(solution)/shard_map/ppermute | solution.py:30
  4.2 2.9 %collective-permute-start.1 = (bf16[2,33,256]{2,1,0:T(8,128)(2,1)S(1)}, bf16[2,33,256]{2,1,0:T(8,128)(2,1)S(1)}, u32[]{:S(2)}, u32[]{:S(2)}) collective-permute-start(bf16[2,33,256]{2,1,0:T(8,128)(2,1)S(1)} %maximum_select_fusion.3), channel_id=1, source_target_pairs={{0,2},{1,3},{2,0},{3,1},{4,6},{5,7},{6,4},{7,5},{8,10},{9,11},{10,... | collective-permute-start | bytes 101384 | tf_op jit(solution)/shard_map/ppermute | solution.py:30
  7.1 3.4 %collective-permute-start.2 = (bf16[4,33,256]{2,1,0:T(8,128)(2,1)S(1)}, bf16[4,33,256]{2,1,0:T(8,128)(2,1)S(1)}, u32[]{:S(2)}, u32[]{:S(2)}) collective-permute-start(bf16[4,33,256]{2,1,0:T(8,128)(2,1)S(1)} %maximum_select_fusion.2), channel_id=1, source_target_pairs={{0,4},{1,5},{2,6},{3,7},{4,0},{5,1},{6,2},{7,3},{8,12},{9,13},{10,... | collective-permute-start | bytes 202760 | tf_op jit(solution)/shard_map/ppermute | solution.py:30
  10.5 9.1 %collective-permute-start.3 = (bf16[8,33,256]{2,1,0:T(8,128)(2,1)S(1)}, bf16[8,33,256]{2,1,0:T(8,128)(2,1)S(1)}, u32[]{:S(2)}, u32[]{:S(2)}) collective-permute-start(bf16[8,33,256]{2,1,0:T(8,128)(2,1)S(1)} %maximum_select_fusion.1), channel_id=1, source_target_pairs={{0,8},{1,9},{2,10},{3,11},{4,12},{5,13},{6,14},{7,15},{8,0},{9,1},... | collective-permute-start | bytes 405512 | tf_op jit(solution)/shard_map/ppermute | solution.py:30
  12.4 14.8 %copy-start = (bf16[128,4096]{1,0:T(8,128)(2,1)}, bf16[128,4096]{1,0:T(8,128)(2,1)S(1)}, u32[]{:S(2)}) copy-start(bf16[128,4096]{1,0:T(8,128)(2,1)S(1)} %multiply_convert_fusion.g_ref) | copy-start | bytes 3145732
  12.4 12.8 %copy-start.4 = (s32[128]{0:T(128)S(1)}, s32[128]{0:T(128)}, u32[]{:S(2)}) copy-start(s32[128]{0:T(128)} %param.11) | copy-start | bytes 1540
  19.6 38.8 %collective-permute-start.5 = (bf16[128,4096]{1,0:T(8,128)(2,1)S(1)}, bf16[128,4096]{1,0:T(8,128)(2,1)S(1)}, u32[]{:S(2)}, u32[]{:S(2)}) collective-permute-start(bf16[128,4096]{1,0:T(8,128)(2,1)S(1)} %multiply_convert_fusion.g_ref), channel_id=1, source_target_pairs={{0,4},{1,5},{2,6},{3,7},{4,8},{5,9},{6,10},{7,11},{8,12},{9,13},{1... | collective-permute-start | bytes 3145736 | tf_op jit(solution)/shard_map/ppermute | solution.py:14
  20.9 46.9 %collective-permute-start.4 = (bf16[128,4096]{1,0:T(8,128)(2,1)S(1)}, bf16[128,4096]{1,0:T(8,128)(2,1)}, u32[]{:S(2)}, u32[]{:S(2)}) collective-permute-start(bf16[128,4096]{1,0:T(8,128)(2,1)S(1)} %multiply_convert_fusion.g_ref), channel_id=1, source_target_pairs={{0,2},{1,3},{2,4},{3,5},{4,6},{5,7},{6,8},{7,9},{8,10},{9,11},{10,... | collective-permute-start | bytes 3145736 | tf_op jit(solution)/shard_map/ppermute | solution.py:14
  58.4 17.6 %copy-start.1 = (bf16[128,4096]{1,0:T(8,128)(2,1)}, bf16[128,4096]{1,0:T(8,128)(2,1)S(1)}, u32[]{:S(2)}) copy-start(bf16[128,4096]{1,0:T(8,128)(2,1)S(1)} %collective-permute-done.5.refs_0_) | copy-start | bytes 3145732
  67.9 7.1 %collective-permute-start.6 = (bf16[128,4096]{1,0:T(8,128)(2,1)S(1)}, bf16[128,4096]{1,0:T(8,128)(2,1)S(1)}, u32[]{:S(2)}, u32[]{:S(2)}) collective-permute-start(bf16[128,4096]{1,0:T(8,128)(2,1)S(1)} %broadcast_select_fusion), channel_id=1, source_target_pairs={{0,1},{1,0},{2,3},{3,2},{4,5},{5,4},{6,7},{7,6},{8,9},{9,8},{10,11... | collective-permute-start | bytes 3145736 | tf_op jit(solution)/shard_map/ppermute | solution.py:19
  72.0 4.0 %collective-permute-start.7 = (bf16[128,4096]{1,0:T(8,128)(2,1)}, bf16[128,4096]{1,0:T(8,128)(2,1)S(1)}, u32[]{:S(2)}, u32[]{:S(2)}) collective-permute-start(bf16[128,4096]{1,0:T(8,128)(2,1)} %collective-permute-done.4.refs_2_), channel_id=1, source_target_pairs={{0,1},{1,0},{2,3},{3,2},{4,5},{5,4},{6,7},{7,6},{8,9},{9,8},{10,11... | collective-permute-start | bytes 3145736 | tf_op jit(solution)/shard_map/ppermute | solution.py:19
  75.0 1.0 %copy-start.2 = (bf16[128,4096]{1,0:T(8,128)(2,1)}, bf16[128,4096]{1,0:T(8,128)(2,1)S(1)}, u32[]{:S(2)}) copy-start(bf16[128,4096]{1,0:T(8,128)(2,1)S(1)} %collective-permute-done.6.refs_1_) | copy-start | bytes 3145732
  76.0 0.9 copy-start.3

commit v13 on v12

--- a/solution.py
+++ b/solution.py
@@ -25,13 +25,16 @@
         return lax.all_gather(value, axis, axis=0, tiled=False)
     index = lax.axis_index(axis)
     blocks = value[None]
-    step = 1
-    while step < count:
+    step = count // 2
+    while step >= 1:
         received = lax.ppermute(blocks, axis, [(s, s ^ step) for s in range(count)])
         later = (index & step) != 0
         blocks = jnp.where(later, jnp.concatenate([received, blocks]), jnp.concatenate([blocks, received]))
-        step *= 2
-    return blocks
+        step //= 2
+    rounds = count.bit_length() - 1
+    blocks = blocks.reshape((2,) * rounds + value.shape)
+    blocks = blocks.transpose(tuple(range(rounds))[::-1] + tuple(range(rounds, rounds + value.ndim)))
+    return blocks.reshape((count,) + value.shape)
 
 
 def weight_kernel(p_ref, m_ref, g_ref, w_ref, a_ref, lhs_ref, rhs_ref, *, lags, rows, group_size):

time: 95.5 us -> 94.7 us (level)
  waiting for transfers between devices: 25.9 us -> 23.8 us
  starting transfers between devices: 11 us -> 12.3 us
    ppermute x4, waiting for transfers between devices: 12.6 us -> 8.42 us  [gathered(): received = lax.ppermute(blocks, axis, [(s, s ^ step) for s in range(count)])]
    ppermute x4, starting transfers between devices: 2.34 us -> 5.68 us  [gathered(): received = lax.ppermute(blocks, axis, [(s, s ^ step) for s in range(count)])]
    ppermute x2, waiting for transfers between devices: 9.41 us -> 11.4 us  [shifted(): lax.ppermute(value, axis, [(source, source + steps) for source in range(f...]
    ppermute x2, starting transfers between devices: 4.2 us -> 2.16 us  [swapped(): lax.ppermute(value, axis, [(source, source ^ 1) for source in range(count)])]
  transfers between devices with their start and end apart: 8 -> 8, of which waited for: 7 -> 6; matrix products, arithmetic and copies ran while one was open for 5% -> 5% of each run, Pallas kernels for 33% -> 33%
where the time goes in v13:
time: 94.7 us; the launch traced here: 94.4 us
  Pallas kernels  49.3 us (52%)
  waiting for transfers between devices  23.8 us (25%)
  starting transfers between devices  12.3 us (13%)
  other arithmetic  6.72 us (7%)
  local copies, waits for them, and re-layouts  2.09 us (2%)
    pallas_call x1, Pallas kernels, shards(): pl.pallas_call(functools.partial(weight_kernel, lags=lags, rows=rows, gro...  31.1 us
    pallas_call x1, Pallas kernels, shards(): pl.pallas_call(kernel, grid_spec=pltpu.PrefetchScalarGridSpec(num_scalar_...  18.2 us
    ppermute x2, waiting for transfers between devices, shifted(): lax.ppermute(value, axis, [(source, source + steps) for source in range(f...  11.4 us
    ppermute x4, waiting for transfers between devices, gathered(): received = lax.ppermute(blocks, axis, [(s, s ^ step) for s in range(count)])  8.42 us
    ppermute x4, starting transfers between devices, gathered(): received = lax.ppermute(blocks, axis, [(s, s ^ step) for s in range(count)])  5.68 us
    ppermute x2, starting transfers between devices, shifted(): lax.ppermute(value, axis, [(source, source + steps) for source in range(f...  4.44 us
    ppermute x2, waiting for transfers between devices, swapped(): lax.ppermute(value, axis, [(source, source ^ 1) for source in range(count)])  3.92 us
    ppermute x2, starting transfers between devices, swapped(): lax.ppermute(value, axis, [(source, source ^ 1) for source in range(count)])  2.16 us
  transfers between devices with their start and end apart: 8, of which 6 were waited for; matrix products, arithmetic and copies ran while one was open for 5% of the time, Pallas kernels for 33%

profile of v13, /device:TPU:25, one launch (start us, length us, event | category | flops | bytes accessed | tf_op | source)
XLA Modules:
  0.0 94.4 jit_solution(4032462656252654683)
XLA Ops:
  0.0 0.6 compare_reduce_fusion
  0.6 1.3 %fusion.3 = bf16[1,128]{1,0:T(2,128)(2,1)S(1)} fusion(pred[]{:T(512)} %compare_reduce_fusion, s32[128]{0:T(128)} %param.11), kind=kLoop, calls=%fused_computation.26 | loop fusion | flops 256 | bytes 769 | tf_op jit(solution)/shard_map/reshape.31
  1.9 0.7 fusion.2
  2.7 3.6 %collective-permute-done = bf16[1,33,256]{2,1,0:T(8,128)(2,1)S(1)} collective-permute-done((bf16[1,33,256]{2,1,0:T(8,128)(2,1)S(1)}, bf16[1,33,256]{2,1,0:T(8,128)(2,1)S(1)}, u32[]{:S(2)}, u32[]{:S(2)}) %collective-permute-start) | collective-permute-done | bytes 16928 | tf_op jit(solution)/shard_map/ppermute | solution.py:30
  6.3 0.1 collective-permute-start.1
  6.5 2.8 %collective-permute-done.1 = bf16[2,33,256]{2,1,0:T(8,128)(2,1)S(1)} collective-permute-done((bf16[2,33,256]{2,1,0:T(8,128)(2,1)S(1)}, bf16[2,33,256]{2,1,0:T(8,128)(2,1)S(1)}, u32[]{:S(2)}, u32[]{:S(2)}) %collective-permute-start.1) | collective-permute-done | bytes 33824 | tf_op jit(solution)/shard_map/ppermute | solution.py:30
  9.3 1.3 %collective-permute-start.2 = (bf16[4,33,256]{2,1,0:T(8,128)(2,1)S(1)}, bf16[4,33,256]{2,1,0:T(8,128)(2,1)S(1)}, u32[]{:S(2)}, u32[]{:S(2)}) collective-permute-start(bf16[4,33,256]{2,1,0:T(8,128)(2,1)S(1)} %maximum_select_fusion.2), channel_id=1, source_target_pairs={{0,2},{1,3},{2,0},{3,1},{4,6},{5,7},{6,4},{7,5},{8,10},{9,11},{10,... | collective-permute-start | bytes 202760 | tf_op jit(solution)/shard_map/ppermute | solution.py:30
  10.6 2.1 %collective-permute-done.2 = bf16[4,33,256]{2,1,0:T(8,128)(2,1)S(1)} collective-permute-done((bf16[4,33,256]{2,1,0:T(8,128)(2,1)S(1)}, bf16[4,33,256]{2,1,0:T(8,128)(2,1)S(1)}, u32[]{:S(2)}, u32[]{:S(2)}) %collective-permute-start.2) | collective-permute-done | bytes 67616 | tf_op jit(solution)/shard_map/ppermute | solution.py:30
  12.6 4.2 %collective-permute-start.3 = (bf16[8,33,256]{2,1,0:T(8,128)(2,1)S(1)}, bf16[8,33,256]{2,1,0:T(8,128)(2,1)S(1)}, u32[]{:S(2)}, u32[]{:S(2)}) collective-permute-start(bf16[8,33,256]{2,1,0:T(8,128)(2,1)S(1)} %maximum_select_fusion.1), channel_id=1, source_target_pairs={{0,1},{1,0},{2,3},{3,2},{4,5},{5,4},{6,7},{7,6},{8,9},{9,8},{10,11... | collective-permute-start | bytes 405512 | tf_op jit(solution)/shard_map/ppermute | solution.py:30
  16.8 1.8 %multiply_convert_fusion.g_ref = bf16[128,4096]{1,0:T(8,128)(2,1)S(1)} fusion(bf16[128,4096]{1,0:T(8,128)(2,1)} %param.9, bf16[128,4096]{1,0:T(8,128)(2,1)} %param.8), kind=kLoop, calls=%fused_computation | loop fusion | flops 2097152 | bytes 3145728 | tf_op jit(solution)/shard_map/convert_element_type | solution.py:110
  18.9 1.3 %collective-permute-start.5 = (bf16[128,4096]{1,0:T(8,128)(2,1)S(1)}, bf16[128,4096]{1,0:T(8,128)(2,1)S(1)}, u32[]{:S(2)}, u32[]{:S(2)}) collective-permute-start(bf16[128,4096]{1,0:T(8,128)(2,1)S(1)} %multiply_convert_fusion.g_ref), channel_id=1, source_target_pairs={{0,4},{1,5},{2,6},{3,7},{4,8},{5,9},{6,10},{7,11},{8,12},{9,13},{1... | collective-permute-start | bytes 3145736 | tf_op jit(solution)/shard_map/ppermute | solution.py:14
  20.2 3.1 %collective-permute-start.4 = (bf16[128,4096]{1,0:T(8,128)(2,1)S(1)}, bf16[128,4096]{1,0:T(8,128)(2,1)}, u32[]{:S(2)}, u32[]{:S(2)}) collective-permute-start(bf16[128,4096]{1,0:T(8,128)(2,1)S(1)} %multiply_convert_fusion.g_ref), channel_id=1, source_target_pairs={{0,2},{1,3},{2,4},{3,5},{4,6},{5,7},{6,8},{7,9},{8,10},{9,11},{10,... | collective-permute-start | bytes 3145736 | tf_op jit(solution)/shard_map/ppermute | solution.py:14
  23.4 0.2 copy.9
  23.6 0.8 rev.3
  24.5 0.8 compare_convert_fusion.m_ref
  25.3 1.2 %maximum_maximum_fusion.p_ref = f32[256,768]{1,0:T(8,128)} fusion(f32[256,512]{1,0:T(8,128)S(1)} %rev.3, f32[768]{0:T(1024)S(1)} %pad.7.clone, f32[768]{0:T(1024)S(1)} %pad.5.clone), kind=kLoop, calls=%fused_computation.2 | loop fusion | flops 393216 | bytes 1316864 | tf_op jit(solution)/shard_map/concatenate | solution.py:115
  26.5 31.1 %shard_map.55 = (bf16[4,128,32768]{2,1,0:T(8,128)(2,1)}, f32[128,4096]{1,0:T(8,128)}) custom-call(f32[256,768]{1,0:T(8,128)} %maximum_maximum_fusion.p_ref, f32[128,640]{1,0:T(8,128)} %compare_convert_fusion.m_ref, bf16[128,4096]{1,0:T(8,128)(2,1)} %copy-done), custom_call_target="tpu_custom_call" | custom-call | tf_op jit(solution)/shard_map/pallas_call | solution.py:134
  57.6 11.4 %collective-permute-done.4.refs_2_ = bf16[128,4096]{1,0:T(8,128)(2,1)} collective-permute-done((bf16[128,4096]{1,0:T(8,128)(2,1)S(1)}, bf16[128,4096]{1,0:T(8,128)(2,1)}, u32[]{:S(2)}, u32[]{:S(2)}) %collective-permute-start.4) | collective-permute-done | bytes 1048608 | tf_op jit(solution)/shard_map/ppermute | solution.py:14
  69.1 0.1 broadcast_select_fusion
  69.2 2.1 %collective-permute-start.6 = (bf16[128,4096]{1,0:T(8,128)(2,1)S(1)}, bf16[128,4096]{1,0:T(8,128)(2,1)S(1)}, u32[]{:S(2)}, u32[]{:S(2)}) collective-permute-start(bf16[128,4096]{1,0:T(8,128)(2,1)S(1)} %broadcast_select_fusion), channel_id=1, source_target_pairs={{0,1},{1,0},{2,3},{3,2},{4,5},{5,4},{6,7},{7,6},{8,9},{9,8},{10,11... | collective-permute-start | bytes 3145736 | tf_op jit(solution)/shard_map/ppermute | solution.py:19
  71.4 2.9 %collective-permute-done.6.refs_1_ = bf16[128,4096]{1,0:T(8,128)(2,1)S(1)} collective-permute-done((bf16[128,4096]{1,0:T(8,128)(2,1)S(1)}, bf16[128,4096]{1,0:T(8,128)(2,1)S(1)}, u32[]{:S(2)}, u32[]{:S(2)}) %collective-permute-start.6) | collective-permute-done | bytes 1048608 | tf_op jit(solution)/shard_map/ppermute | solution.py:19
  74.3 1.0 %collective-permute-done.7.refs_3_ = bf16[128,4096]{1,0:T(8,128)(2,1)S(1)} collective-permute-done((bf16[128,4096]{1,0:T(8,128)(2,1)}, bf16[128,4096]{1,0:T(8,128)(2,1)S(1)}, u32[]{:S(2)}, u32[]{:S(2)}) %collective-permute-start.7) | collective-permute-done | bytes 1048608 | tf_op jit(solution)/shard_map/ppermute | solution.py:19
  75.3 0.9 copy-done.3
  76.2 18.2 %shard_map.56 = bf16[128,4096]{1,0:T(8,128)(2,1)} custom-call(s32[1]{0:T(128)} %bitcast.core_ref, bf16[128,4096]{1,0:T(8,128)(2,1)} %copy-done.1, bf16[128,4096]{1,0:T(8,128)(2,1)} %copy-done.2, bf16[128,4096]{1,0:T(8,128)(2,1)} %collective-permute-done.4.refs_2_, bf16[128,4096]{1,0:T(8,128)(2,1)} %copy-done.3, ...), custom_call_target="tpu_custom_call" | custom-call | tf_op jit(solution)/shard_map/pallas_call | solution.py:161
  (31 shorter events, 0.5 us)
Async XLA Ops:
  2.7 3.6 %collective-permute-start = (bf16[1,33,256]{2,1,0:T(8,128)(2,1)S(1)}, bf16[1,33,256]{2,1,0:T(8,128)(2,1)S(1)}, u32[]{:S(2)}, u32[]{:S(2)}) collective-permute-start(bf16[1,33,256]{2,1,0:T(8,128)(2,1)S(1)} %fusion.2), channel_id=1, source_target_pairs={{0,8},{1,9},{2,10},{3,11},{4,12},{5,13},{6,14},{7,15},{8,0},{9,1},... | collective-permute-start | bytes 50696 | tf_op jit(solution)/shard_map/ppermute | solution.py:30
  6.3 2.9 %collective-permute-start.1 = (bf16[2,33,256]{2,1,0:T(8,128)(2,1)S(1)}, bf16[2,33,256]{2,1,0:T(8,128)(2,1)S(1)}, u32[]{:S(2)}, u32[]{:S(2)}) collective-permute-start(bf16[2,33,256]{2,1,0:T(8,128)(2,1)S(1)} %maximum_select_fusion.3), channel_id=1, source_target_pairs={{0,4},{1,5},{2,6},{3,7},{4,0},{5,1},{6,2},{7,3},{8,12},{9,13},{10,... | collective-permute-start | bytes 101384 | tf_op jit(solution)/shard_map/ppermute | solution.py:30
  9.3 3.4 %collective-permute-start.2 = (bf16[4,33,256]{2,1,0:T(8,128)(2,1)S(1)}, bf16[4,33,256]{2,1,0:T(8,128)(2,1)S(1)}, u32[]{:S(2)}, u32[]{:S(2)}) collective-permute-start(bf16[4,33,256]{2,1,0:T(8,128)(2,1)S(1)} %maximum_select_fusion.2), channel_id=1, source_target_pairs={{0,2},{1,3},{2,0},{3,1},{4,6},{5,7},{6,4},{7,5},{8,10},{9,11},{10,... | collective-permute-start | bytes 202760 | tf_op jit(solution)/shard_map/ppermute | solution.py:30
  12.6 6.1 %collective-permute-start.3 = (bf16[8,33,256]{2,1,0:T(8,128)(2,1)S(1)}, bf16[8,33,256]{2,1,0:T(8,128)(2,1)S(1)}, u32[]{:S(2)}, u32[]{:S(2)}) collective-permute-start(bf16[8,33,256]{2,1,0:T(8,128)(2,1)S(1)} %maximum_select_fusion.1), channel_id=1, source_target_pairs={{0,1},{1,0},{2,3},{3,2},{4,5},{5,4},{6,7},{7,6},{8,9},{9,8},{10,11... | collective-permute-start | bytes 405512 | tf_op jit(solution)/shard_map/ppermute | solution.py:30
  18.6 7.9 %copy-start = (bf16[128,4096]{1,0:T(8,128)(2,1)}, bf16[128,4096]{1,0:T(8,128)(2,1)S(1)}, u32[]{:S(2)}) copy-start(bf16[128,4096]{1,0:T(8,128)(2,1)S(1)} %multiply_convert_fusion.g_ref) | copy-start | bytes 3145732
  18.8 5.7 %copy-start.4 = (s32[128]{0:T(128)S(1)}, s32[128]{0:T(128)}, u32[]{:S(2)}) copy-start(s32[128]{0:T(128)} %param.11) | copy-start | bytes 1540
  18.9 38.8 %collective-permute-start.5 = (bf16[128,4096]{1,0:T(8,128)(2,1)S(1)}, bf16[128,4096]{1,0:T(8,128)(2,1)S(1)}, u32[]{:S(2)}, u32[]{:S(2)}) collective-permute-start(bf16[128,4096]{1,0:T(8,128)(2,1)S(1)} %multiply_convert_fusion.g_ref), channel_id=1, source_target_pairs={{0,4},{1,5},{2,6},{3,7},{4,8},{5,9},{6,10},{7,11},{8,12},{9,13},{1... | collective-permute-start | bytes 3145736 | tf_op jit(solution)/shard_map/ppermute | solution.py:14
  20.2 48.9 %collective-permute-start.4 = (bf16[128,4096]{1,0:T(8,128)(2,1)S(1)}, bf16[128,4096]{1,0:T(8,128)(2,1)}, u32[]{:S(2)}, u32[]{:S(2)}) collective-permute-start(bf16[128,4096]{1,0:T(8,128)(2,1)S(1)} %multiply_convert_fusion.g_ref), channel_id=1, source_target_pairs={{0,2},{1,3},{2,4},{3,5},{4,6},{5,7},{6,8},{7,9},{8,10},{9,11},{10,... | collective-permute-start | bytes 3145736 | tf_op jit(solution)/shard_map/ppermute | solution.py:14
  57.6 17.6 %copy-start.1 = (bf16[128,4096]{1,0:T(8,128)(2,1)}, bf16[128,4096]{1,0:T(8,128)(2,1)S(1)}, u32[]{:S(2)}) copy-start(bf16[128,4096]{1,0:T(8,128)(2,1)S(1)} %collective-permute-done.5.refs_0_) | copy-start | bytes 3145732
  69.2 5.1 %collective-permute-start.6 = (bf16[128,4096]{1,0:T(8,128)(2,1)S(1)}, bf16[128,4096]{1,0:T(8,128)(2,1)S(1)}, u32[]{:S(2)}, u32[]{:S(2)}) collective-permute-start(bf16[128,4096]{1,0:T(8,128)(2,1)S(1)} %broadcast_select_fusion), channel_id=1, source_target_pairs={{0,1},{1,0},{2,3},{3,2},{4,5},{5,4},{6,7},{7,6},{8,9},{9,8},{10,11... | collective-permute-start | bytes 3145736 | tf_op jit(solution)/shard_map/ppermute | solution.py:19
  71.3 4.0 %collective-permute-start.7 = (bf16[128,4096]{1,0:T(8,128)(2,1)}, bf16[128,4096]{1,0:T(8,128)(2,1)S(1)}, u32[]{:S(2)}, u32[]{:S(2)}) collective-permute-start(bf16[128,4096]{1,0:T(8,128)(2,1)} %collective-permute-done.4.refs_2_), channel_id=1, source_target_pairs={{0,1},{1,0},{2,3},{3,2},{4,5},{5,4},{6,7},{7,6},{8,9},{9,8},{10,11... | collective-permute-start | bytes 3145736 | tf_op jit(solution)/shard_map/ppermute | solution.py:19
  74.3 1.0 %copy-start.2 = (bf16[128,4096]{1,0:T(8,128)(2,1)}, bf16[128,4096]{1,0:T(8,128)(2,1)S(1)}, u32[]{:S(2)}) copy-start(bf16[128,4096]{1,0:T(8,128)(2,1)S(1)} %collective-permute-done.6.refs_1_) | copy-start | bytes 3145732
  75.3 0.9 copy-start.3

commit v14 on v12

--- a/solution.py
+++ b/solution.py
@@ -19,19 +19,22 @@
     return lax.ppermute(value, axis, [(source, source ^ 1) for source in range(count)])
 
 
-def gathered(value, axis):
+def gather_rounds(blocks, axis, steps):
+    index = lax.axis_index(axis)
     count = lax.axis_size(axis)
-    if count & (count - 1):
-        return lax.all_gather(value, axis, axis=0, tiled=False)
-    index = lax.axis_index(axis)
-    blocks = value[None]
-    step = 1
-    while step < count:
+    for step in steps:
         received = lax.ppermute(blocks, axis, [(s, s ^ step) for s in range(count)])
         later = (index & step) != 0
         blocks = jnp.where(later, jnp.concatenate([received, blocks]), jnp.concatenate([blocks, received]))
-        step *= 2
     return blocks
+
+
+def unreversed(blocks, count):
+    rounds = count.bit_length() - 1
+    shape = blocks.shape[1:]
+    blocks = blocks.reshape((2,) * rounds + shape)
+    blocks = blocks.transpose(tuple(range(rounds))[::-1] + tuple(range(rounds, rounds + len(shape))))
+    return blocks.reshape((count,) + shape)
 
 
 def weight_kernel(p_ref, m_ref, g_ref, w_ref, a_ref, lhs_ref, rhs_ref, *, lags, rows, group_size):
@@ -105,8 +108,13 @@
     seg_row = jnp.zeros((1, filters), jnp.bfloat16).at[0, :rows].set(segment_ids.astype(jnp.bfloat16))
     packed = jnp.concatenate([taps, seg_row], axis=0)
     gated = (keys.astype(jnp.float32) * values.astype(jnp.float32)).astype(jnp.bfloat16)
-    packed = gathered(packed, "ctx")
+    assert ctx_count & (ctx_count - 1) == 0
+    steps = [ctx_count >> r for r in range(1, ctx_count.bit_length())]
+    packed = gather_rounds(packed[None], "ctx", steps[:-1])
     packed, gated = lax.optimization_barrier((packed, gated))
+    two_back = shifted(gated, "ctx", 2)
+    four_back = shifted(gated, "ctx", 4)
+    packed = unreversed(gather_rounds(packed, "ctx", steps[-1:]), ctx_count)
     all_taps = packed[:, :tap_rows].reshape(filt_len, filters).astype(jnp.float32)
     all_segs = packed[:, tap_rows, :rows].astype(jnp.int32)
     padded = jnp.concatenate(
@@ -122,8 +130,6 @@
         for lag in range(lags, -1, -1)
     ]
     mask = (segment_ids[:, None] == jnp.concatenate(seg_sources)[None, :]).astype(jnp.float32)
-    two_back = shifted(gated, "ctx", 2)
-    four_back = shifted(gated, "ctx", 4)
     lane_chunk = 128
     step_lanes = lane_chunk * 4 if channels % (lane_chunk * 4) == 0 else lane_chunk
     span = (lags + 1) * rows

time: 95.5 us -> 92.8 us (0.972)
  waiting for transfers between devices: 25.9 us -> 21.8 us
  starting transfers between devices: 11 us -> 12.3 us
    ppermute x4, waiting for transfers between devices: 12.6 us -> 6.61 us  [gather_rounds(): received = lax.ppermute(blocks, axis, [(s, s ^ step) for s in range(count)])]
    ppermute x4, starting transfers between devices: 2.34 us -> 5.68 us  [gather_rounds(): received = lax.ppermute(blocks, axis, [(s, s ^ step) for s in range(count)])]
    ppermute x2, starting transfers between devices: 4.2 us -> 2.22 us  [swapped(): lax.ppermute(value, axis, [(source, source ^ 1) for source in range(count)])]
    ppermute x2, waiting for transfers between devices: 9.41 us -> 11.3 us  [shifted(): lax.ppermute(value, axis, [(source, source + steps) for source in range(f...]
  transfers between devices with their start and end apart: 8 -> 8, of which waited for: 7 -> 6; matrix products, arithmetic and copies ran while one was open for 5% -> 5% of each run, Pallas kernels for 33% -> 34%
where the time goes in v14:
time: 92.8 us; the launch traced here: 92.5 us
  Pallas kernels  49.3 us (53%)
  waiting for transfers between devices  21.8 us (23%)
  starting transfers between devices  12.3 us (13%)
  other arithmetic  6.72 us (7%)
  local copies, waits for them, and re-layouts  2.1 us (2%)
    pallas_call x1, Pallas kernels, shards(): pl.pallas_call(functools.partial(weight_kernel, lags=lags, rows=rows, gro...  31.1 us
    pallas_call x1, Pallas kernels, shards(): pl.pallas_call(kernel, grid_spec=pltpu.PrefetchScalarGridSpec(num_scalar_...  18.2 us
    ppermute x2, waiting for transfers between devices, shifted(): lax.ppermute(value, axis, [(source, source + steps) for source in range(f...  11.3 us
    ppermute x4, waiting for transfers between devices, gather_rounds(): received = lax.ppermute(blocks, axis, [(s, s ^ step) for s in range(count)])  6.61 us
    ppermute x4, starting transfers between devices, gather_rounds(): received = lax.ppermute(blocks, axis, [(s, s ^ step) for s in range(count)])  5.68 us
    ppermute x2, starting transfers between devices, shifted(): lax.ppermute(value, axis, [(source, source + steps) for source in range(f...  4.44 us
    ppermute x2, waiting for transfers between devices, swapped(): lax.ppermute(value, axis, [(source, source ^ 1) for source in range(count)])  3.92 us
    ppermute x2, starting transfers between devices, swapped(): lax.ppermute(value, axis, [(source, source ^ 1) for source in range(count)])  2.22 us
  transfers between devices with their start and end apart: 8, of which 6 were waited for; matrix products, arithmetic and copies ran while one was open for 5% of the time, Pallas kernels for 34%

profile of v14, /device:TPU:25, one launch (start us, length us, event | category | flops | bytes accessed | tf_op | source)
XLA Modules:
  0.0 92.5 jit_solution(8043770975160136149)
XLA Ops:
  0.0 0.6 compare_reduce_fusion
  0.6 1.3 %fusion.3 = bf16[1,128]{1,0:T(2,128)(2,1)S(1)} fusion(pred[]{:T(512)} %compare_reduce_fusion, s32[128]{0:T(128)} %param.11), kind=kLoop, calls=%fused_computation.26 | loop fusion | flops 256 | bytes 769 | tf_op jit(solution)/shard_map/reshape.31
  1.9 0.7 fusion.2
  2.7 3.6 %collective-permute-done = bf16[1,33,256]{2,1,0:T(8,128)(2,1)S(1)} collective-permute-done((bf16[1,33,256]{2,1,0:T(8,128)(2,1)S(1)}, bf16[1,33,256]{2,1,0:T(8,128)(2,1)S(1)}, u32[]{:S(2)}, u32[]{:S(2)}) %collective-permute-start) | collective-permute-done | bytes 16928 | tf_op jit(solution)/shard_map/ppermute | solution.py:26
  6.3 0.1 collective-permute-start.1
  6.5 2.8 %collective-permute-done.1 = bf16[2,33,256]{2,1,0:T(8,128)(2,1)S(1)} collective-permute-done((bf16[2,33,256]{2,1,0:T(8,128)(2,1)S(1)}, bf16[2,33,256]{2,1,0:T(8,128)(2,1)S(1)}, u32[]{:S(2)}, u32[]{:S(2)}) %collective-permute-start.1) | collective-permute-done | bytes 33824 | tf_op jit(solution)/shard_map/ppermute | solution.py:26
  9.3 1.3 %collective-permute-start.2 = (bf16[4,33,256]{2,1,0:T(8,128)(2,1)S(1)}, bf16[4,33,256]{2,1,0:T(8,128)(2,1)S(1)}, u32[]{:S(2)}, u32[]{:S(2)}) collective-permute-start(bf16[4,33,256]{2,1,0:T(8,128)(2,1)S(1)} %maximum_select_fusion.2), channel_id=1, source_target_pairs={{0,2},{1,3},{2,0},{3,1},{4,6},{5,7},{6,4},{7,5},{8,10},{9,11},{10,... | collective-permute-start | bytes 202760 | tf_op jit(solution)/shard_map/ppermute | solution.py:26
  10.6 1.8 %multiply_convert_fusion.g_ref = bf16[128,4096]{1,0:T(8,128)(2,1)S(1)} fusion(bf16[128,4096]{1,0:T(8,128)(2,1)} %param.9, bf16[128,4096]{1,0:T(8,128)(2,1)} %param.8), kind=kLoop, calls=%fused_computation | loop fusion | flops 2097152 | bytes 3145728 | tf_op jit(solution)/shard_map/convert_element_type | solution.py:110
  12.4 0.2 collective-permute-done.2
  12.6 4.2 %collective-permute-start.3 = (bf16[8,33,256]{2,1,0:T(8,128)(2,1)S(1)}, bf16[8,33,256]{2,1,0:T(8,128)(2,1)S(1)}, u32[]{:S(2)}, u32[]{:S(2)}) collective-permute-start(bf16[8,33,256]{2,1,0:T(8,128)(2,1)S(1)} %maximum_select_fusion.1), channel_id=1, source_target_pairs={{0,1},{1,0},{2,3},{3,2},{4,5},{5,4},{6,7},{7,6},{8,9},{9,8},{10,11... | collective-permute-start | bytes 405512 | tf_op jit(solution)/shard_map/ppermute | solution.py:26
  16.9 1.3 %collective-permute-start.5 = (bf16[128,4096]{1,0:T(8,128)(2,1)S(1)}, bf16[128,4096]{1,0:T(8,128)(2,1)S(1)}, u32[]{:S(2)}, u32[]{:S(2)}) collective-permute-start(bf16[128,4096]{1,0:T(8,128)(2,1)S(1)} %multiply_convert_fusion.g_ref), channel_id=1, source_target_pairs={{0,4},{1,5},{2,6},{3,7},{4,8},{5,9},{6,10},{7,11},{8,12},{9,13},{1... | collective-permute-start | bytes 3145736 | tf_op jit(solution)/shard_map/ppermute | solution.py:14
  18.2 3.2 %collective-permute-start.4 = (bf16[128,4096]{1,0:T(8,128)(2,1)S(1)}, bf16[128,4096]{1,0:T(8,128)(2,1)}, u32[]{:S(2)}, u32[]{:S(2)}) collective-permute-start(bf16[128,4096]{1,0:T(8,128)(2,1)S(1)} %multiply_convert_fusion.g_ref), channel_id=1, source_target_pairs={{0,2},{1,3},{2,4},{3,5},{4,6},{5,7},{6,8},{7,9},{8,10},{9,11},{10,... | collective-permute-start | bytes 3145736 | tf_op jit(solution)/shard_map/ppermute | solution.py:14
  21.6 0.2 copy.9
  21.8 0.8 rev.3
  22.7 0.8 compare_convert_fusion.m_ref
  23.5 1.2 %maximum_maximum_fusion.p_ref = f32[256,768]{1,0:T(8,128)} fusion(f32[256,512]{1,0:T(8,128)S(1)} %rev.3, f32[768]{0:T(1024)S(1)} %pad.7.clone, f32[768]{0:T(1024)S(1)} %pad.5.clone), kind=kLoop, calls=%fused_computation.2 | loop fusion | flops 393216 | bytes 1316864 | tf_op jit(solution)/shard_map/concatenate | solution.py:120
  24.7 31.1 %shard_map.55 = (bf16[4,128,32768]{2,1,0:T(8,128)(2,1)}, f32[128,4096]{1,0:T(8,128)}) custom-call(f32[256,768]{1,0:T(8,128)} %maximum_maximum_fusion.p_ref, f32[128,640]{1,0:T(8,128)} %compare_convert_fusion.m_ref, bf16[128,4096]{1,0:T(8,128)(2,1)} %copy-done), custom_call_target="tpu_custom_call" | custom-call | tf_op jit(solution)/shard_map/pallas_call | solution.py:137
  55.8 11.3 %collective-permute-done.4.refs_2_ = bf16[128,4096]{1,0:T(8,128)(2,1)} collective-permute-done((bf16[128,4096]{1,0:T(8,128)(2,1)S(1)}, bf16[128,4096]{1,0:T(8,128)(2,1)}, u32[]{:S(2)}, u32[]{:S(2)}) %collective-permute-start.4) | collective-permute-done | bytes 1048608 | tf_op jit(solution)/shard_map/ppermute | solution.py:14
  67.1 0.1 broadcast_select_fusion
  67.2 2.1 %collective-permute-start.6 = (bf16[128,4096]{1,0:T(8,128)(2,1)S(1)}, bf16[128,4096]{1,0:T(8,128)(2,1)S(1)}, u32[]{:S(2)}, u32[]{:S(2)}) collective-permute-start(bf16[128,4096]{1,0:T(8,128)(2,1)S(1)} %broadcast_select_fusion), channel_id=1, source_target_pairs={{0,1},{1,0},{2,3},{3,2},{4,5},{5,4},{6,7},{7,6},{8,9},{9,8},{10,11... | collective-permute-start | bytes 3145736 | tf_op jit(solution)/shard_map/ppermute | solution.py:19
  69.4 2.9 %collective-permute-done.6.refs_1_ = bf16[128,4096]{1,0:T(8,128)(2,1)S(1)} collective-permute-done((bf16[128,4096]{1,0:T(8,128)(2,1)S(1)}, bf16[128,4096]{1,0:T(8,128)(2,1)S(1)}, u32[]{:S(2)}, u32[]{:S(2)}) %collective-permute-start.6) | collective-permute-done | bytes 1048608 | tf_op jit(solution)/shard_map/ppermute | solution.py:19
  72.3 1.0 %collective-permute-done.7.refs_3_ = bf16[128,4096]{1,0:T(8,128)(2,1)S(1)} collective-permute-done((bf16[128,4096]{1,0:T(8,128)(2,1)}, bf16[128,4096]{1,0:T(8,128)(2,1)S(1)}, u32[]{:S(2)}, u32[]{:S(2)}) %collective-permute-start.7) | collective-permute-done | bytes 1048608 | tf_op jit(solution)/shard_map/ppermute | solution.py:19
  73.3 0.9 %copy-done.3 = bf16[128,4096]{1,0:T(8,128)(2,1)} copy-done((bf16[128,4096]{1,0:T(8,128)(2,1)}, bf16[128,4096]{1,0:T(8,128)(2,1)S(1)}, u32[]{:S(2)}) %copy-start.3) | copy-done | bytes 1048600
  74.3 18.2 %shard_map.56 = bf16[128,4096]{1,0:T(8,128)(2,1)} custom-call(s32[1]{0:T(128)} %bitcast.core_ref, bf16[128,4096]{1,0:T(8,128)(2,1)} %copy-done.1, bf16[128,4096]{1,0:T(8,128)(2,1)} %copy-done.2, bf16[128,4096]{1,0:T(8,128)(2,1)} %collective-permute-done.4.refs_2_, bf16[128,4096]{1,0:T(8,128)(2,1)} %copy-done.3, ...), custom_call_target="tpu_custom_call" | custom-call | tf_op jit(solution)/shard_map/pallas_call | solution.py:164
  (31 shorter events, 0.5 us)
Async XLA Ops:
  2.7 3.6 %collective-permute-start = (bf16[1,33,256]{2,1,0:T(8,128)(2,1)S(1)}, bf16[1,33,256]{2,1,0:T(8,128)(2,1)S(1)}, u32[]{:S(2)}, u32[]{:S(2)}) collective-permute-start(bf16[1,33,256]{2,1,0:T(8,128)(2,1)S(1)} %fusion.2), channel_id=1, source_target_pairs={{0,8},{1,9},{2,10},{3,11},{4,12},{5,13},{6,14},{7,15},{8,0},{9,1},... | collective-permute-start | bytes 50696 | tf_op jit(solution)/shard_map/ppermute | solution.py:26
  6.3 2.9 %collective-permute-start.1 = (bf16[2,33,256]{2,1,0:T(8,128)(2,1)S(1)}, bf16[2,33,256]{2,1,0:T(8,128)(2,1)S(1)}, u32[]{:S(2)}, u32[]{:S(2)}) collective-permute-start(bf16[2,33,256]{2,1,0:T(8,128)(2,1)S(1)} %maximum_select_fusion.3), channel_id=1, source_target_pairs={{0,4},{1,5},{2,6},{3,7},{4,0},{5,1},{6,2},{7,3},{8,12},{9,13},{10,... | collective-permute-start | bytes 101384 | tf_op jit(solution)/shard_map/ppermute | solution.py:26
  9.3 3.4 %collective-permute-start.2 = (bf16[4,33,256]{2,1,0:T(8,128)(2,1)S(1)}, bf16[4,33,256]{2,1,0:T(8,128)(2,1)S(1)}, u32[]{:S(2)}, u32[]{:S(2)}) collective-permute-start(bf16[4,33,256]{2,1,0:T(8,128)(2,1)S(1)} %maximum_select_fusion.2), channel_id=1, source_target_pairs={{0,2},{1,3},{2,0},{3,1},{4,6},{5,7},{6,4},{7,5},{8,10},{9,11},{10,... | collective-permute-start | bytes 202760 | tf_op jit(solution)/shard_map/ppermute | solution.py:26
  12.4 12.3 %copy-start = (bf16[128,4096]{1,0:T(8,128)(2,1)}, bf16[128,4096]{1,0:T(8,128)(2,1)S(1)}, u32[]{:S(2)}) copy-start(bf16[128,4096]{1,0:T(8,128)(2,1)S(1)} %multiply_convert_fusion.g_ref) | copy-start | bytes 3145732
  12.6 8.7 %collective-permute-start.3 = (bf16[8,33,256]{2,1,0:T(8,128)(2,1)S(1)}, bf16[8,33,256]{2,1,0:T(8,128)(2,1)S(1)}, u32[]{:S(2)}, u32[]{:S(2)}) collective-permute-start(bf16[8,33,256]{2,1,0:T(8,128)(2,1)S(1)} %maximum_select_fusion.1), channel_id=1, source_target_pairs={{0,1},{1,0},{2,3},{3,2},{4,5},{5,4},{6,7},{7,6},{8,9},{9,8},{10,11... | collective-permute-start | bytes 405512 | tf_op jit(solution)/shard_map/ppermute | solution.py:26
  16.9 38.9 %collective-permute-start.5 = (bf16[128,4096]{1,0:T(8,128)(2,1)S(1)}, bf16[128,4096]{1,0:T(8,128)(2,1)S(1)}, u32[]{:S(2)}, u32[]{:S(2)}) collective-permute-start(bf16[128,4096]{1,0:T(8,128)(2,1)S(1)} %multiply_convert_fusion.g_ref), channel_id=1, source_target_pairs={{0,4},{1,5},{2,6},{3,7},{4,8},{5,9},{6,10},{7,11},{8,12},{9,13},{1... | collective-permute-start | bytes 3145736 | tf_op jit(solution)/shard_map/ppermute | solution.py:14
  18.2 48.9 %collective-permute-start.4 = (bf16[128,4096]{1,0:T(8,128)(2,1)S(1)}, bf16[128,4096]{1,0:T(8,128)(2,1)}, u32[]{:S(2)}, u32[]{:S(2)}) collective-permute-start(bf16[128,4096]{1,0:T(8,128)(2,1)S(1)} %multiply_convert_fusion.g_ref), channel_id=1, source_target_pairs={{0,2},{1,3},{2,4},{3,5},{4,6},{5,7},{6,8},{7,9},{8,10},{9,11},{10,... | collective-permute-start | bytes 3145736 | tf_op jit(solution)/shard_map/ppermute | solution.py:14
  21.4 1.2 %copy-start.4 = (s32[128]{0:T(128)S(1)}, s32[128]{0:T(128)}, u32[]{:S(2)}) copy-start(s32[128]{0:T(128)} %param.11) | copy-start | bytes 1540
  55.8 17.5 %copy-start.1 = (bf16[128,4096]{1,0:T(8,128)(2,1)}, bf16[128,4096]{1,0:T(8,128)(2,1)S(1)}, u32[]{:S(2)}) copy-start(bf16[128,4096]{1,0:T(8,128)(2,1)S(1)} %collective-permute-done.5.refs_0_) | copy-start | bytes 3145732
  67.2 5.1 %collective-permute-start.6 = (bf16[128,4096]{1,0:T(8,128)(2,1)S(1)}, bf16[128,4096]{1,0:T(8,128)(2,1)S(1)}, u32[]{:S(2)}, u32[]{:S(2)}) collective-permute-start(bf16[128,4096]{1,0:T(8,128)(2,1)S(1)} %broadcast_select_fusion), channel_id=1, source_target_pairs={{0,1},{1,0},{2,3},{3,2},{4,5},{5,4},{6,7},{7,6},{8,9},{9,8},{10,11... | collective-permute-start | bytes 3145736 | tf_op jit(solution)/shard_map/ppermute | solution.py:19
  69.3 4.0 %collective-permute-start.7 = (bf16[128,4096]{1,0:T(8,128)(2,1)}, bf16[128,4096]{1,0:T(8,128)(2,1)S(1)}, u32[]{:S(2)}, u32[]{:S(2)}) collective-permute-start(bf16[128,4096]{1,0:T(8,128)(2,1)} %collective-permute-done.4.refs_2_), channel_id=1, source_target_pairs={{0,1},{1,0},{2,3},{3,2},{4,5},{5,4},{6,7},{7,6},{8,9},{9,8},{10,11... | collective-permute-start | bytes 3145736 | tf_op jit(solution)/shard_map/ppermute | solution.py:19
  72.3 1.0 %copy-start.2 = (bf16[128,4096]{1,0:T(8,128)(2,1)}, bf16[128,4096]{1,0:T(8,128)(2,1)S(1)}, u32[]{:S(2)}) copy-start(bf16[128,4096]{1,0:T(8,128)(2,1)S(1)} %collective-permute-done.6.refs_1_) | copy-start | bytes 3145732
  73.3 0.9 %copy-start.3 = (bf16[128,4096]{1,0:T(8,128)(2,1)}, bf16[128,4096]{1,0:T(8,128)(2,1)S(1)}, u32[]{:S(2)}) copy-start(bf16[128,4096]{1,0:T(8,128)(2,1)S(1)} %collective-permute-done.7.refs_3_) | copy-start | bytes 3145732

commit v15 on v14

--- a/solution.py
+++ b/solution.py
@@ -72,7 +72,7 @@
 
 def conv_kernel(core_ref, *refs, lags, rows, group_size):
     g_refs = list(refs[:lags])
-    w_ref, a_ref, q_ref, o_ref, rhs_ref = refs[lags:]
+    own_ref, w_ref, a_ref, q_ref, o_ref, rhs_ref = refs[lags:]
     lane_chunk = rhs_ref.shape[1]
     per_chunk = lane_chunk // group_size
     owner = lax.broadcasted_iota(jnp.int32, (rows, lane_chunk), 1) // group_size
@@ -80,6 +80,7 @@
     for u in range(q_ref.shape[1] // lane_chunk):
         lanes = slice(lane_chunk * u, lane_chunk * (u + 1))
         blocks = [g[:, lanes] for g in g_refs]
+        blocks[lags - 3] = jnp.where(even, blocks[lags - 3], own_ref[:, lanes])
         near, far = blocks[lags - 1], blocks[lags - 3]
         blocks[lags - 1] = jnp.where(even, near, far)
         blocks[lags - 3] = jnp.where(even, far, near)
@@ -157,8 +158,11 @@
     )(padded, mask, gated)
     weights, own_term, two_back, four_back = lax.optimization_barrier((weights, own_term, two_back, four_back))
     swap_a = swapped(two_back, "ctx")
-    swap_b = swapped(jnp.where(core == 1, four_back, gated), "ctx")
-    sources = [four_back, swap_b, two_back, swap_a]
+    own_out, _ = lax.optimization_barrier((gated, packed))
+    pairs = [(source, source ^ 1) for source in range(ctx_count)]
+    sibling_own = lax.ppermute(own_out, "ctx", [(s, d) for s, d in pairs if s % 2 == 0])
+    sibling_four = lax.ppermute(four_back, "ctx", [(s, d) for s, d in pairs if s % 2 == 1])
+    sources = [four_back, sibling_four, two_back, swap_a, sibling_own]
     kernel = functools.partial(conv_kernel, lags=lags, rows=rows, group_size=group_size)
     block = pl.BlockSpec((rows, step_lanes), lambda j, c: (0, j))
     return pl.pallas_call(
@@ -166,7 +170,7 @@
         grid_spec=pltpu.PrefetchScalarGridSpec(
             num_scalar_prefetch=1,
             grid=(channels // step_lanes,),
-            in_specs=[block] * lags
+            in_specs=[block] * (lags + 1)
             + [
                 pl.BlockSpec((lags, rows, step_filters * rows), lambda j, c: (0, 0, j)),
                 block,

time: 92.8 us -> 92.3 us (level)
  starting transfers between devices: 12.3 us -> 14.3 us
  waiting for transfers between devices: 21.8 us -> 20.6 us
  local copies, waits for them, and re-layouts: 2.1 us -> 1.16 us
    ppermute x0 -> x2, starting transfers between devices: none -> 4.1 us  [the longest x1 2.8 us: shards(): lax.ppermute(four_back, 'ctx', [(s, d) for s, d in pairs if s % 2 == 1])]
    ppermute x2 -> x1, starting transfers between devices: 2.22 us -> 0.07 us  [swapped(): lax.ppermute(value, axis, [(source, source ^ 1) for source in range(count)])]
    ppermute x0 -> x2, waiting for transfers between devices: none -> 2.1 us  [the longest x1 2.1 us: shards(): lax.ppermute(four_back, 'ctx', [(s, d) for s, d in pairs if s % 2 == 1])]
    ppermute x2 -> x1, waiting for transfers between devices: 3.92 us -> 1.84 us  [swapped(): lax.ppermute(value, axis, [(source, source ^ 1) for source in range(count)])]
    ppermute x2, waiting for transfers between devices: 11.3 us -> 10.1 us  [shifted(): lax.ppermute(value, axis, [(source, source + steps) for source in range(f...]
    unnamed x14 -> x12, local copies, waits for them, and re-layouts: 1 us -> 0.07 us
  transfers between devices with their start and end apart: 8 -> 9, of which waited for: 6 -> 6; matrix products, arithmetic and copies ran while one was open for 5% -> 5% of each run, Pallas kernels for 34% -> 34%
where the time goes in v15:
time: 92.3 us; the launch traced here: 92 us
  Pallas kernels  49.2 us (53%)
  waiting for transfers between devices  20.6 us (22%)
  starting transfers between devices  14.3 us (15%)
  other arithmetic  6.53 us (7%)
  local copies, waits for them, and re-layouts  1.16 us (1%)
    pallas_call x1, Pallas kernels, shards(): pl.pallas_call(functools.partial(weight_kernel, lags=lags, rows=rows, gro...  31.1 us
    pallas_call x1, Pallas kernels, shards(): pl.pallas_call(kernel, grid_spec=pltpu.PrefetchScalarGridSpec(num_scalar_...  18.1 us
    ppermute x2, waiting for transfers between devices, shifted(): lax.ppermute(value, axis, [(source, source + steps) for source in range(f...  10.1 us
    ppermute x4, waiting for transfers between devices, gather_rounds(): received = lax.ppermute(blocks, axis, [(s, s ^ step) for s in range(count)])  6.61 us
    ppermute x4, starting transfers between devices, gather_rounds(): received = lax.ppermute(blocks, axis, [(s, s ^ step) for s in range(count)])  5.68 us
    ppermute x2, starting transfers between devices, shifted(): lax.ppermute(value, axis, [(source, source + steps) for source in range(f...  4.43 us
    ppermute x1, starting transfers between devices, shards(): lax.ppermute(four_back, 'ctx', [(s, d) for s, d in pairs if s % 2 == 1])  2.8 us
    ppermute x1, waiting for transfers between devices, shards(): lax.ppermute(four_back, 'ctx', [(s, d) for s, d in pairs if s % 2 == 1])  2.1 us
  transfers between devices with their start and end apart: 9, of which 6 were waited for; matrix products, arithmetic and copies ran while one was open for 5% of the time, Pallas kernels for 34%

profile of v15, /device:TPU:25, one launch (start us, length us, event | category | flops | bytes accessed | tf_op | source)
XLA Modules:
  0.0 92.0 jit_solution(2156996648711194355)
XLA Ops:
  0.0 0.6 compare_reduce_fusion
  0.6 1.3 %fusion.3 = bf16[1,128]{1,0:T(2,128)(2,1)S(1)} fusion(pred[]{:T(512)} %compare_reduce_fusion, s32[128]{0:T(128)} %param.11), kind=kLoop, calls=%fused_computation.25 | loop fusion | flops 256 | bytes 769 | tf_op jit(solution)/shard_map/reshape.31
  1.9 0.7 fusion.2
  2.7 3.6 %collective-permute-done = bf16[1,33,256]{2,1,0:T(8,128)(2,1)S(1)} collective-permute-done((bf16[1,33,256]{2,1,0:T(8,128)(2,1)S(1)}, bf16[1,33,256]{2,1,0:T(8,128)(2,1)S(1)}, u32[]{:S(2)}, u32[]{:S(2)}) %collective-permute-start) | collective-permute-done | bytes 16928 | tf_op jit(solution)/shard_map/ppermute | solution.py:26
  6.3 0.1 collective-permute-start.1
  6.5 2.8 %collective-permute-done.1 = bf16[2,33,256]{2,1,0:T(8,128)(2,1)S(1)} collective-permute-done((bf16[2,33,256]{2,1,0:T(8,128)(2,1)S(1)}, bf16[2,33,256]{2,1,0:T(8,128)(2,1)S(1)}, u32[]{:S(2)}, u32[]{:S(2)}) %collective-permute-start.1) | collective-permute-done | bytes 33824 | tf_op jit(solution)/shard_map/ppermute | solution.py:26
  9.3 1.3 %collective-permute-start.2 = (bf16[4,33,256]{2,1,0:T(8,128)(2,1)S(1)}, bf16[4,33,256]{2,1,0:T(8,128)(2,1)S(1)}, u32[]{:S(2)}, u32[]{:S(2)}) collective-permute-start(bf16[4,33,256]{2,1,0:T(8,128)(2,1)S(1)} %maximum_select_fusion.2), channel_id=1, source_target_pairs={{0,2},{1,3},{2,0},{3,1},{4,6},{5,7},{6,4},{7,5},{8,10},{9,11},{10,... | collective-permute-start | bytes 202760 | tf_op jit(solution)/shard_map/ppermute | solution.py:26
  10.6 1.8 %multiply_convert_fusion.g_ref = bf16[128,4096]{1,0:T(8,128)(2,1)S(1)} fusion(bf16[128,4096]{1,0:T(8,128)(2,1)} %param.9, bf16[128,4096]{1,0:T(8,128)(2,1)} %param.8), kind=kLoop, calls=%fused_computation | loop fusion | flops 2097152 | bytes 3145728 | tf_op jit(solution)/shard_map/convert_element_type | solution.py:111
  12.4 0.2 collective-permute-done.2
  12.6 4.2 %collective-permute-start.3 = (bf16[8,33,256]{2,1,0:T(8,128)(2,1)S(1)}, bf16[8,33,256]{2,1,0:T(8,128)(2,1)S(1)}, u32[]{:S(2)}, u32[]{:S(2)}) collective-permute-start(bf16[8,33,256]{2,1,0:T(8,128)(2,1)S(1)} %maximum_select_fusion.1), channel_id=1, source_target_pairs={{0,1},{1,0},{2,3},{3,2},{4,5},{5,4},{6,7},{7,6},{8,9},{9,8},{10,11... | collective-permute-start | bytes 405512 | tf_op jit(solution)/shard_map/ppermute | solution.py:26
  16.8 0.1 pad.7.clone
  16.9 1.3 %collective-permute-start.5 = (bf16[128,4096]{1,0:T(8,128)(2,1)S(1)}, bf16[128,4096]{1,0:T(8,128)(2,1)S(1)}, u32[]{:S(2)}, u32[]{:S(2)}) collective-permute-start(bf16[128,4096]{1,0:T(8,128)(2,1)S(1)} %multiply_convert_fusion.g_ref), channel_id=1, source_target_pairs={{0,4},{1,5},{2,6},{3,7},{4,8},{5,9},{6,10},{7,11},{8,12},{9,13},{1... | collective-permute-start | bytes 3145736 | tf_op jit(solution)/shard_map/ppermute | solution.py:14
  18.2 3.1 %collective-permute-start.4 = (bf16[128,4096]{1,0:T(8,128)(2,1)S(1)}, bf16[128,4096]{1,0:T(8,128)(2,1)}, u32[]{:S(2)}, u32[]{:S(2)}) collective-permute-start(bf16[128,4096]{1,0:T(8,128)(2,1)S(1)} %multiply_convert_fusion.g_ref), channel_id=1, source_target_pairs={{0,2},{1,3},{2,4},{3,5},{4,6},{5,7},{6,8},{7,9},{8,10},{9,11},{10,... | collective-permute-start | bytes 3145736 | tf_op jit(solution)/shard_map/ppermute | solution.py:14
  21.6 0.2 copy.9
  21.8 0.8 rev.3
  22.5 1.3 %collective-permute-start.8 = (bf16[128,4096]{1,0:T(8,128)(2,1)S(1)}, bf16[128,4096]{1,0:T(8,128)(2,1)}, u32[]{:S(2)}, u32[]{:S(2)}) collective-permute-start(bf16[128,4096]{1,0:T(8,128)(2,1)S(1)} %multiply_convert_fusion.g_ref), channel_id=1, source_target_pairs={{0,1},{2,3},{4,5},{6,7},{8,9},{10,11},{12,13},{14,15},{16,17},{18,... | collective-permute-start | bytes 3145736 | tf_op jit(solution)/shard_map/ppermute | solution.py:163
  23.9 0.8 compare_convert_fusion.m_ref
  24.8 1.1 %maximum_maximum_fusion.p_ref = f32[256,768]{1,0:T(8,128)} fusion(f32[256,512]{1,0:T(8,128)S(1)} %rev.3, f32[768]{0:T(1024)S(1)} %pad.7.clone, f32[768]{0:T(1024)S(1)} %pad.5.clone), kind=kLoop, calls=%fused_computation.1 | loop fusion | flops 393216 | bytes 1316864 | tf_op jit(solution)/shard_map/concatenate | solution.py:121
  25.9 31.1 %shard_map.55 = (bf16[4,128,32768]{2,1,0:T(8,128)(2,1)}, f32[128,4096]{1,0:T(8,128)}) custom-call(f32[256,768]{1,0:T(8,128)} %maximum_maximum_fusion.p_ref, f32[128,640]{1,0:T(8,128)} %compare_convert_fusion.m_ref, bf16[128,4096]{1,0:T(8,128)(2,1)} %copy-done), custom_call_target="tpu_custom_call" | custom-call | tf_op jit(solution)/shard_map/pallas_call | solution.py:138
  57.0 10.1 %collective-permute-done.4.refs_2_ = bf16[128,4096]{1,0:T(8,128)(2,1)} collective-permute-done((bf16[128,4096]{1,0:T(8,128)(2,1)S(1)}, bf16[128,4096]{1,0:T(8,128)(2,1)}, u32[]{:S(2)}, u32[]{:S(2)}) %collective-permute-start.4) | collective-permute-done | bytes 1048608 | tf_op jit(solution)/shard_map/ppermute | solution.py:14
  67.1 2.8 %collective-permute-start.6 = (bf16[128,4096]{1,0:T(8,128)(2,1)S(1)}, bf16[128,4096]{1,0:T(8,128)(2,1)S(1)}, u32[]{:S(2)}, u32[]{:S(2)}) collective-permute-start(bf16[128,4096]{1,0:T(8,128)(2,1)S(1)} %collective-permute-done.5.refs_0_), channel_id=1, source_target_pairs={{1,0},{3,2},{5,4},{7,6},{9,8},{11,10},{13,12},{15,14},{17,16},{19,... | collective-permute-start | bytes 3145736 | tf_op jit(solution)/shard_map/ppermute | solution.py:164
  70.0 2.1 %collective-permute-done.6.refs_1_ = bf16[128,4096]{1,0:T(8,128)(2,1)S(1)} collective-permute-done((bf16[128,4096]{1,0:T(8,128)(2,1)S(1)}, bf16[128,4096]{1,0:T(8,128)(2,1)S(1)}, u32[]{:S(2)}, u32[]{:S(2)}) %collective-permute-start.6) | collective-permute-done | bytes 1048608 | tf_op jit(solution)/shard_map/ppermute | solution.py:164
  72.1 1.8 %collective-permute-done.7.refs_3_ = bf16[128,4096]{1,0:T(8,128)(2,1)} collective-permute-done((bf16[128,4096]{1,0:T(8,128)(2,1)}, bf16[128,4096]{1,0:T(8,128)(2,1)}, u32[]{:S(2)}, u32[]{:S(2)}) %collective-permute-start.7) | collective-permute-done | bytes 1048608 | tf_op jit(solution)/shard_map/ppermute | solution.py:19
  73.9 18.1 %shard_map.56 = bf16[128,4096]{1,0:T(8,128)(2,1)} custom-call(s32[1]{0:T(128)} %bitcast.core_ref, bf16[128,4096]{1,0:T(8,128)(2,1)} %copy-done.1, bf16[128,4096]{1,0:T(8,128)(2,1)} %copy-done.2, bf16[128,4096]{1,0:T(8,128)(2,1)} %collective-permute-done.4.refs_2_, bf16[128,4096]{1,0:T(8,128)(2,1)} %collective-permute-done.7.refs_3_, ...), custom_call_target="tpu_custom_call" | custom-call | tf_op jit(solution)/shard_map/pallas_call | solution.py:168
  (30 shorter events, 0.4 us)
Async XLA Ops:
  2.7 3.6 %collective-permute-start = (bf16[1,33,256]{2,1,0:T(8,128)(2,1)S(1)}, bf16[1,33,256]{2,1,0:T(8,128)(2,1)S(1)}, u32[]{:S(2)}, u32[]{:S(2)}) collective-permute-start(bf16[1,33,256]{2,1,0:T(8,128)(2,1)S(1)} %fusion.2), channel_id=1, source_target_pairs={{0,8},{1,9},{2,10},{3,11},{4,12},{5,13},{6,14},{7,15},{8,0},{9,1},... | collective-permute-start | bytes 50696 | tf_op jit(solution)/shard_map/ppermute | solution.py:26
  6.3 2.9 %collective-permute-start.1 = (bf16[2,33,256]{2,1,0:T(8,128)(2,1)S(1)}, bf16[2,33,256]{2,1,0:T(8,128)(2,1)S(1)}, u32[]{:S(2)}, u32[]{:S(2)}) collective-permute-start(bf16[2,33,256]{2,1,0:T(8,128)(2,1)S(1)} %maximum_select_fusion.3), channel_id=1, source_target_pairs={{0,4},{1,5},{2,6},{3,7},{4,0},{5,1},{6,2},{7,3},{8,12},{9,13},{10,... | collective-permute-start | bytes 101384 | tf_op jit(solution)/shard_map/ppermute | solution.py:26
  9.3 3.4 %collective-permute-start.2 = (bf16[4,33,256]{2,1,0:T(8,128)(2,1)S(1)}, bf16[4,33,256]{2,1,0:T(8,128)(2,1)S(1)}, u32[]{:S(2)}, u32[]{:S(2)}) collective-permute-start(bf16[4,33,256]{2,1,0:T(8,128)(2,1)S(1)} %maximum_select_fusion.2), channel_id=1, source_target_pairs={{0,2},{1,3},{2,0},{3,1},{4,6},{5,7},{6,4},{7,5},{8,10},{9,11},{10,... | collective-permute-start | bytes 202760 | tf_op jit(solution)/shard_map/ppermute | solution.py:26
  12.4 10.2 %copy-start = (bf16[128,4096]{1,0:T(8,128)(2,1)}, bf16[128,4096]{1,0:T(8,128)(2,1)S(1)}, u32[]{:S(2)}) copy-start(bf16[128,4096]{1,0:T(8,128)(2,1)S(1)} %multiply_convert_fusion.g_ref) | copy-start | bytes 3145732
  12.6 8.7 %collective-permute-start.3 = (bf16[8,33,256]{2,1,0:T(8,128)(2,1)S(1)}, bf16[8,33,256]{2,1,0:T(8,128)(2,1)S(1)}, u32[]{:S(2)}, u32[]{:S(2)}) collective-permute-start(bf16[8,33,256]{2,1,0:T(8,128)(2,1)S(1)} %maximum_select_fusion.1), channel_id=1, source_target_pairs={{0,1},{1,0},{2,3},{3,2},{4,5},{5,4},{6,7},{7,6},{8,9},{9,8},{10,11... | collective-permute-start | bytes 405512 | tf_op jit(solution)/shard_map/ppermute | solution.py:26
  16.9 40.1 %collective-permute-start.5 = (bf16[128,4096]{1,0:T(8,128)(2,1)S(1)}, bf16[128,4096]{1,0:T(8,128)(2,1)S(1)}, u32[]{:S(2)}, u32[]{:S(2)}) collective-permute-start(bf16[128,4096]{1,0:T(8,128)(2,1)S(1)} %multiply_convert_fusion.g_ref), channel_id=1, source_target_pairs={{0,4},{1,5},{2,6},{3,7},{4,8},{5,9},{6,10},{7,11},{8,12},{9,13},{1... | collective-permute-start | bytes 3145736 | tf_op jit(solution)/shard_map/ppermute | solution.py:14
  18.2 48.9 %collective-permute-start.4 = (bf16[128,4096]{1,0:T(8,128)(2,1)S(1)}, bf16[128,4096]{1,0:T(8,128)(2,1)}, u32[]{:S(2)}, u32[]{:S(2)}) collective-permute-start(bf16[128,4096]{1,0:T(8,128)(2,1)S(1)} %multiply_convert_fusion.g_ref), channel_id=1, source_target_pairs={{0,2},{1,3},{2,4},{3,5},{4,6},{5,7},{6,8},{7,9},{8,10},{9,11},{10,... | collective-permute-start | bytes 3145736 | tf_op jit(solution)/shard_map/ppermute | solution.py:14
  21.4 2.5 %copy-start.3 = (s32[128]{0:T(128)S(1)}, s32[128]{0:T(128)}, u32[]{:S(2)}) copy-start(s32[128]{0:T(128)} %param.11) | copy-start | bytes 1540
  22.5 47.4 %collective-permute-start.8 = (bf16[128,4096]{1,0:T(8,128)(2,1)S(1)}, bf16[128,4096]{1,0:T(8,128)(2,1)}, u32[]{:S(2)}, u32[]{:S(2)}) collective-permute-start(bf16[128,4096]{1,0:T(8,128)(2,1)S(1)} %multiply_convert_fusion.g_ref), channel_id=1, source_target_pairs={{0,1},{2,3},{4,5},{6,7},{8,9},{10,11},{12,13},{14,15},{16,17},{18,... | collective-permute-start | bytes 3145736 | tf_op jit(solution)/shard_map/ppermute | solution.py:163
  57.0 16.9 %copy-start.1 = (bf16[128,4096]{1,0:T(8,128)(2,1)}, bf16[128,4096]{1,0:T(8,128)(2,1)S(1)}, u32[]{:S(2)}) copy-start(bf16[128,4096]{1,0:T(8,128)(2,1)S(1)} %collective-permute-done.5.refs_0_) | copy-start | bytes 3145732
  67.1 5.0 %collective-permute-start.6 = (bf16[128,4096]{1,0:T(8,128)(2,1)S(1)}, bf16[128,4096]{1,0:T(8,128)(2,1)S(1)}, u32[]{:S(2)}, u32[]{:S(2)}) collective-permute-start(bf16[128,4096]{1,0:T(8,128)(2,1)S(1)} %collective-permute-done.5.refs_0_), channel_id=1, source_target_pairs={{1,0},{3,2},{5,4},{7,6},{9,8},{11,10},{13,12},{15,14},{17,16},{19,... | collective-permute-start | bytes 3145736 | tf_op jit(solution)/shard_map/ppermute | solution.py:164
  69.9 4.0 %collective-permute-start.7 = (bf16[128,4096]{1,0:T(8,128)(2,1)}, bf16[128,4096]{1,0:T(8,128)(2,1)}, u32[]{:S(2)}, u32[]{:S(2)}) collective-permute-start(bf16[128,4096]{1,0:T(8,128)(2,1)} %collective-permute-done.4.refs_2_), channel_id=1, source_target_pairs={{0,1},{1,0},{2,3},{3,2},{4,5},{5,4},{6,7},{7,6},{8,9},{9,8},{10,11... | collective-permute-start | bytes 3145736 | tf_op jit(solution)/shard_map/ppermute | solution.py:19
  72.1 1.8 %copy-start.2 = (bf16[128,4096]{1,0:T(8,128)(2,1)}, bf16[128,4096]{1,0:T(8,128)(2,1)S(1)}, u32[]{:S(2)}) copy-start(bf16[128,4096]{1,0:T(8,128)(2,1)S(1)} %collective-permute-done.6.refs_1_) | copy-start | bytes 3145732

commit v16 on v15

--- a/solution.py
+++ b/solution.py
@@ -156,7 +156,7 @@
             pltpu.VMEM((rows * (lane_chunk // group_size), lane_chunk), jnp.bfloat16),
         ],
     )(padded, mask, gated)
-    weights, own_term, two_back, four_back = lax.optimization_barrier((weights, own_term, two_back, four_back))
+    weights, own_term, four_back = lax.optimization_barrier((weights, own_term, four_back))
     swap_a = swapped(two_back, "ctx")
     own_out, _ = lax.optimization_barrier((gated, packed))
     pairs = [(source, source ^ 1) for source in range(ctx_count)]

time: 92.3 us -> 88.9 us (0.963)
  waiting for transfers between devices: 20.6 us -> 15.2 us
  starting transfers between devices: 14.3 us -> 16.3 us
    ppermute x2, waiting for transfers between devices: 10.1 us -> 5.96 us  [shifted(): lax.ppermute(value, axis, [(source, source + steps) for source in range(f...]
    ppermute x1, waiting for transfers between devices: 2.1 us -> 0.01 us  [shards(): lax.ppermute(four_back, 'ctx', [(s, d) for s, d in pairs if s % 2 == 1])]
    ppermute x1, starting transfers between devices: 2.8 us -> 4.1 us  [shards(): lax.ppermute(four_back, 'ctx', [(s, d) for s, d in pairs if s % 2 == 1])]
  transfers between devices with their start and end apart: 9 -> 9, of which waited for: 6 -> 5; matrix products, arithmetic and copies ran while one was open for 5% -> 6% of each run, Pallas kernels for 34% -> 35%
where the time goes in v16:
time: 88.9 us; the launch traced here: 88.6 us
  Pallas kernels  49.2 us (55%)
  starting transfers between devices  16.3 us (18%)
  waiting for transfers between devices  15.2 us (17%)
  other arithmetic  6.53 us (7%)
  local copies, waits for them, and re-layouts  1.16 us (1%)
    pallas_call x1, Pallas kernels, shards(): pl.pallas_call(functools.partial(weight_kernel, lags=lags, rows=rows, gro...  31.1 us
    pallas_call x1, Pallas kernels, shards(): pl.pallas_call(kernel, grid_spec=pltpu.PrefetchScalarGridSpec(num_scalar_...  18.1 us
    ppermute x4, waiting for transfers between devices, gather_rounds(): received = lax.ppermute(blocks, axis, [(s, s ^ step) for s in range(count)])  6.61 us
    ppermute x2, waiting for transfers between devices, shifted(): lax.ppermute(value, axis, [(source, source + steps) for source in range(f...  5.96 us
    ppermute x4, starting transfers between devices, gather_rounds(): received = lax.ppermute(blocks, axis, [(s, s ^ step) for s in range(count)])  5.68 us
    ppermute x2, starting transfers between devices, shifted(): lax.ppermute(value, axis, [(source, source + steps) for source in range(f...  4.43 us
    ppermute x1, starting transfers between devices, shards(): lax.ppermute(four_back, 'ctx', [(s, d) for s, d in pairs if s % 2 == 1])  4.1 us
    ppermute x1, waiting for transfers between devices, swapped(): lax.ppermute(value, axis, [(source, source ^ 1) for source in range(count)])  2.62 us
  transfers between devices with their start and end apart: 9, of which 5 were waited for; matrix products, arithmetic and copies ran while one was open for 6% of the time, Pallas kernels for 35%

profile of v16, /device:TPU:25, one launch (start us, length us, event | category | flops | bytes accessed | tf_op | source)
XLA Modules:
  0.0 88.6 jit_solution(17835294664830131733)
XLA Ops:
  0.0 0.6 compare_reduce_fusion
  0.6 1.3 %fusion.3 = bf16[1,128]{1,0:T(2,128)(2,1)S(1)} fusion(pred[]{:T(512)} %compare_reduce_fusion, s32[128]{0:T(128)} %param.11), kind=kLoop, calls=%fused_computation.25 | loop fusion | flops 256 | bytes 769 | tf_op jit(solution)/shard_map/reshape.31
  1.9 0.7 fusion.2
  2.7 3.6 %collective-permute-done = bf16[1,33,256]{2,1,0:T(8,128)(2,1)S(1)} collective-permute-done((bf16[1,33,256]{2,1,0:T(8,128)(2,1)S(1)}, bf16[1,33,256]{2,1,0:T(8,128)(2,1)S(1)}, u32[]{:S(2)}, u32[]{:S(2)}) %collective-permute-start) | collective-permute-done | bytes 16928 | tf_op jit(solution)/shard_map/ppermute | solution.py:26
  6.3 0.1 collective-permute-start.1
  6.5 2.8 %collective-permute-done.1 = bf16[2,33,256]{2,1,0:T(8,128)(2,1)S(1)} collective-permute-done((bf16[2,33,256]{2,1,0:T(8,128)(2,1)S(1)}, bf16[2,33,256]{2,1,0:T(8,128)(2,1)S(1)}, u32[]{:S(2)}, u32[]{:S(2)}) %collective-permute-start.1) | collective-permute-done | bytes 33824 | tf_op jit(solution)/shard_map/ppermute | solution.py:26
  9.3 1.3 %collective-permute-start.2 = (bf16[4,33,256]{2,1,0:T(8,128)(2,1)S(1)}, bf16[4,33,256]{2,1,0:T(8,128)(2,1)S(1)}, u32[]{:S(2)}, u32[]{:S(2)}) collective-permute-start(bf16[4,33,256]{2,1,0:T(8,128)(2,1)S(1)} %maximum_select_fusion.2), channel_id=1, source_target_pairs={{0,2},{1,3},{2,0},{3,1},{4,6},{5,7},{6,4},{7,5},{8,10},{9,11},{10,... | collective-permute-start | bytes 202760 | tf_op jit(solution)/shard_map/ppermute | solution.py:26
  10.6 1.8 %multiply_convert_fusion.g_ref = bf16[128,4096]{1,0:T(8,128)(2,1)S(1)} fusion(bf16[128,4096]{1,0:T(8,128)(2,1)} %param.9, bf16[128,4096]{1,0:T(8,128)(2,1)} %param.8), kind=kLoop, calls=%fused_computation | loop fusion | flops 2097152 | bytes 3145728 | tf_op jit(solution)/shard_map/convert_element_type | solution.py:111
  12.4 0.2 collective-permute-done.2
  12.6 4.2 %collective-permute-start.3 = (bf16[8,33,256]{2,1,0:T(8,128)(2,1)S(1)}, bf16[8,33,256]{2,1,0:T(8,128)(2,1)S(1)}, u32[]{:S(2)}, u32[]{:S(2)}) collective-permute-start(bf16[8,33,256]{2,1,0:T(8,128)(2,1)S(1)} %maximum_select_fusion.1), channel_id=1, source_target_pairs={{0,1},{1,0},{2,3},{3,2},{4,5},{5,4},{6,7},{7,6},{8,9},{9,8},{10,11... | collective-permute-start | bytes 405512 | tf_op jit(solution)/shard_map/ppermute | solution.py:26
  16.8 0.1 pad.7.clone
  16.9 1.3 %collective-permute-start.4 = (bf16[128,4096]{1,0:T(8,128)(2,1)S(1)}, bf16[128,4096]{1,0:T(8,128)(2,1)S(1)}, u32[]{:S(2)}, u32[]{:S(2)}) collective-permute-start(bf16[128,4096]{1,0:T(8,128)(2,1)S(1)} %multiply_convert_fusion.g_ref), channel_id=1, source_target_pairs={{0,4},{1,5},{2,6},{3,7},{4,8},{5,9},{6,10},{7,11},{8,12},{9,13},{1... | collective-permute-start | bytes 3145736 | tf_op jit(solution)/shard_map/ppermute | solution.py:14
  18.2 3.1 %collective-permute-start.6 = (bf16[128,4096]{1,0:T(8,128)(2,1)S(1)}, bf16[128,4096]{1,0:T(8,128)(2,1)}, u32[]{:S(2)}, u32[]{:S(2)}) collective-permute-start(bf16[128,4096]{1,0:T(8,128)(2,1)S(1)} %multiply_convert_fusion.g_ref), channel_id=1, source_target_pairs={{0,2},{1,3},{2,4},{3,5},{4,6},{5,7},{6,8},{7,9},{8,10},{9,11},{10,... | collective-permute-start | bytes 3145736 | tf_op jit(solution)/shard_map/ppermute | solution.py:14
  21.6 0.2 copy.9
  21.8 0.8 rev.3
  22.5 1.3 %collective-permute-start.8 = (bf16[128,4096]{1,0:T(8,128)(2,1)S(1)}, bf16[128,4096]{1,0:T(8,128)(2,1)}, u32[]{:S(2)}, u32[]{:S(2)}) collective-permute-start(bf16[128,4096]{1,0:T(8,128)(2,1)S(1)} %multiply_convert_fusion.g_ref), channel_id=1, source_target_pairs={{0,1},{2,3},{4,5},{6,7},{8,9},{10,11},{12,13},{14,15},{16,17},{18,... | collective-permute-start | bytes 3145736 | tf_op jit(solution)/shard_map/ppermute | solution.py:163
  23.9 0.8 compare_convert_fusion.m_ref
  24.8 1.1 %maximum_maximum_fusion.p_ref = f32[256,768]{1,0:T(8,128)} fusion(f32[256,512]{1,0:T(8,128)S(1)} %rev.3, f32[768]{0:T(1024)S(1)} %pad.7.clone, f32[768]{0:T(1024)S(1)} %pad.5.clone), kind=kLoop, calls=%fused_computation.1 | loop fusion | flops 393216 | bytes 1316864 | tf_op jit(solution)/shard_map/concatenate | solution.py:121
  25.9 31.1 %shard_map.55 = (bf16[4,128,32768]{2,1,0:T(8,128)(2,1)}, f32[128,4096]{1,0:T(8,128)}) custom-call(f32[256,768]{1,0:T(8,128)} %maximum_maximum_fusion.p_ref, f32[128,640]{1,0:T(8,128)} %compare_convert_fusion.m_ref, bf16[128,4096]{1,0:T(8,128)(2,1)} %copy-done), custom_call_target="tpu_custom_call" | custom-call | tf_op jit(solution)/shard_map/pallas_call | solution.py:138
  57.0 4.1 %collective-permute-start.5 = (bf16[128,4096]{1,0:T(8,128)(2,1)S(1)}, bf16[128,4096]{1,0:T(8,128)(2,1)S(1)}, u32[]{:S(2)}, u32[]{:S(2)}) collective-permute-start(bf16[128,4096]{1,0:T(8,128)(2,1)S(1)} %collective-permute-done.4.refs_0_), channel_id=1, source_target_pairs={{1,0},{3,2},{5,4},{7,6},{9,8},{11,10},{13,12},{15,14},{17,16},{19,... | collective-permute-start | bytes 3145736 | tf_op jit(solution)/shard_map/ppermute | solution.py:164
  61.1 6.0 %collective-permute-done.6.refs_2_ = bf16[128,4096]{1,0:T(8,128)(2,1)} collective-permute-done((bf16[128,4096]{1,0:T(8,128)(2,1)S(1)}, bf16[128,4096]{1,0:T(8,128)(2,1)}, u32[]{:S(2)}, u32[]{:S(2)}) %collective-permute-start.6) | collective-permute-done | bytes 1048608 | tf_op jit(solution)/shard_map/ppermute | solution.py:14
  67.1 0.8 collective-permute-start.7
  67.9 2.6 %collective-permute-done.7.refs_3_ = bf16[128,4096]{1,0:T(8,128)(2,1)} collective-permute-done((bf16[128,4096]{1,0:T(8,128)(2,1)}, bf16[128,4096]{1,0:T(8,128)(2,1)}, u32[]{:S(2)}, u32[]{:S(2)}) %collective-permute-start.7) | collective-permute-done | bytes 1048608 | tf_op jit(solution)/shard_map/ppermute | solution.py:19
  70.5 18.1 %shard_map.56 = bf16[128,4096]{1,0:T(8,128)(2,1)} custom-call(s32[1]{0:T(128)} %bitcast.core_ref, bf16[128,4096]{1,0:T(8,128)(2,1)} %copy-done.1, bf16[128,4096]{1,0:T(8,128)(2,1)} %copy-done.2, bf16[128,4096]{1,0:T(8,128)(2,1)} %collective-permute-done.6.refs_2_, bf16[128,4096]{1,0:T(8,128)(2,1)} %collective-permute-done.7.refs_3_, ...), custom_call_target="tpu_custom_call" | custom-call | tf_op jit(solution)/shard_map/pallas_call | solution.py:168
  (30 shorter events, 0.4 us)
Async XLA Ops:
  2.7 3.6 %collective-permute-start = (bf16[1,33,256]{2,1,0:T(8,128)(2,1)S(1)}, bf16[1,33,256]{2,1,0:T(8,128)(2,1)S(1)}, u32[]{:S(2)}, u32[]{:S(2)}) collective-permute-start(bf16[1,33,256]{2,1,0:T(8,128)(2,1)S(1)} %fusion.2), channel_id=1, source_target_pairs={{0,8},{1,9},{2,10},{3,11},{4,12},{5,13},{6,14},{7,15},{8,0},{9,1},... | collective-permute-start | bytes 50696 | tf_op jit(solution)/shard_map/ppermute | solution.py:26
  6.3 2.9 %collective-permute-start.1 = (bf16[2,33,256]{2,1,0:T(8,128)(2,1)S(1)}, bf16[2,33,256]{2,1,0:T(8,128)(2,1)S(1)}, u32[]{:S(2)}, u32[]{:S(2)}) collective-permute-start(bf16[2,33,256]{2,1,0:T(8,128)(2,1)S(1)} %maximum_select_fusion.3), channel_id=1, source_target_pairs={{0,4},{1,5},{2,6},{3,7},{4,0},{5,1},{6,2},{7,3},{8,12},{9,13},{10,... | collective-permute-start | bytes 101384 | tf_op jit(solution)/shard_map/ppermute | solution.py:26
  9.3 3.4 %collective-permute-start.2 = (bf16[4,33,256]{2,1,0:T(8,128)(2,1)S(1)}, bf16[4,33,256]{2,1,0:T(8,128)(2,1)S(1)}, u32[]{:S(2)}, u32[]{:S(2)}) collective-permute-start(bf16[4,33,256]{2,1,0:T(8,128)(2,1)S(1)} %maximum_select_fusion.2), channel_id=1, source_target_pairs={{0,2},{1,3},{2,0},{3,1},{4,6},{5,7},{6,4},{7,5},{8,10},{9,11},{10,... | collective-permute-start | bytes 202760 | tf_op jit(solution)/shard_map/ppermute | solution.py:26
  12.4 10.2 %copy-start = (bf16[128,4096]{1,0:T(8,128)(2,1)}, bf16[128,4096]{1,0:T(8,128)(2,1)S(1)}, u32[]{:S(2)}) copy-start(bf16[128,4096]{1,0:T(8,128)(2,1)S(1)} %multiply_convert_fusion.g_ref) | copy-start | bytes 3145732
  12.6 8.7 %collective-permute-start.3 = (bf16[8,33,256]{2,1,0:T(8,128)(2,1)S(1)}, bf16[8,33,256]{2,1,0:T(8,128)(2,1)S(1)}, u32[]{:S(2)}, u32[]{:S(2)}) collective-permute-start(bf16[8,33,256]{2,1,0:T(8,128)(2,1)S(1)} %maximum_select_fusion.1), channel_id=1, source_target_pairs={{0,1},{1,0},{2,3},{3,2},{4,5},{5,4},{6,7},{7,6},{8,9},{9,8},{10,11... | collective-permute-start | bytes 405512 | tf_op jit(solution)/shard_map/ppermute | solution.py:26
  16.9 40.1 %collective-permute-start.4 = (bf16[128,4096]{1,0:T(8,128)(2,1)S(1)}, bf16[128,4096]{1,0:T(8,128)(2,1)S(1)}, u32[]{:S(2)}, u32[]{:S(2)}) collective-permute-start(bf16[128,4096]{1,0:T(8,128)(2,1)S(1)} %multiply_convert_fusion.g_ref), channel_id=1, source_target_pairs={{0,4},{1,5},{2,6},{3,7},{4,8},{5,9},{6,10},{7,11},{8,12},{9,13},{1... | collective-permute-start | bytes 3145736 | tf_op jit(solution)/shard_map/ppermute | solution.py:14
  18.2 48.9 %collective-permute-start.6 = (bf16[128,4096]{1,0:T(8,128)(2,1)S(1)}, bf16[128,4096]{1,0:T(8,128)(2,1)}, u32[]{:S(2)}, u32[]{:S(2)}) collective-permute-start(bf16[128,4096]{1,0:T(8,128)(2,1)S(1)} %multiply_convert_fusion.g_ref), channel_id=1, source_target_pairs={{0,2},{1,3},{2,4},{3,5},{4,6},{5,7},{6,8},{7,9},{8,10},{9,11},{10,... | collective-permute-start | bytes 3145736 | tf_op jit(solution)/shard_map/ppermute | solution.py:14
  21.4 2.5 %copy-start.3 = (s32[128]{0:T(128)S(1)}, s32[128]{0:T(128)}, u32[]{:S(2)}) copy-start(s32[128]{0:T(128)} %param.11) | copy-start | bytes 1540
  22.5 45.4 %collective-permute-start.8 = (bf16[128,4096]{1,0:T(8,128)(2,1)S(1)}, bf16[128,4096]{1,0:T(8,128)(2,1)}, u32[]{:S(2)}, u32[]{:S(2)}) collective-permute-start(bf16[128,4096]{1,0:T(8,128)(2,1)S(1)} %multiply_convert_fusion.g_ref), channel_id=1, source_target_pairs={{0,1},{2,3},{4,5},{6,7},{8,9},{10,11},{12,13},{14,15},{16,17},{18,... | collective-permute-start | bytes 3145736 | tf_op jit(solution)/shard_map/ppermute | solution.py:163
  57.0 13.5 %copy-start.1 = (bf16[128,4096]{1,0:T(8,128)(2,1)}, bf16[128,4096]{1,0:T(8,128)(2,1)S(1)}, u32[]{:S(2)}) copy-start(bf16[128,4096]{1,0:T(8,128)(2,1)S(1)} %collective-permute-done.4.refs_0_) | copy-start | bytes 3145732
  57.0 10.9 %collective-permute-start.5 = (bf16[128,4096]{1,0:T(8,128)(2,1)S(1)}, bf16[128,4096]{1,0:T(8,128)(2,1)S(1)}, u32[]{:S(2)}, u32[]{:S(2)}) collective-permute-start(bf16[128,4096]{1,0:T(8,128)(2,1)S(1)} %collective-permute-done.4.refs_0_), channel_id=1, source_target_pairs={{1,0},{3,2},{5,4},{7,6},{9,8},{11,10},{13,12},{15,14},{17,16},{19,... | collective-permute-start | bytes 3145736 | tf_op jit(solution)/shard_map/ppermute | solution.py:164
  67.1 3.5 %collective-permute-start.7 = (bf16[128,4096]{1,0:T(8,128)(2,1)}, bf16[128,4096]{1,0:T(8,128)(2,1)}, u32[]{:S(2)}, u32[]{:S(2)}) collective-permute-start(bf16[128,4096]{1,0:T(8,128)(2,1)} %collective-permute-done.6.refs_2_), channel_id=1, source_target_pairs={{0,1},{1,0},{2,3},{3,2},{4,5},{5,4},{6,7},{7,6},{8,9},{9,8},{10,11... | collective-permute-start | bytes 3145736 | tf_op jit(solution)/shard_map/ppermute | solution.py:19
  67.9 2.6 %copy-start.2 = (bf16[128,4096]{1,0:T(8,128)(2,1)}, bf16[128,4096]{1,0:T(8,128)(2,1)S(1)}, u32[]{:S(2)}) copy-start(bf16[128,4096]{1,0:T(8,128)(2,1)S(1)} %collective-permute-done.5.refs_1_) | copy-start | bytes 3145732
